TPU v7x, 256 devices: a whole 4x4x8 slice. The times are simulated.
256 devices in a mesh: group: 8 (over x, core), dev: 32 (over y, z).
Axes of the slice: x: 4, y: 4, z: 8, core: 2. Of those that a mesh axis runs over, the one named last changes fastest.
Arguments:
- em_image: bfloat16 [256, 1024, 512], P('group', 'dev'), may hold values from -6 to 6
- level_set: float32 [256, 1024, 512], P('group', 'dev'), may hold values from -6 to 6
- speeds: float32 [8], replicated, may hold values from -1 to 1.5
- brick_of_band: int32 [2048], P(('group', 'dev')), may hold values from 0 to 4095, as said below
- neighbours: int32 [4096, 6], P(('group', 'dev')), may hold values from -1 to 2047, as said below
- speed_index: int32 [4096], P(('group', 'dev')), may hold values from 0 to 7
Outputs:
- level_out: float32 [2048, 16, 16, 128], P(('group', 'dev'))
Inputs may be any that keep to these rules, and one draw needn't show every extreme that they name: `brick_of_band`: No brick is named twice. Band index j names a brick of the slab group of device j // 8. No device holds two bricks named by band indices that go to the same device j // 8. `neighbours`: entry k of brick b's list (sides x-, x+, y-, y+, z-, z+) is the band index j with brick_of_band[j] equal to the brick beside b on side k, or -1 where that side is the volume's boundary or the brick beside has no band index.
All inputs are finite; a program needn't handle non-finite values.
Results may differ from a plain program's by a relative error of at most 0.0003.
Values may be sent and summed in bfloat16 or wider, within the bound.
No kernel may reach another device: no remote copies, remote signals or barrier semaphores. Data moves between devices by JAX's collectives and lax.ppermute only.
A program may use at most 64 MiB of HBM per device.

v0:
```python
import math

import jax
import jax.numpy as jnp
from jax import lax
from jax.sharding import PartitionSpec as P

BX = 16
BY = 16
BZ = 128
BXN = 2
BYN = 2
BZN = 4
STEPS = 4


gauss_raw = [math.exp(-0.5 * position * position) for position in range(-2, 3)]
gauss_taps = [weight / sum(gauss_raw) for weight in gauss_raw]
time_step = 0.2
smoothing = 0.15
contrast = 0.02


def shortened(value):
    return jax.tree.map(lambda a: a.astype(jnp.bfloat16) if a.dtype == jnp.float32 else a, value)


def extended(cells, sides, width):
    for axis, dim in sides:
        count = lax.axis_size(axis)
        ends = count - 1
        head = lax.slice_in_dim(cells, 0, width, axis=dim)
        tail = lax.slice_in_dim(cells, cells.shape[dim] - width, cells.shape[dim], axis=dim)
        cells = jnp.concatenate(
            [
                lax.ppermute(tail, axis, [(i, (i + 1) % count) for i in range(ends)]),
                cells,
                lax.ppermute(head, axis, [((i + 1) % count, i) for i in range(ends)]),
            ],
            axis=dim,
        )
    return cells


def smooth_axis(values, along):
    length = values.shape[along] - 4
    summed = gauss_taps[0] * lax.slice_in_dim(values, 0, length, axis=along)
    for offset in range(1, 5):
        summed = summed + gauss_taps[offset] * lax.slice_in_dim(
            values, offset, offset + length, axis=along
        )
    return summed


def edge_map(window):
    smoothed = smooth_axis(smooth_axis(smooth_axis(window, 0), 1), 2)
    grad_x = (smoothed[2:, 1:-1, 1:-1] - smoothed[:-2, 1:-1, 1:-1]) * 0.5
    grad_y = (smoothed[1:-1, 2:, 1:-1] - smoothed[1:-1, :-2, 1:-1]) * 0.5
    grad_z = (smoothed[1:-1, 1:-1, 2:] - smoothed[1:-1, 1:-1, :-2]) * 0.5
    return 1.0 / (1.0 + (grad_x * grad_x + grad_y * grad_y + grad_z * grad_z) / contrast)


def to_bricks(block):
    shaped = block.reshape(BXN, BX, BYN, BY, BZN, BZ)
    return shaped.transpose(0, 2, 4, 1, 3, 5).reshape(BXN * BYN * BZN, BX, BY, BZ)


def own_faces(levels):
    side_faces = jnp.stack([levels[:, 0], levels[:, -1], levels[:, :, 0], levels[:, :, -1]], axis=1)
    end_faces = jnp.stack([levels[:, :, :, 0], levels[:, :, :, -1]], axis=1)
    return (side_faces, end_faces)


def advance(levels, side_ghost, end_ghost, edge_maps, speed_rows):
    with_z = jnp.concatenate(
        [end_ghost[:, 0][..., None], levels, end_ghost[:, 1][..., None]], axis=3
    )
    y_faces = jnp.pad(side_ghost[:, 2:4], ((0, 0), (0, 0), (0, 0), (1, 1)))
    with_y = jnp.concatenate(
        [y_faces[:, 0][:, :, None, :], with_z, y_faces[:, 1][:, :, None, :]], axis=2
    )
    x_faces = jnp.pad(side_ghost[:, 0:2], ((0, 0), (0, 0), (1, 1), (1, 1)))
    padded = jnp.concatenate([x_faces[:, 0][:, None], with_y, x_faces[:, 1][:, None]], axis=1)
    centre = padded[:, 1:-1, 1:-1, 1:-1]
    minus_x = padded[:, :-2, 1:-1, 1:-1]
    plus_x = padded[:, 2:, 1:-1, 1:-1]
    minus_y = padded[:, 1:-1, :-2, 1:-1]
    plus_y = padded[:, 1:-1, 2:, 1:-1]
    minus_z = padded[:, 1:-1, 1:-1, :-2]
    plus_z = padded[:, 1:-1, 1:-1, 2:]
    laplace = plus_x + minus_x + (plus_y + minus_y) + (plus_z + minus_z) - 6.0 * centre
    diff_x = (plus_x - minus_x) * 0.5
    diff_y = (plus_y - minus_y) * 0.5
    diff_z = (plus_z - minus_z) * 0.5
    gradient = diff_x * diff_x + diff_y * diff_y + diff_z * diff_z
    force = smoothing * laplace + speed_rows[:, None, None, None]
    return centre + time_step * edge_maps * force * jnp.sqrt(1.0 + gradient)


def assemble_ghosts(side_faces, end_faces, beside_lists):
    face_grid = side_faces.reshape((BXN, BYN, BZN) + side_faces.shape[1:])
    widened = extended(shortened(face_grid), (("group", 0), ("dev", 1)), 1).astype(face_grid.dtype)
    from_side = jnp.stack(
        [
            widened[:-2, 1:-1, :, 1],
            widened[2:, 1:-1, :, 0],
            widened[1:-1, :-2, :, 3],
            widened[1:-1, 2:, :, 2],
        ],
        axis=3,
    ).reshape(side_faces.shape)
    end_grid = end_faces.reshape((BXN, BYN, BZN) + end_faces.shape[1:])
    zero_faces = jnp.zeros_like(end_grid[:, :, :1, 0])
    lower_ghost = jnp.concatenate([zero_faces, end_grid[:, :, :-1, 1]], axis=2)
    upper_ghost = jnp.concatenate([end_grid[:, :, 1:, 0], zero_faces], axis=2)
    from_ends = jnp.stack([lower_ghost, upper_ghost], axis=3).reshape(end_faces.shape)
    linked = beside_lists >= 0
    side_ghost = jnp.where(linked[:, :4, None, None], from_side, side_faces)
    end_ghost = jnp.where(linked[:, 4:, None, None], from_ends, end_faces)
    return (side_ghost, end_ghost)


def place_rows(values, target, usable, partners):
    items = values.shape[0]
    matches = (target[None, :] == jnp.arange(partners)[:, None]) & usable[None, :]
    chosen = jnp.sum(jnp.where(matches, jnp.arange(items)[None, :], 0), axis=1)
    present = jnp.any(matches, axis=1)
    picked = jnp.take(values, chosen, axis=0)
    return jnp.where(
        present.reshape((partners,) + (1,) * (values.ndim - 1)), picked, jnp.zeros((), values.dtype)
    )


def extended_many(items, sides):
    cells = [value for value, width in items]
    widths = [width for value, width in items]
    for axis, dim in sides:
        count = lax.axis_size(axis)
        ends = count - 1
        heads = tuple(lax.slice_in_dim(c, 0, w, axis=dim) for c, w in zip(cells, widths))
        tails = tuple(
            lax.slice_in_dim(c, c.shape[dim] - w, c.shape[dim], axis=dim) for c, w in zip(cells, widths)
        )
        from_below = lax.ppermute(tails, axis, [(i, (i + 1) % count) for i in range(ends)])
        from_above = lax.ppermute(heads, axis, [((i + 1) % count, i) for i in range(ends)])
        cells = [
            jnp.concatenate([below, c, above], axis=dim)
            for below, c, above in zip(from_below, cells, from_above)
        ]
    return cells


def extended_packed(em_image, level_set, info):
    cells = [em_image, level_set, info]
    widths = [3 + STEPS, STEPS, 1]
    for axis, dim in (("group", 0), ("dev", 1)):
        count = lax.axis_size(axis)
        ends = count - 1
        parts = []
        for end in (0, 1):
            pieces = []
            for c, w in zip(cells, widths):
                start = 0 if end == 0 else c.shape[dim] - w
                pieces.append(lax.slice_in_dim(c, start, start + w, axis=dim))
            parts.append(pieces)
        def sent(pieces, pairs):
            image_part = lax.ppermute(pieces[0], axis, pairs)
            flat = jnp.concatenate([pieces[1].reshape(-1), pieces[2].reshape(-1)])
            flat = lax.ppermute(flat, axis, pairs)
            size = pieces[1].size
            return [
                image_part,
                flat[:size].reshape(pieces[1].shape),
                flat[size:].reshape(pieces[2].shape),
            ]
        from_below = sent(parts[1], [(i, i + 1) for i in range(ends)])
        from_above = sent(parts[0], [(i + 1, i) for i in range(ends)])
        cells = [
            jnp.concatenate([below, c, above], axis=dim)
            for below, c, above in zip(from_below, cells, from_above)
        ]
    return cells


def region_step(lvl, edge, rate, code):
    centre = lvl[1:-1, 1:-1]
    shifted = (
        lvl[:-2, 1:-1],
        lvl[2:, 1:-1],
        lvl[1:-1, :-2],
        lvl[1:-1, 2:],
        jnp.concatenate([centre[:, :, :1], centre[:, :, :-1]], axis=2),
        jnp.concatenate([centre[:, :, 1:], centre[:, :, -1:]], axis=2),
    )
    minus_x, plus_x, minus_y, plus_y, minus_z, plus_z = (
        jnp.where((code >> side) & 1 == 1, value, centre) for side, value in enumerate(shifted)
    )
    laplace = plus_x + minus_x + (plus_y + minus_y) + (plus_z + minus_z) - 6.0 * centre
    diff_x = (plus_x - minus_x) * 0.5
    diff_y = (plus_y - minus_y) * 0.5
    diff_z = (plus_z - minus_z) * 0.5
    gradient = diff_x * diff_x + diff_y * diff_y + diff_z * diff_z
    force = smoothing * laplace + rate
    return centre + time_step * edge * force * jnp.sqrt(1.0 + gradient)


def per_device(em_image, level_set, speeds, brick_of_band, neighbours, speed_index):
    partners = lax.axis_size("dev")
    bricks_here = BXN * BYN * BZN
    choose = speed_index[:, None] == jnp.arange(speeds.shape[0])[None, :]
    rates_here = jnp.sum(jnp.where(choose, speeds[None, :], 0.0), axis=1)
    info = jnp.concatenate(
        [(neighbours >= 0).astype(jnp.float32), rates_here[:, None]], axis=1
    ).reshape(BXN, BYN, BZN, 7)
    margin, wide_level, wide_info = extended_packed(em_image, level_set, info)
    window = jnp.pad(margin.astype(jnp.float32), ((0, 0), (0, 0), (3, 3)))
    edge = edge_map(window)
    span_x, span_y, span_z = wide_level.shape
    lead = BX - STEPS
    weights = jnp.asarray([1 << side for side in range(6)] + [0], jnp.int32)
    brick_code = jnp.sum(jnp.where(wide_info > 0.5, weights, 0), axis=-1)
    def planes(per_brick):
        spread = jnp.broadcast_to(
            per_brick.reshape(BXN + 2, BYN + 2, 1, BZN, 1), (BXN + 2, BYN + 2, BY, BZN, BZ)
        ).reshape(BXN + 2, (BYN + 2) * BY, BZN * BZ)
        return spread[:, lead : lead + span_y]
    def across_x(per_brick):
        table = planes(per_brick)
        xe = lax.broadcasted_iota(jnp.int32, wide_level.shape, 0) + lead
        value = table[BXN + 1][None]
        for bx in range(BXN, -1, -1):
            value = jnp.where(xe < (bx + 1) * BX, table[bx][None], value)
        return value
    rate = across_x(wide_info[..., 6])
    place = (
        lax.broadcasted_iota(jnp.int32, wide_level.shape, 0) + lead,
        lax.broadcasted_iota(jnp.int32, wide_level.shape, 1) + lead,
        lax.broadcasted_iota(jnp.int32, wide_level.shape, 2),
    )
    sizes = (BX, BX, BY, BY, BZ, BZ)
    code = across_x(brick_code)
    for side in range(6):
        pos = place[side // 2] % sizes[side]
        inner = pos != (0 if side % 2 == 0 else sizes[side] - 1)
        code = code | (inner.astype(jnp.int32) << side)
    lvl = wide_level
    for repeat in range(STEPS):
        lo = repeat + 1
        hi_x = span_x - repeat - 1
        hi_y = span_y - repeat - 1
        lvl = region_step(lvl, edge[lo:hi_x, lo:hi_y], rate[lo:hi_x, lo:hi_y], code[lo:hi_x, lo:hi_y])
    level_bricks = to_bricks(lvl)
    band_here = brick_of_band.shape[0]
    lower = jnp.concatenate([neighbours[1:, 4], neighbours[:1, 4]])
    upper = jnp.concatenate([neighbours[-1:, 5], neighbours[:-1, 5]])
    first_in_z = jnp.arange(bricks_here, dtype=jnp.int32) % BZN == 0
    band_of = jnp.where(first_in_z, lower, upper)
    in_band = band_of >= 0
    owner_dev = band_of // band_here % partners
    source_dev = brick_of_band // bricks_here % partners
    arrived = lax.all_to_all(
        place_rows(level_bricks, owner_dev, in_band, partners),
        "dev",
        split_axis=0,
        concat_axis=0,
        tiled=True,
    )
    return jnp.take(arrived, source_dev, axis=0)


def solution(mesh):
    placed = (
        P("group", "dev", None),
        P("group", "dev", None),
        P(),
        P(("group", "dev")),
        P(("group", "dev"), None),
        P(("group", "dev")),
    )
    return jax.shard_map(
        per_device,
        mesh=mesh,
        in_specs=placed,
        out_specs=P(("group", "dev"), None, None, None),
        check_vma=False,
    )
```

profile of v0, /device:TPU:1, one launch (start us, length us, event | category | flops | bytes accessed | tf_op | source)
XLA Modules:
  0.0 248.7 jit_solution(11511745078409920338)
XLA Ops:
  0.0 0.9 copy.24
  0.9 0.8 select_reduce_fusion.2
  1.9 1.1 fusion.64
  3.1 5.1 %collective-permute-start.1 = (f32[65592]{0:T(1024)S(1)}, f32[65592]{0:T(1024)S(1)}, u32[]{:S(2)}, u32[]{:S(2)}) collective-permute-start(f32[65592]{0:T(1024)S(1)} %pad_maximum_fusion.4), channel_id=1, source_target_pairs={{32,0},{64,32},{96,64},{128,96},{160,128},{192,160},{224,192},{33,... | collective-permute-start | bytes 787112 | tf_op jit(solution)/shard_map/ppermute | solution.py:169
  8.4 1.9 collective-permute-start
  10.3 1.9 collective-permute-start.4
  12.3 2.4 collective-permute-start.5
  14.7 0.6 fusion.53
  15.3 0.5 compare_and_fusion
  15.8 0.6 iota_and_fusion
  16.4 0.6 compare_select_fusion.3
  17.1 0.6 fusion.68
  17.7 1.3 broadcast_compare_fusion
  19.1 0.6 fusion.43
  19.7 0.6 pad_clamp_fusion.1
  20.3 0.6 fusion.48
  20.9 0.6 compare_and_fusion.1
  21.7 1.1 copy-done.2
  22.8 0.8 fusion.65
  23.7 1.3 collective-permute-start.7
  25.0 4.7 %collective-permute-start.6 = (bf16[46,7,512]{2,1,0:T(8,128)(2,1)S(1)}, bf16[46,7,512]{2,1,0:T(8,128)(2,1)}, u32[]{:S(2)}, u32[]{:S(2)}) collective-permute-start(bf16[46,7,512]{2,1,0:T(8,128)(2,1)S(1)} %get-tuple-element.31), channel_id=1, source_target_pairs={{0,1},{1,2},{2,3},{3,4},{4,5},{5,6},{6,7},{7,8},{8,9},{9,10},{10,1... | collective-permute-start | bytes 989192 | tf_op jit(solution)/shard_map/ppermute | solution.py:167
  30.0 0.6 reshape.204
  30.7 1.8 constant_dynamic-update-slice_fusion.1
  32.9 1.4 pad_maximum_fusion.2
  34.3 1.3 collective-permute-start.3
  35.8 4.7 %collective-permute-start.2 = (f32[82032]{0:T(1024)S(1)}, f32[82032]{0:T(1024)}, u32[]{:S(2)}, u32[]{:S(2)}) collective-permute-start(f32[82032]{0:T(1024)S(1)} %pad_maximum_fusion.1), channel_id=1, source_target_pairs={{0,1},{1,2},{2,3},{3,4},{4,5},{5,6},{6,7},{7,8},{8,9},{9,10},{10,1... | collective-permute-start | bytes 984392 | tf_op jit(solution)/shard_map/ppermute | solution.py:169
  40.6 3.8 %fusion.35 = f32[46,46,518]{2,1,0:T(8,128)S(1)} fusion(bf16[46,7,512]{2,1,0:T(8,128)(2,1)} %collective-permute-done.7, bf16[46,32,512]{2,1,0:T(8,128)(2,1)} %copy-done.2, bf16[46,7,512]{2,1,0:T(8,128)(2,1)} %collective-permute-done.6), kind=kLoop, calls=%fused_computation.95 | loop fusion | flops 13153056 | bytes 6551136 | tf_op jit(solution)/shard_map/jit(_pad)/pad | solution.py:216
  44.4 2.6 %fusion.9 = f32[42,46,518]{2,1,0:T(8,128)S(1)} fusion(f32[46,46,518]{2,1,0:T(8,128)S(1)} %fusion.35), kind=kLoop, calls=%fused_computation.24 | loop fusion | flops 9006984 | bytes 24018624 | tf_op jit(solution)/shard_map/add | solution.py:49
  47.0 2.9 %fusion.5 = f32[42,42,518]{2,1,0:T(8,128)S(1)} fusion(f32[42,46,518]{2,1,0:T(8,128)S(1)} %fusion.9), kind=kLoop, calls=%fused_computation.15 | loop fusion | flops 8223768 | bytes 21930048 | tf_op jit(solution)/shard_map/add | solution.py:49
  49.9 5.5 %fusion.1 = f32[42,42,514]{2,1,0:T(8,128)S(1)} fusion(f32[42,42,518]{2,1,0:T(8,128)S(1)} %fusion.5), kind=kLoop, calls=%fused_computation.6 | loop fusion | flops 8160264 | bytes 21760704 | tf_op jit(solution)/shard_map/add | solution.py:49
  55.4 6.1 %fusion.18 = f32[40,40,512]{2,1,0:T(8,128)} fusion(f32[42,42,514]{2,1,0:T(8,128)S(1)} %fusion.1), kind=kLoop, calls=%fused_computation.45 | loop fusion | flops 11468800 | bytes 22937600 | tf_op jit(solution)/shard_map/div | solution.py:60
  61.5 1.0 slice.451
  62.5 0.8 reshape.205
  63.4 1.0 slice.448
  64.4 0.8 reshape.202
  65.2 2.3 pad_maximum_fusion
  67.6 4.0 %fusion.56 = (f32[38,38,511]{2,1,0:T(8,128)}, f32[38,38,511]{2,1,0:T(8,128)}) fusion(f32[40,40,512]{2,1,0:T(8,128)S(1)} %pad_maximum_fusion), kind=kLoop, calls=%fused_computation.209 | loop fusion | bytes 11806144 | tf_op jit(solution)/shard_map/slice | solution.py:193
  71.6 1.4 fusion.57
  73.0 0.7 slice.478
  73.8 0.7 slice.477
  74.6 0.4 select_reduce_fusion
  75.1 0.9 broadcast_in_dim.182
  76.1 2.1 reshape.209
  78.1 1.7 slice_bitcast_fusion.5
  79.9 0.9 broadcast_in_dim.172
  80.8 2.0 reshape.208
  82.9 1.1 slice_bitcast_fusion.9
  84.0 1.9 select_select_fusion.1
  86.0 5.2 %shift-left_or_fusion = s32[40,40,512]{2,1,0:T(8,128)S(1)} fusion(s32[512]{0:T(512)S(1)} %copy-done.9, s32[512]{0:T(512)S(1)} %copy-done.10, s32[40]{0:T(128)} %get-tuple-element.53, s32[40]{0:T(128)} %get-tuple-element.54, s32[40,512]{1,0:T(8,128)S(1)} %get-tuple-element.36, s32[40,512]{1,0:T(8,128)S(1)} %get-tuple-element.37, ...), kind=kLoop, calls=%fused_computation.55 | loop fusion | flops 24576000 | bytes 3609568 | tf_op jit(solution)/shard_map/or | solution.py:245
  91.2 10.3 %fusion.29 = f32[38,38,512]{2,1,0:T(8,128)S(1)} fusion(f32[40,40,512]{2,1,0:T(8,128)S(1)} %select_select_fusion.1, f32[40,40,512]{2,1,0:T(8,128)S(1)} %copy-done, f32[38,38,511]{2,1,0:T(8,128)} %get-tuple-element.12, f32[38,38,1]{2,1,0:T(8,128)S(1)} %copy-done.4, f32[38,38,1]{2,1,0:T(8,128)S(1)} %copy-done.3, f32[38,38,511]{2,1,0:T(8,128)} %get-tuple-element.11, ...), kind=kLoop, calls=%fused_computation.62 | loop fusion | flops 37705728 | bytes 32530432 | tf_op jit(solution)/shard_map/add | solution.py:204
  101.5 1.5 fusion.58
  103.3 7.4 %fusion.32 = f32[36,36,512]{2,1,0:T(8,128)S(1)} fusion(f32[40,40,512]{2,1,0:T(8,128)S(1)} %select_select_fusion.1, f32[40,40,512]{2,1,0:T(8,128)S(1)} %copy-done, f32[36,36,511]{2,1,0:T(8,128)S(1)} %get-tuple-element.16, f32[36,36,1]{2,1,0:T(8,128)S(1)} %get-tuple-element.18, f32[36,36,1]{2,1,0:T(8,128)S(1)} %get-tuple-element.17, ...), kind=kLoop, calls=%fused_computation.79 | loop fusion | flops 33841152 | bytes 29196288 | tf_op jit(solution)/shard_map/add | solution.py:204
  110.7 1.4 fusion.60
  112.4 8.0 %fusion.38 = f32[34,34,512]{2,1,0:T(8,128)S(1)} fusion(f32[40,40,512]{2,1,0:T(8,128)S(1)} %select_select_fusion.1, f32[40,40,512]{2,1,0:T(8,128)S(1)} %copy-done, f32[34,34,511]{2,1,0:T(8,128)S(1)} %get-tuple-element.20, f32[34,34,1]{2,1,0:T(8,128)S(1)} %get-tuple-element.22, f32[34,34,1]{2,1,0:T(8,128)S(1)} %get-tuple-element.21, ...), kind=kLoop, calls=%fused_computation.99 | loop fusion | flops 30185472 | bytes 26042368 | tf_op jit(solution)/shard_map/add | solution.py:204
  120.4 1.0 fusion.62
  121.7 5.4 %fusion.41 = f32[32,32,512]{2,1,0:T(8,128)S(1)} fusion(f32[40,40,512]{2,1,0:T(8,128)S(1)} %select_select_fusion.1, f32[40,40,512]{2,1,0:T(8,128)S(1)} %copy-done, f32[32,32,511]{2,1,0:T(8,128)S(1)} %get-tuple-element.24, f32[32,32,1]{2,1,0:T(8,128)S(1)} %get-tuple-element.26, f32[32,32,1]{2,1,0:T(8,128)S(1)} %get-tuple-element.25, ...), kind=kLoop, calls=%fused_computation.116 | loop fusion | flops 26738688 | bytes 23068672 | tf_op jit(solution)/shard_map/add | solution.py:204
  127.1 1.7 reshape.210
  128.9 1.8 copy.29
  130.7 2.9 %gather_fusion = f32[32,16,16,128]{3,2,1,0:T(8,128)} fusion(f32[16,16,16,128]{3,2,1,0:T(8,128)S(1)} %bitcast.42, s32[1024]{0:T(1024)} %pad_clamp_fusion.1), kind=kCustom, calls=%fused_computation | custom fusion | bytes 8388736 | tf_op jit(solution)/shard_map/jit(_take)/gather | solution.py:128
  133.6 5.1 %select_select_fusion = f32[32,16,16,128]{3,2,1,0:T(8,128)} fusion(f32[32,16,16,128]{3,2,1,0:T(8,128)} %gather_fusion, pred[32]{0:T(512)(128)(4,1)S(1)} %copy-done.16, pred[32]{0:T(512)(128)(4,1)S(1)} %copy-done.15), kind=kLoop, calls=%fused_computation.38 | loop fusion | flops 2097152 | bytes 8388672 | tf_op jit(solution)/shard_map/jit(_where)/select_n | solution.py:129
  138.7 12.3 %all-to-all-start = ((f32[32,16,16,128]{3,2,1,0:T(8,128)}), f32[32,16,16,128]{3,2,1,0:T(8,128)}, u32[]{:S(2)}, u32[]{:S(2)}) async-start(f32[32,16,16,128]{3,2,1,0:T(8,128)} %select_select_fusion), calls=%async_computation | async-start | bytes 8388608 | tf_op jit(solution)/shard_map/all_to_all | solution.py:261
  151.1 93.7 %all-to-all-done = f32[32,16,16,128]{3,2,1,0:T(8,128)} async-done(((f32[32,16,16,128]{3,2,1,0:T(8,128)}), f32[32,16,16,128]{3,2,1,0:T(8,128)}, u32[]{:S(2)}, u32[]{:S(2)}) %all-to-all-start) | async-done | bytes 4194336 | tf_op jit(solution)/shard_map/all_to_all | solution.py:261
  244.8 2.8 %gather_fusion.1 = f32[8,16,16,128]{3,2,1,0:T(8,128)S(1)} fusion(f32[32,16,16,128]{3,2,1,0:T(8,128)} %all-to-all-done, s32[1024]{0:T(1024)S(1)} %pad_clamp_fusion), kind=kCustom, calls=%fused_computation.1 | custom fusion | bytes 2097184 | tf_op jit(solution)/shard_map/jit(_take)/gather | solution.py:268
  247.6 1.1 broadcast_select_fusion
  (88 shorter events, 3.2 us)
Async XLA Ops:
  0.0 17.0 %copy-start.8 = (s32[16,6]{0,1:T(8,128)S(1)}, s32[16,6]{0,1:T(8,128)}, u32[]{:S(2)}) copy-start(s32[16,6]{0,1:T(8,128)} %param.11) | copy-start | bytes 1156
  0.0 10.3 %copy-start.5 = (bf16[32,32,512]{2,1,0:T(8,128)(2,1)S(1)}, bf16[32,32,512]{2,1,0:T(8,128)(2,1)}, u32[]{:S(2)}) copy-start(bf16[32,32,512]{2,1,0:T(8,128)(2,1)} %param.7) | copy-start | bytes 3145732
  3.1 26.6 %collective-permute-start.1 = (f32[65592]{0:T(1024)S(1)}, f32[65592]{0:T(1024)S(1)}, u32[]{:S(2)}, u32[]{:S(2)}) collective-permute-start(f32[65592]{0:T(1024)S(1)} %pad_maximum_fusion.4), channel_id=1, source_target_pairs={{32,0},{64,32},{96,64},{128,96},{160,128},{192,160},{224,192},{33,... | collective-permute-start | bytes 787112 | tf_op jit(solution)/shard_map/ppermute | solution.py:169
  8.4 21.4 %collective-permute-start = (f32[65592]{0:T(1024)S(1)}, f32[65592]{0:T(1024)S(1)}, u32[]{:S(2)}, u32[]{:S(2)}) collective-permute-start(f32[65592]{0:T(1024)S(1)} %pad_maximum_fusion.3), channel_id=1, source_target_pairs={{0,32},{32,64},{64,96},{96,128},{128,160},{160,192},{192,224},{1,3... | collective-permute-start | bytes 787112 | tf_op jit(solution)/shard_map/ppermute | solution.py:169
  10.3 11.2 %collective-permute-start.4 = (bf16[7,32,512]{2,1,0:T(8,128)(2,1)S(1)}, bf16[7,32,512]{2,1,0:T(8,128)(2,1)S(1)}, u32[]{:S(2)}, u32[]{:S(2)}) collective-permute-start(bf16[7,32,512]{2,1,0:T(8,128)(2,1)S(1)} %get-tuple-element.34), channel_id=1, source_target_pairs={{0,32},{32,64},{64,96},{96,128},{128,160},{160,192},{192,224},{1,3... | collective-permute-start | bytes 688136 | tf_op jit(solution)/shard_map/ppermute | solution.py:167
  12.3 9.4 %collective-permute-start.5 = (bf16[7,32,512]{2,1,0:T(8,128)(2,1)S(1)}, bf16[7,32,512]{2,1,0:T(8,128)(2,1)S(1)}, u32[]{:S(2)}, u32[]{:S(2)}) collective-permute-start(bf16[7,32,512]{2,1,0:T(8,128)(2,1)S(1)} %get-tuple-element.33), channel_id=1, source_target_pairs={{32,0},{64,32},{96,64},{128,96},{160,128},{192,160},{224,192},{33,... | collective-permute-start | bytes 688136 | tf_op jit(solution)/shard_map/ppermute | solution.py:167
  21.7 1.2 copy-start.2
  23.7 16.9 %collective-permute-start.7 = (bf16[46,7,512]{2,1,0:T(8,128)(2,1)}, bf16[46,7,512]{2,1,0:T(8,128)(2,1)}, u32[]{:S(2)}, u32[]{:S(2)}) collective-permute-start(bf16[46,7,512]{2,1,0:T(8,128)(2,1)} %get-tuple-element.32), channel_id=1, source_target_pairs={{1,0},{2,1},{3,2},{4,3},{5,4},{6,5},{7,6},{8,7},{9,8},{10,9},{11,1... | collective-permute-start | bytes 989192 | tf_op jit(solution)/shard_map/ppermute | solution.py:167
  25.0 15.6 %collective-permute-start.6 = (bf16[46,7,512]{2,1,0:T(8,128)(2,1)S(1)}, bf16[46,7,512]{2,1,0:T(8,128)(2,1)}, u32[]{:S(2)}, u32[]{:S(2)}) collective-permute-start(bf16[46,7,512]{2,1,0:T(8,128)(2,1)S(1)} %get-tuple-element.31), channel_id=1, source_target_pairs={{0,1},{1,2},{2,3},{3,4},{4,5},{5,6},{6,7},{7,8},{8,9},{9,10},{10,1... | collective-permute-start | bytes 989192 | tf_op jit(solution)/shard_map/ppermute | solution.py:167
  29.7 0.9 copy-start.6
  30.7 1.9 copy-start.7
  32.7 11.7 %copy-start.1 = (f32[40,32,512]{2,1,0:T(8,128)}, f32[40,32,512]{2,1,0:T(8,128)S(1)}, u32[]{:S(2)}) copy-start(f32[40,32,512]{2,1,0:T(8,128)S(1)} %constant_dynamic-update-slice_fusion) | copy-start | bytes 7864324
  34.3 27.2 %collective-permute-start.3 = (f32[82032]{0:T(1024)}, f32[82032]{0:T(1024)}, u32[]{:S(2)}, u32[]{:S(2)}) collective-permute-start(f32[82032]{0:T(1024)} %pad_maximum_fusion.2), channel_id=1, source_target_pairs={{1,0},{2,1},{3,2},{4,3},{5,4},{6,5},{7,6},{8,7},{9,8},{10,9},{11,1... | collective-permute-start | bytes 984392 | tf_op jit(solution)/shard_map/ppermute | solution.py:169
  35.8 27.5 %collective-permute-start.2 = (f32[82032]{0:T(1024)S(1)}, f32[82032]{0:T(1024)}, u32[]{:S(2)}, u32[]{:S(2)}) collective-permute-start(f32[82032]{0:T(1024)S(1)} %pad_maximum_fusion.1), channel_id=1, source_target_pairs={{0,1},{1,2},{2,3},{3,4},{4,5},{5,6},{6,7},{7,8},{8,9},{9,10},{10,1... | collective-permute-start | bytes 984392 | tf_op jit(solution)/shard_map/ppermute | solution.py:169
  71.6 3.0 %copy-start.17 = (s32[7]{0:T(128)S(1)}, s32[7]{0:T(128)}, u32[]{:S(2)}) copy-start(s32[7]{0:T(128)} %constant.217.clone) | copy-start | bytes 88
  79.8 6.1 %copy-start.9 = (s32[512]{0:T(512)S(1)}, s32[512]{0:T(512)}, u32[]{:S(2)}) copy-start(s32[512]{0:T(512)} %get-tuple-element.55) | copy-start | bytes 6148
  79.8 6.1 %copy-start.10 = (s32[512]{0:T(512)S(1)}, s32[512]{0:T(512)}, u32[]{:S(2)}) copy-start(s32[512]{0:T(512)} %get-tuple-element.56) | copy-start | bytes 6148
  79.8 6.1 %copy-start.11 = (pred[40]{0:T(512)(128)(4,1)S(1)}, pred[40]{0:T(512)(128)(4,1)}, u32[]{:S(2)}) copy-start(pred[40]{0:T(512)(128)(4,1)} %get-tuple-element.51) | copy-start | bytes 124
  79.8 6.1 %copy-start.12 = (pred[40]{0:T(512)(128)(4,1)S(1)}, pred[40]{0:T(512)(128)(4,1)}, u32[]{:S(2)}) copy-start(pred[40]{0:T(512)(128)(4,1)} %get-tuple-element.52) | copy-start | bytes 124
  79.9 6.1 %copy-start.13 = (pred[40]{0:T(512)(128)(4,1)S(1)}, pred[40]{0:T(512)(128)(4,1)}, u32[]{:S(2)}) copy-start(pred[40]{0:T(512)(128)(4,1)} %get-tuple-element.58) | copy-start | bytes 124
  79.9 6.1 %copy-start.14 = (pred[40]{0:T(512)(128)(4,1)S(1)}, pred[40]{0:T(512)(128)(4,1)}, u32[]{:S(2)}) copy-start(pred[40]{0:T(512)(128)(4,1)} %get-tuple-element.57) | copy-start | bytes 124
  83.9 7.2 %copy-start = (f32[40,40,512]{2,1,0:T(8,128)S(1)}, f32[40,40,512]{2,1,0:T(8,128)}, u32[]{:S(2)}) copy-start(f32[40,40,512]{2,1,0:T(8,128)} %fusion.18) | copy-start | bytes 9830404
  83.9 7.2 %copy-start.3 = (f32[38,38,1]{2,1,0:T(8,128)S(1)}, f32[38,38,1]{2,1,0:T(8,128)}, u32[]{:S(2)}) copy-start(f32[38,38,1]{2,1,0:T(8,128)} %get-tuple-element.13) | copy-start | bytes 17332
  84.0 7.2 %copy-start.4 = (f32[38,38,1]{2,1,0:T(8,128)S(1)}, f32[38,38,1]{2,1,0:T(8,128)}, u32[]{:S(2)}) copy-start(f32[38,38,1]{2,1,0:T(8,128)} %get-tuple-element.14) | copy-start | bytes 17332
  130.7 2.9 %copy-start.15 = (pred[32]{0:T(512)(128)(4,1)S(1)}, pred[32]{0:T(512)(128)(4,1)}, u32[]{:S(2)}) copy-start(pred[32]{0:T(512)(128)(4,1)} %fusion.43) | copy-start | bytes 100
  130.7 2.9 %copy-start.16 = (pred[32]{0:T(512)(128)(4,1)S(1)}, pred[32]{0:T(512)(128)(4,1)}, u32[]{:S(2)}) copy-start(pred[32]{0:T(512)(128)(4,1)} %compare_and_fusion.1) | copy-start | bytes 100
  138.7 12.3 %copy-start.18 = (s32[8]{0:T(128)S(1)}, s32[8]{0:T(128)}, u32[]{:S(2)}) copy-start(s32[8]{0:T(128)} %param.10) | copy-start | bytes 100
  138.7 106.1 %all-to-all-start = ((f32[32,16,16,128]{3,2,1,0:T(8,128)}), f32[32,16,16,128]{3,2,1,0:T(8,128)}, u32[]{:S(2)}, u32[]{:S(2)}) async-start(f32[32,16,16,128]{3,2,1,0:T(8,128)} %select_select_fusion), calls=%async_computation | async-start | bytes 8388608 | tf_op jit(solution)/shard_map/all_to_all | solution.py:261
where the time goes:
time: 253 us; the launch traced here: 249 us
  waiting for transfers between devices  93.7 us (37%)
  other arithmetic  76.5 us (30%)
  local copies, waits for them, and re-layouts  42.2 us (17%)
  starting transfers between devices  35.7 us (14%)
    all_to_all x1, waiting for transfers between devices, per_device(): lax.all_to_all(place_rows(level_bricks, owner_dev, in_band, partners), 'd...  93.7 us
    add x4, other arithmetic, region_step(): return centre + time_step * edge * force * jnp.sqrt(1.0 + gradient)  31 us
    ppermute x4, starting transfers between devices, sent(): flat = lax.ppermute(flat, axis, pairs)  13 us
    all_to_all x1, starting transfers between devices, per_device(): lax.all_to_all(place_rows(level_bricks, owner_dev, in_band, partners), 'd...  12.3 us
    add x3, other arithmetic, smooth_axis(): summed + gauss_taps[offset] * lax.slice_in_dim(values, offset, offset + l...  11 us
    ppermute x4, starting transfers between devices, sent(): image_part = lax.ppermute(pieces[0], axis, pairs)  10.4 us
    slice x4, local copies, waits for them, and re-layouts, region_step(): centre[:, :, 1:]  8.01 us
    div x1, other arithmetic, edge_map(): 1.0 / (1.0 + (grad_x * grad_x + grad_y * grad_y + grad_z * grad_z) / cont...  6.12 us
  transfers between devices with their start and end apart: 9, of which 1 were waited for; matrix products, arithmetic and copies ran while one was open for 14% of the time, Pallas kernels for 0%

commit v1 on v0

--- a/solution.py
+++ b/solution.py
@@ -249,7 +249,6 @@
         hi_x = span_x - repeat - 1
         hi_y = span_y - repeat - 1
         lvl = region_step(lvl, edge[lo:hi_x, lo:hi_y], rate[lo:hi_x, lo:hi_y], code[lo:hi_x, lo:hi_y])
-    level_bricks = to_bricks(lvl)
     band_here = brick_of_band.shape[0]
     lower = jnp.concatenate([neighbours[1:, 4], neighbours[:1, 4]])
     upper = jnp.concatenate([neighbours[-1:, 5], neighbours[:-1, 5]])
@@ -258,13 +257,11 @@
     in_band = band_of >= 0
     owner_dev = band_of // band_here % partners
     source_dev = brick_of_band // bricks_here % partners
-    arrived = lax.all_to_all(
-        place_rows(level_bricks, owner_dev, in_band, partners),
-        "dev",
-        split_axis=0,
-        concat_axis=0,
-        tiled=True,
-    )
+    matches = (owner_dev[None, :] == jnp.arange(partners)[:, None]) & in_band[None, :]
+    chosen = jnp.sum(jnp.where(matches, jnp.arange(bricks_here)[None, :], 0), axis=1)
+    view = lvl.reshape(BXN, BX, BYN, BY, BZN, BZ)
+    sending = view[chosen // (BYN * BZN), :, chosen // BZN % BYN, :, chosen % BZN, :]
+    arrived = lax.all_to_all(sending, "dev", split_axis=0, concat_axis=0, tiled=True)
     return jnp.take(arrived, source_dev, axis=0)
 
 

time: 253 us -> 245 us (0.968)
  other arithmetic: 76.5 us -> 69.3 us
    select_n x2 -> x0, other arithmetic: 5.08 us -> none  [the longest x1 5.08 us: place_rows(): jnp.where(present.reshape((partners,) + (1,) * (values.ndim - 1)), picked...]
where the time goes in v1:
time: 245 us; the launch traced here: 242 us
  waiting for transfers between devices  94.2 us (38%)
  other arithmetic  69.3 us (28%)
  local copies, waits for them, and re-layouts  42.2 us (17%)
  starting transfers between devices  35.8 us (15%)
    all_to_all x1, waiting for transfers between devices, per_device(): lax.all_to_all(sending, 'dev', split_axis=0, concat_axis=0, tiled=True)  94.2 us
    add x4, other arithmetic, region_step(): return centre + time_step * edge * force * jnp.sqrt(1.0 + gradient)  31 us
    ppermute x4, starting transfers between devices, sent(): flat = lax.ppermute(flat, axis, pairs)  13 us
    all_to_all x1, starting transfers between devices, per_device(): lax.all_to_all(sending, 'dev', split_axis=0, concat_axis=0, tiled=True)  12.4 us
    add x3, other arithmetic, smooth_axis(): summed + gauss_taps[offset] * lax.slice_in_dim(values, offset, offset + l...  11 us
    ppermute x4, starting transfers between devices, sent(): image_part = lax.ppermute(pieces[0], axis, pairs)  10.4 us
    slice x4, local copies, waits for them, and re-layouts, region_step(): centre[:, :, 1:]  8 us
    div x1, other arithmetic, edge_map(): 1.0 / (1.0 + (grad_x * grad_x + grad_y * grad_y + grad_z * grad_z) / cont...  6.09 us
  transfers between devices with their start and end apart: 9, of which 1 were waited for; matrix products, arithmetic and copies ran while one was open for 14% of the time, Pallas kernels for 0%

profile of v1, /device:TPU:1, one launch (start us, length us, event | category | flops | bytes accessed | tf_op | source)
XLA Modules:
  0.0 242.0 jit_solution(11652704331463374198)
XLA Ops:
  0.0 0.9 copy.24
  0.9 0.8 select_reduce_fusion.2
  1.9 1.1 fusion.72
  3.1 5.1 %collective-permute-start.1 = (f32[65592]{0:T(1024)S(1)}, f32[65592]{0:T(1024)S(1)}, u32[]{:S(2)}, u32[]{:S(2)}) collective-permute-start(f32[65592]{0:T(1024)S(1)} %pad_maximum_fusion.4), channel_id=1, source_target_pairs={{32,0},{64,32},{96,64},{128,96},{160,128},{192,160},{224,192},{33,... | collective-permute-start | bytes 787112 | tf_op jit(solution)/shard_map/ppermute | solution.py:169
  8.4 1.9 collective-permute-start
  10.3 1.9 collective-permute-start.4
  12.3 2.4 collective-permute-start.5
  14.7 0.6 fusion.61
  15.3 0.5 compare_and_fusion
  15.8 0.6 iota_and_fusion
  16.4 0.6 compare_select_fusion.8
  17.1 0.6 fusion.76
  17.7 1.4 broadcast_compare_fusion
  19.2 0.6 fusion.47
  20.0 1.2 copy-done.2
  21.2 1.0 fusion.73
  22.2 1.3 collective-permute-start.7
  23.5 4.7 %collective-permute-start.6 = (bf16[46,7,512]{2,1,0:T(8,128)(2,1)}, bf16[46,7,512]{2,1,0:T(8,128)(2,1)}, u32[]{:S(2)}, u32[]{:S(2)}) collective-permute-start(bf16[46,7,512]{2,1,0:T(8,128)(2,1)} %get-tuple-element.31), channel_id=1, source_target_pairs={{0,1},{1,2},{2,3},{3,4},{4,5},{5,6},{6,7},{7,8},{8,9},{9,10},{10,1... | collective-permute-start | bytes 989192 | tf_op jit(solution)/shard_map/ppermute | solution.py:167
  28.6 0.3 copy-done.8
  29.1 1.8 constant_dynamic-update-slice_fusion.1
  31.2 1.0 pad_maximum_fusion.2
  32.2 1.3 collective-permute-start.3
  33.7 4.7 %collective-permute-start.2 = (f32[82032]{0:T(1024)S(1)}, f32[82032]{0:T(1024)}, u32[]{:S(2)}, u32[]{:S(2)}) collective-permute-start(f32[82032]{0:T(1024)S(1)} %pad_maximum_fusion.1), channel_id=1, source_target_pairs={{0,1},{1,2},{2,3},{3,4},{4,5},{5,6},{6,7},{7,8},{8,9},{9,10},{10,1... | collective-permute-start | bytes 984392 | tf_op jit(solution)/shard_map/ppermute | solution.py:169
  38.5 3.8 %fusion.35 = f32[46,46,518]{2,1,0:T(8,128)S(1)} fusion(bf16[46,7,512]{2,1,0:T(8,128)(2,1)} %collective-permute-done.7, bf16[46,32,512]{2,1,0:T(8,128)(2,1)} %copy-done.2, bf16[46,7,512]{2,1,0:T(8,128)(2,1)} %collective-permute-done.6), kind=kLoop, calls=%fused_computation.94 | loop fusion | flops 13153056 | bytes 6551136 | tf_op jit(solution)/shard_map/jit(_pad)/pad | solution.py:216
  42.3 2.6 %fusion.9 = f32[42,46,518]{2,1,0:T(8,128)S(1)} fusion(f32[46,46,518]{2,1,0:T(8,128)S(1)} %fusion.35), kind=kLoop, calls=%fused_computation.24 | loop fusion | flops 9006984 | bytes 24018624 | tf_op jit(solution)/shard_map/add | solution.py:49
  44.9 2.9 %fusion.5 = f32[42,42,518]{2,1,0:T(8,128)S(1)} fusion(f32[42,46,518]{2,1,0:T(8,128)S(1)} %fusion.9), kind=kLoop, calls=%fused_computation.15 | loop fusion | flops 8223768 | bytes 21930048 | tf_op jit(solution)/shard_map/add | solution.py:49
  47.8 5.5 %fusion.1 = f32[42,42,514]{2,1,0:T(8,128)S(1)} fusion(f32[42,42,518]{2,1,0:T(8,128)S(1)} %fusion.5), kind=kLoop, calls=%fused_computation.6 | loop fusion | flops 8160264 | bytes 21760704 | tf_op jit(solution)/shard_map/add | solution.py:49
  53.3 6.1 %fusion.18 = f32[40,40,512]{2,1,0:T(8,128)} fusion(f32[42,42,514]{2,1,0:T(8,128)S(1)} %fusion.1), kind=kLoop, calls=%fused_computation.44 | loop fusion | flops 11468800 | bytes 22937600 | tf_op jit(solution)/shard_map/div | solution.py:60
  59.4 1.0 slice.452
  60.4 0.8 reshape.348
  61.2 1.0 slice.449
  62.2 0.8 reshape.345
  63.1 2.3 pad_maximum_fusion
  65.4 4.0 %fusion.64 = (f32[38,38,511]{2,1,0:T(8,128)}, f32[38,38,511]{2,1,0:T(8,128)}) fusion(f32[40,40,512]{2,1,0:T(8,128)S(1)} %pad_maximum_fusion), kind=kLoop, calls=%fused_computation.228 | loop fusion | bytes 11806144 | tf_op jit(solution)/shard_map/slice | solution.py:193
  69.5 1.4 fusion.65
  70.9 0.7 slice.479
  71.7 0.7 slice.478
  72.5 0.4 select_reduce_fusion
  72.9 0.2 slice_reduce_fusion
  73.1 0.9 broadcast_in_dim.159
  74.0 2.1 reshape.352
  76.1 1.7 slice_bitcast_fusion.5
  77.8 0.9 broadcast_in_dim.149
  78.7 2.0 reshape.351
  80.8 1.1 slice_bitcast_fusion.9
  81.9 1.9 select_select_fusion
  83.9 5.2 %shift-left_or_fusion = s32[40,40,512]{2,1,0:T(8,128)S(1)} fusion(s32[512]{0:T(512)S(1)} %copy-done.13, s32[512]{0:T(512)S(1)} %copy-done.14, s32[40]{0:T(128)} %get-tuple-element.53, s32[40]{0:T(128)} %get-tuple-element.54, s32[40,512]{1,0:T(8,128)S(1)} %get-tuple-element.36, s32[40,512]{1,0:T(8,128)S(1)} %get-tuple-element.37, ...), kind=kLoop, calls=%fused_computation.54 | loop fusion | flops 24576000 | bytes 3609568 | tf_op jit(solution)/shard_map/or | solution.py:245
  89.1 10.3 %fusion.29 = f32[38,38,512]{2,1,0:T(8,128)S(1)} fusion(f32[40,40,512]{2,1,0:T(8,128)S(1)} %select_select_fusion, f32[40,40,512]{2,1,0:T(8,128)S(1)} %copy-done, f32[38,38,511]{2,1,0:T(8,128)} %get-tuple-element.12, f32[38,38,1]{2,1,0:T(8,128)S(1)} %copy-done.4, f32[38,38,1]{2,1,0:T(8,128)S(1)} %copy-done.3, f32[38,38,511]{2,1,0:T(8,128)} %get-tuple-element.11, ...), kind=kLoop, calls=%fused_computation.61 | loop fusion | flops 37705728 | bytes 32530432 | tf_op jit(solution)/shard_map/add | solution.py:204
  99.4 1.5 fusion.66
  100.9 0.3 fusion.67
  101.2 7.4 %fusion.32 = f32[36,36,512]{2,1,0:T(8,128)S(1)} fusion(f32[40,40,512]{2,1,0:T(8,128)S(1)} %select_select_fusion, f32[40,40,512]{2,1,0:T(8,128)S(1)} %copy-done, f32[36,36,511]{2,1,0:T(8,128)S(1)} %get-tuple-element.16, f32[36,36,1]{2,1,0:T(8,128)S(1)} %get-tuple-element.18, f32[36,36,1]{2,1,0:T(8,128)S(1)} %get-tuple-element.17, ...), kind=kLoop, calls=%fused_computation.78 | loop fusion | flops 33841152 | bytes 29196288 | tf_op jit(solution)/shard_map/add | solution.py:204
  108.6 1.4 fusion.68
  110.0 0.3 fusion.69
  110.3 8.0 %fusion.38 = f32[34,34,512]{2,1,0:T(8,128)S(1)} fusion(f32[40,40,512]{2,1,0:T(8,128)S(1)} %select_select_fusion, f32[40,40,512]{2,1,0:T(8,128)S(1)} %copy-done, f32[34,34,511]{2,1,0:T(8,128)S(1)} %get-tuple-element.20, f32[34,34,1]{2,1,0:T(8,128)S(1)} %get-tuple-element.22, f32[34,34,1]{2,1,0:T(8,128)S(1)} %get-tuple-element.21, ...), kind=kLoop, calls=%fused_computation.98 | loop fusion | flops 30185472 | bytes 26042368 | tf_op jit(solution)/shard_map/add | solution.py:204
  118.3 1.0 fusion.70
  119.3 0.3 fusion.71
  119.6 5.4 %fusion.41 = f32[32,32,512]{2,1,0:T(8,128)S(1)} fusion(f32[40,40,512]{2,1,0:T(8,128)S(1)} %select_select_fusion, f32[40,40,512]{2,1,0:T(8,128)S(1)} %copy-done, f32[32,32,511]{2,1,0:T(8,128)S(1)} %get-tuple-element.24, f32[32,32,1]{2,1,0:T(8,128)S(1)} %get-tuple-element.26, f32[32,32,1]{2,1,0:T(8,128)S(1)} %get-tuple-element.25, ...), kind=kLoop, calls=%fused_computation.115 | loop fusion | flops 26738688 | bytes 23068672 | tf_op jit(solution)/shard_map/add | solution.py:204
  125.0 1.7 reshape.353
  126.8 1.8 copy.29
  128.6 2.9 %gather_fusion = f32[32,16,16,128]{3,2,1,0:T(8,128)} fusion(f32[2,16,2,16,4,128]{5,3,4,2,1,0:T(8,128)S(1)} %copy.29, s32[32]{0:T(128)S(1)} %fusion.60), kind=kCustom, calls=%fused_computation | custom fusion | bytes 8388992 | tf_op jit(solution)/shard_map/gather | solution.py:263
  131.5 12.4 %all-to-all-start = ((f32[32,16,16,128]{3,2,1,0:T(8,128)}), f32[32,16,16,128]{3,2,1,0:T(8,128)}, u32[]{:S(2)}, u32[]{:S(2)}) async-start(f32[32,16,16,128]{3,2,1,0:T(8,128)} %gather_fusion), calls=%async_computation | async-start | bytes 8388608 | tf_op jit(solution)/shard_map/all_to_all | solution.py:264
  143.9 94.2 %all-to-all-done = f32[32,16,16,128]{3,2,1,0:T(8,128)} async-done(((f32[32,16,16,128]{3,2,1,0:T(8,128)}), f32[32,16,16,128]{3,2,1,0:T(8,128)}, u32[]{:S(2)}, u32[]{:S(2)}) %all-to-all-start) | async-done | bytes 4194336 | tf_op jit(solution)/shard_map/all_to_all | solution.py:264
  238.1 2.8 %gather_fusion.1 = f32[8,16,16,128]{3,2,1,0:T(8,128)S(1)} fusion(f32[32,16,16,128]{3,2,1,0:T(8,128)} %all-to-all-done, s32[1024]{0:T(1024)S(1)} %pad_clamp_fusion), kind=kCustom, calls=%fused_computation.1 | custom fusion | bytes 2097184 | tf_op jit(solution)/shard_map/jit(_take)/gather | solution.py:265
  240.9 1.1 broadcast_select_fusion
  (86 shorter events, 2.3 us)
Async XLA Ops:
  0.0 17.0 %copy-start.12 = (s32[16,6]{0,1:T(8,128)S(1)}, s32[16,6]{0,1:T(8,128)}, u32[]{:S(2)}) copy-start(s32[16,6]{0,1:T(8,128)} %param.11) | copy-start | bytes 1156
  0.0 10.3 %copy-start.5 = (bf16[32,32,512]{2,1,0:T(8,128)(2,1)S(1)}, bf16[32,32,512]{2,1,0:T(8,128)(2,1)}, u32[]{:S(2)}) copy-start(bf16[32,32,512]{2,1,0:T(8,128)(2,1)} %param.7) | copy-start | bytes 3145732
  3.1 25.2 %collective-permute-start.1 = (f32[65592]{0:T(1024)S(1)}, f32[65592]{0:T(1024)S(1)}, u32[]{:S(2)}, u32[]{:S(2)}) collective-permute-start(f32[65592]{0:T(1024)S(1)} %pad_maximum_fusion.4), channel_id=1, source_target_pairs={{32,0},{64,32},{96,64},{128,96},{160,128},{192,160},{224,192},{33,... | collective-permute-start | bytes 787112 | tf_op jit(solution)/shard_map/ppermute | solution.py:169
  8.4 19.9 %collective-permute-start = (f32[65592]{0:T(1024)S(1)}, f32[65592]{0:T(1024)S(1)}, u32[]{:S(2)}, u32[]{:S(2)}) collective-permute-start(f32[65592]{0:T(1024)S(1)} %pad_maximum_fusion.3), channel_id=1, source_target_pairs={{0,32},{32,64},{64,96},{96,128},{128,160},{160,192},{192,224},{1,3... | collective-permute-start | bytes 787112 | tf_op jit(solution)/shard_map/ppermute | solution.py:169
  10.3 9.5 %collective-permute-start.4 = (bf16[7,32,512]{2,1,0:T(8,128)(2,1)S(1)}, bf16[7,32,512]{2,1,0:T(8,128)(2,1)S(1)}, u32[]{:S(2)}, u32[]{:S(2)}) collective-permute-start(bf16[7,32,512]{2,1,0:T(8,128)(2,1)S(1)} %get-tuple-element.34), channel_id=1, source_target_pairs={{0,32},{32,64},{64,96},{96,128},{128,160},{160,192},{192,224},{1,3... | collective-permute-start | bytes 688136 | tf_op jit(solution)/shard_map/ppermute | solution.py:167
  12.3 7.7 %collective-permute-start.5 = (bf16[7,32,512]{2,1,0:T(8,128)(2,1)S(1)}, bf16[7,32,512]{2,1,0:T(8,128)(2,1)S(1)}, u32[]{:S(2)}, u32[]{:S(2)}) collective-permute-start(bf16[7,32,512]{2,1,0:T(8,128)(2,1)S(1)} %get-tuple-element.33), channel_id=1, source_target_pairs={{32,0},{64,32},{96,64},{128,96},{160,128},{192,160},{224,192},{33,... | collective-permute-start | bytes 688136 | tf_op jit(solution)/shard_map/ppermute | solution.py:167
  19.8 8.8 %copy-start.6 = (f32[2,2,4,1]{3,2,1,0:T(4,128)}, f32[2,2,4,1]{3,2,1,0:T(4,128)S(1)}, u32[]{:S(2)}) copy-start(f32[2,2,4,1]{3,2,1,0:T(4,128)S(1)} %concatenate.126) | copy-start | bytes 196
  20.0 1.2 copy-start.2
  22.2 16.3 %collective-permute-start.7 = (bf16[46,7,512]{2,1,0:T(8,128)(2,1)}, bf16[46,7,512]{2,1,0:T(8,128)(2,1)}, u32[]{:S(2)}, u32[]{:S(2)}) collective-permute-start(bf16[46,7,512]{2,1,0:T(8,128)(2,1)} %get-tuple-element.32), channel_id=1, source_target_pairs={{1,0},{2,1},{3,2},{4,3},{5,4},{6,5},{7,6},{8,7},{9,8},{10,9},{11,1... | collective-permute-start | bytes 989192 | tf_op jit(solution)/shard_map/ppermute | solution.py:167
  23.5 15.0 %collective-permute-start.6 = (bf16[46,7,512]{2,1,0:T(8,128)(2,1)}, bf16[46,7,512]{2,1,0:T(8,128)(2,1)}, u32[]{:S(2)}, u32[]{:S(2)}) collective-permute-start(bf16[46,7,512]{2,1,0:T(8,128)(2,1)} %get-tuple-element.31), channel_id=1, source_target_pairs={{0,1},{1,2},{2,3},{3,4},{4,5},{5,6},{6,7},{7,8},{8,9},{9,10},{10,1... | collective-permute-start | bytes 989192 | tf_op jit(solution)/shard_map/ppermute | solution.py:167
  28.3 0.6 copy-start.8
  28.4 0.6 copy-start.10
  31.0 11.3 %copy-start.1 = (f32[40,32,512]{2,1,0:T(8,128)}, f32[40,32,512]{2,1,0:T(8,128)S(1)}, u32[]{:S(2)}) copy-start(f32[40,32,512]{2,1,0:T(8,128)S(1)} %constant_dynamic-update-slice_fusion) | copy-start | bytes 7864324
  32.2 27.2 %collective-permute-start.3 = (f32[82032]{0:T(1024)}, f32[82032]{0:T(1024)}, u32[]{:S(2)}, u32[]{:S(2)}) collective-permute-start(f32[82032]{0:T(1024)} %pad_maximum_fusion.2), channel_id=1, source_target_pairs={{1,0},{2,1},{3,2},{4,3},{5,4},{6,5},{7,6},{8,7},{9,8},{10,9},{11,1... | collective-permute-start | bytes 984392 | tf_op jit(solution)/shard_map/ppermute | solution.py:169
  33.7 27.5 %collective-permute-start.2 = (f32[82032]{0:T(1024)S(1)}, f32[82032]{0:T(1024)}, u32[]{:S(2)}, u32[]{:S(2)}) collective-permute-start(f32[82032]{0:T(1024)S(1)} %pad_maximum_fusion.1), channel_id=1, source_target_pairs={{0,1},{1,2},{2,3},{3,4},{4,5},{5,6},{6,7},{7,8},{8,9},{9,10},{10,1... | collective-permute-start | bytes 984392 | tf_op jit(solution)/shard_map/ppermute | solution.py:169
  69.5 3.0 %copy-start.7 = (f32[2,2,4,1]{3,2,1,0:T(4,128)S(1)}, f32[2,2,4,1]{3,2,1,0:T(4,128)}, u32[]{:S(2)}) copy-start(f32[2,2,4,1]{3,2,1,0:T(4,128)} %copy-done.6) | copy-start | bytes 196
  69.5 3.0 %copy-start.9 = (f32[1,2,4,7]{3,2,1,0:T(4,128)S(1)}, f32[1,2,4,7]{3,2,1,0:T(4,128)}, u32[]{:S(2)}) copy-start(f32[1,2,4,7]{3,2,1,0:T(4,128)} %copy-done.8) | copy-start | bytes 676
  69.5 3.0 %copy-start.11 = (f32[1,2,4,7]{3,2,1,0:T(4,128)S(1)}, f32[1,2,4,7]{3,2,1,0:T(4,128)}, u32[]{:S(2)}) copy-start(f32[1,2,4,7]{3,2,1,0:T(4,128)} %copy-done.10) | copy-start | bytes 676
  69.5 3.0 %copy-start.18 = (s32[7]{0:T(128)S(1)}, s32[7]{0:T(128)}, u32[]{:S(2)}) copy-start(s32[7]{0:T(128)} %constant.240.clone) | copy-start | bytes 88
  70.9 10.9 %copy-start.15 = (pred[40]{0:T(512)(128)(4,1)S(1)}, pred[40]{0:T(512)(128)(4,1)}, u32[]{:S(2)}) copy-start(pred[40]{0:T(512)(128)(4,1)} %get-tuple-element.51) | copy-start | bytes 124
  77.8 6.1 %copy-start.13 = (s32[512]{0:T(512)S(1)}, s32[512]{0:T(512)}, u32[]{:S(2)}) copy-start(s32[512]{0:T(512)} %get-tuple-element.55) | copy-start | bytes 6148
  77.8 6.1 %copy-start.14 = (s32[512]{0:T(512)S(1)}, s32[512]{0:T(512)}, u32[]{:S(2)}) copy-start(s32[512]{0:T(512)} %get-tuple-element.56) | copy-start | bytes 6148
  77.8 6.1 %copy-start.16 = (pred[40]{0:T(512)(128)(4,1)S(1)}, pred[40]{0:T(512)(128)(4,1)}, u32[]{:S(2)}) copy-start(pred[40]{0:T(512)(128)(4,1)} %get-tuple-element.52) | copy-start | bytes 124
  77.8 6.1 %copy-start.17 = (pred[40]{0:T(512)(128)(4,1)S(1)}, pred[40]{0:T(512)(128)(4,1)}, u32[]{:S(2)}) copy-start(pred[40]{0:T(512)(128)(4,1)} %get-tuple-element.58) | copy-start | bytes 124
  81.9 7.2 %copy-start = (f32[40,40,512]{2,1,0:T(8,128)S(1)}, f32[40,40,512]{2,1,0:T(8,128)}, u32[]{:S(2)}) copy-start(f32[40,40,512]{2,1,0:T(8,128)} %fusion.18) | copy-start | bytes 9830404
  81.9 7.2 %copy-start.3 = (f32[38,38,1]{2,1,0:T(8,128)S(1)}, f32[38,38,1]{2,1,0:T(8,128)}, u32[]{:S(2)}) copy-start(f32[38,38,1]{2,1,0:T(8,128)} %get-tuple-element.13) | copy-start | bytes 17332
  81.9 7.2 %copy-start.4 = (f32[38,38,1]{2,1,0:T(8,128)S(1)}, f32[38,38,1]{2,1,0:T(8,128)}, u32[]{:S(2)}) copy-start(f32[38,38,1]{2,1,0:T(8,128)} %get-tuple-element.14) | copy-start | bytes 17332
  131.5 12.4 %copy-start.19 = (s32[8]{0:T(128)S(1)}, s32[8]{0:T(128)}, u32[]{:S(2)}) copy-start(s32[8]{0:T(128)} %param.10) | copy-start | bytes 100
  131.5 106.6 %all-to-all-start = ((f32[32,16,16,128]{3,2,1,0:T(8,128)}), f32[32,16,16,128]{3,2,1,0:T(8,128)}, u32[]{:S(2)}, u32[]{:S(2)}) async-start(f32[32,16,16,128]{3,2,1,0:T(8,128)} %gather_fusion), calls=%async_computation | async-start | bytes 8388608 | tf_op jit(solution)/shard_map/all_to_all | solution.py:264

commit v2 on v1

--- a/solution.py
+++ b/solution.py
@@ -261,7 +261,11 @@
     chosen = jnp.sum(jnp.where(matches, jnp.arange(bricks_here)[None, :], 0), axis=1)
     view = lvl.reshape(BXN, BX, BYN, BY, BZN, BZ)
     sending = view[chosen // (BYN * BZN), :, chosen // BZN % BYN, :, chosen % BZN, :]
-    arrived = lax.all_to_all(sending, "dev", split_axis=0, concat_axis=0, tiled=True)
+    halves = [
+        lax.all_to_all(part, "dev", split_axis=0, concat_axis=0, tiled=True)
+        for part in (sending[:, : BX // 2], sending[:, BX // 2 :])
+    ]
+    arrived = jnp.concatenate(halves, axis=1)
     return jnp.take(arrived, source_dev, axis=0)
 
 

time: 245 us -> 262 us (1.069)
  blocking collectives: 0 us -> 59.7 us
  waiting for transfers between devices: 94.2 us -> 49.2 us
  starting transfers between devices: 35.8 us -> 31.6 us
  other arithmetic: 69.3 us -> 73.2 us
  local copies, waits for them, and re-layouts: 42.2 us -> 46 us
    all_to_all x0 -> x1, blocking collectives: none -> 59.7 us  [per_device(): lax.all_to_all(part, 'dev', split_axis=0, concat_axis=0, tiled=True)]
    all_to_all x1, waiting for transfers between devices: 94.2 us -> 49.2 us  [per_device(): lax.all_to_all(part, 'dev', split_axis=0, concat_axis=0, tiled=True)]
    all_to_all x1, starting transfers between devices: 12.4 us -> 8.21 us  [per_device(): lax.all_to_all(part, 'dev', split_axis=0, concat_axis=0, tiled=True)]
    slice x0 -> x1, local copies, waits for them, and re-layouts: none -> 4.03 us  [per_device(): sending[:, :BX // 2]]
    concatenate x0 -> x1, other arithmetic: none -> 3.97 us  [per_device(): arrived = jnp.concatenate(halves, axis=1)]
  transfers between devices with their start and end apart: 9 -> 9, of which waited for: 1 -> 1; matrix products, arithmetic and copies ran while one was open for 14% -> 13% of each run, Pallas kernels for 0% -> 0%
where the time goes in v2:
time: 262 us; the launch traced here: 260 us
  other arithmetic  73.2 us (28%)
  blocking collectives  59.7 us (23%)
  waiting for transfers between devices  49.2 us (19%)
  local copies, waits for them, and re-layouts  46 us (18%)
  starting transfers between devices  31.6 us (12%)
    all_to_all x1, blocking collectives, per_device(): lax.all_to_all(part, 'dev', split_axis=0, concat_axis=0, tiled=True)  59.7 us
    all_to_all x1, waiting for transfers between devices, per_device(): lax.all_to_all(part, 'dev', split_axis=0, concat_axis=0, tiled=True)  49.2 us
    add x4, other arithmetic, region_step(): return centre + time_step * edge * force * jnp.sqrt(1.0 + gradient)  31 us
    ppermute x4, starting transfers between devices, sent(): flat = lax.ppermute(flat, axis, pairs)  13 us
    add x3, other arithmetic, smooth_axis(): summed + gauss_taps[offset] * lax.slice_in_dim(values, offset, offset + l...  11 us
    ppermute x4, starting transfers between devices, sent(): image_part = lax.ppermute(pieces[0], axis, pairs)  10.4 us
    all_to_all x1, starting transfers between devices, per_device(): lax.all_to_all(part, 'dev', split_axis=0, concat_axis=0, tiled=True)  8.21 us
    slice x4, local copies, waits for them, and re-layouts, region_step(): centre[:, :, 1:]  8 us
  transfers between devices with their start and end apart: 9, of which 1 were waited for; matrix products, arithmetic and copies ran while one was open for 13% of the time, Pallas kernels for 0%

profile of v2, /device:TPU:1, one launch (start us, length us, event | category | flops | bytes accessed | tf_op | source)
XLA Modules:
  0.0 260.4 jit_solution(10500340136836143902)
XLA Ops:
  0.0 0.9 copy.24
  0.9 0.8 select_reduce_fusion.2
  1.9 1.1 fusion.73
  3.1 5.1 %collective-permute-start.1 = (f32[65592]{0:T(1024)S(1)}, f32[65592]{0:T(1024)S(1)}, u32[]{:S(2)}, u32[]{:S(2)}) collective-permute-start(f32[65592]{0:T(1024)S(1)} %pad_maximum_fusion.5), channel_id=1, source_target_pairs={{32,0},{64,32},{96,64},{128,96},{160,128},{192,160},{224,192},{33,... | collective-permute-start | bytes 787112 | tf_op jit(solution)/shard_map/ppermute | solution.py:169
  8.4 1.9 collective-permute-start
  10.3 1.9 collective-permute-start.4
  12.3 2.4 collective-permute-start.5
  14.7 0.6 fusion.61
  15.3 0.6 compare_and_fusion
  15.8 0.6 iota_and_fusion
  16.4 0.6 compare_select_fusion.8
  17.1 0.6 fusion.77
  17.7 1.3 broadcast_compare_fusion
  19.2 0.5 fusion.47
  20.0 1.2 copy-done.2
  21.1 1.0 fusion.74
  22.1 1.3 collective-permute-start.7
  23.4 4.7 %collective-permute-start.6 = (bf16[46,7,512]{2,1,0:T(8,128)(2,1)}, bf16[46,7,512]{2,1,0:T(8,128)(2,1)}, u32[]{:S(2)}, u32[]{:S(2)}) collective-permute-start(bf16[46,7,512]{2,1,0:T(8,128)(2,1)} %get-tuple-element.33), channel_id=1, source_target_pairs={{0,1},{1,2},{2,3},{3,4},{4,5},{5,6},{6,7},{7,8},{8,9},{9,10},{10,1... | collective-permute-start | bytes 989192 | tf_op jit(solution)/shard_map/ppermute | solution.py:167
  29.0 1.8 constant_dynamic-update-slice_fusion.1
  31.2 1.0 pad_maximum_fusion.3
  32.1 1.3 collective-permute-start.3
  33.6 4.7 %collective-permute-start.2 = (f32[82032]{0:T(1024)S(1)}, f32[82032]{0:T(1024)}, u32[]{:S(2)}, u32[]{:S(2)}) collective-permute-start(f32[82032]{0:T(1024)S(1)} %pad_maximum_fusion.2), channel_id=1, source_target_pairs={{0,1},{1,2},{2,3},{3,4},{4,5},{5,6},{6,7},{7,8},{8,9},{9,10},{10,1... | collective-permute-start | bytes 984392 | tf_op jit(solution)/shard_map/ppermute | solution.py:169
  38.4 3.8 %fusion.35 = f32[46,46,518]{2,1,0:T(8,128)S(1)} fusion(bf16[46,7,512]{2,1,0:T(8,128)(2,1)} %collective-permute-done.7, bf16[46,32,512]{2,1,0:T(8,128)(2,1)} %copy-done.2, bf16[46,7,512]{2,1,0:T(8,128)(2,1)} %collective-permute-done.6), kind=kLoop, calls=%fused_computation.95 | loop fusion | flops 13153056 | bytes 6551136 | tf_op jit(solution)/shard_map/jit(_pad)/pad | solution.py:216
  42.2 2.6 %fusion.9 = f32[42,46,518]{2,1,0:T(8,128)S(1)} fusion(f32[46,46,518]{2,1,0:T(8,128)S(1)} %fusion.35), kind=kLoop, calls=%fused_computation.24 | loop fusion | flops 9006984 | bytes 24018624 | tf_op jit(solution)/shard_map/add | solution.py:49
  44.8 2.9 %fusion.5 = f32[42,42,518]{2,1,0:T(8,128)S(1)} fusion(f32[42,46,518]{2,1,0:T(8,128)S(1)} %fusion.9), kind=kLoop, calls=%fused_computation.15 | loop fusion | flops 8223768 | bytes 21930048 | tf_op jit(solution)/shard_map/add | solution.py:49
  47.7 5.5 %fusion.1 = f32[42,42,514]{2,1,0:T(8,128)S(1)} fusion(f32[42,42,518]{2,1,0:T(8,128)S(1)} %fusion.5), kind=kLoop, calls=%fused_computation.6 | loop fusion | flops 8160264 | bytes 21760704 | tf_op jit(solution)/shard_map/add | solution.py:49
  53.2 6.1 %fusion.18 = f32[40,40,512]{2,1,0:T(8,128)} fusion(f32[42,42,514]{2,1,0:T(8,128)S(1)} %fusion.1), kind=kLoop, calls=%fused_computation.45 | loop fusion | flops 11468800 | bytes 22937600 | tf_op jit(solution)/shard_map/div | solution.py:60
  59.3 1.0 slice.460
  60.3 0.8 reshape.348
  61.1 1.0 slice.457
  62.1 0.8 reshape.345
  63.0 2.3 pad_maximum_fusion.1
  65.3 4.1 %fusion.65 = (f32[38,38,511]{2,1,0:T(8,128)}, f32[38,38,511]{2,1,0:T(8,128)}) fusion(f32[40,40,512]{2,1,0:T(8,128)S(1)} %pad_maximum_fusion.1), kind=kLoop, calls=%fused_computation.230 | loop fusion | bytes 11806144 | tf_op jit(solution)/shard_map/slice | solution.py:193
  69.4 1.4 fusion.66
  70.8 0.7 slice.487
  71.6 0.7 slice.486
  72.4 0.4 select_reduce_fusion
  73.0 0.9 broadcast_in_dim.159
  73.9 2.1 reshape.352
  76.0 1.7 slice_bitcast_fusion.5
  77.7 0.9 broadcast_in_dim.149
  78.6 2.0 reshape.351
  80.7 1.1 slice_bitcast_fusion.9
  81.8 1.9 select_select_fusion
  83.8 5.2 %shift-left_or_fusion = s32[40,40,512]{2,1,0:T(8,128)S(1)} fusion(s32[512]{0:T(512)S(1)} %copy-done.13, s32[512]{0:T(512)S(1)} %copy-done.14, s32[40]{0:T(128)} %get-tuple-element.55, s32[40]{0:T(128)} %get-tuple-element.56, s32[40,512]{1,0:T(8,128)S(1)} %get-tuple-element.38, s32[40,512]{1,0:T(8,128)S(1)} %get-tuple-element.39, ...), kind=kLoop, calls=%fused_computation.55 | loop fusion | flops 24576000 | bytes 3609568 | tf_op jit(solution)/shard_map/or | solution.py:245
  89.0 10.3 %fusion.29 = f32[38,38,512]{2,1,0:T(8,128)S(1)} fusion(f32[40,40,512]{2,1,0:T(8,128)S(1)} %select_select_fusion, f32[40,40,512]{2,1,0:T(8,128)S(1)} %copy-done, f32[38,38,511]{2,1,0:T(8,128)} %get-tuple-element.14, f32[38,38,1]{2,1,0:T(8,128)S(1)} %copy-done.4, f32[38,38,1]{2,1,0:T(8,128)S(1)} %copy-done.3, f32[38,38,511]{2,1,0:T(8,128)} %get-tuple-element.13, ...), kind=kLoop, calls=%fused_computation.62 | loop fusion | flops 37705728 | bytes 32530432 | tf_op jit(solution)/shard_map/add | solution.py:204
  99.3 1.5 fusion.67
  100.8 0.3 fusion.68
  101.1 7.4 %fusion.32 = f32[36,36,512]{2,1,0:T(8,128)S(1)} fusion(f32[40,40,512]{2,1,0:T(8,128)S(1)} %select_select_fusion, f32[40,40,512]{2,1,0:T(8,128)S(1)} %copy-done, f32[36,36,511]{2,1,0:T(8,128)S(1)} %get-tuple-element.18, f32[36,36,1]{2,1,0:T(8,128)S(1)} %get-tuple-element.20, f32[36,36,1]{2,1,0:T(8,128)S(1)} %get-tuple-element.19, ...), kind=kLoop, calls=%fused_computation.79 | loop fusion | flops 33841152 | bytes 29196288 | tf_op jit(solution)/shard_map/add | solution.py:204
  108.5 1.4 fusion.69
  109.9 0.3 fusion.70
  110.2 8.0 %fusion.38 = f32[34,34,512]{2,1,0:T(8,128)S(1)} fusion(f32[40,40,512]{2,1,0:T(8,128)S(1)} %select_select_fusion, f32[40,40,512]{2,1,0:T(8,128)S(1)} %copy-done, f32[34,34,511]{2,1,0:T(8,128)S(1)} %get-tuple-element.22, f32[34,34,1]{2,1,0:T(8,128)S(1)} %get-tuple-element.24, f32[34,34,1]{2,1,0:T(8,128)S(1)} %get-tuple-element.23, ...), kind=kLoop, calls=%fused_computation.99 | loop fusion | flops 30185472 | bytes 26042368 | tf_op jit(solution)/shard_map/add | solution.py:204
  118.2 1.0 fusion.71
  119.5 5.4 %fusion.41 = f32[32,32,512]{2,1,0:T(8,128)S(1)} fusion(f32[40,40,512]{2,1,0:T(8,128)S(1)} %select_select_fusion, f32[40,40,512]{2,1,0:T(8,128)S(1)} %copy-done, f32[32,32,511]{2,1,0:T(8,128)S(1)} %get-tuple-element.26, f32[32,32,1]{2,1,0:T(8,128)S(1)} %get-tuple-element.28, f32[32,32,1]{2,1,0:T(8,128)S(1)} %get-tuple-element.27, ...), kind=kLoop, calls=%fused_computation.116 | loop fusion | flops 26738688 | bytes 23068672 | tf_op jit(solution)/shard_map/add | solution.py:204
  124.9 1.7 reshape.353
  126.7 1.8 copy.29
  128.4 2.8 %gather_fusion = f32[32,16,16,128]{3,2,1,0:T(8,128)} fusion(f32[2,16,2,16,4,128]{5,3,4,2,1,0:T(8,128)S(1)} %copy.29, s32[32]{0:T(128)S(1)} %fusion.60), kind=kCustom, calls=%fused_computation | custom fusion | bytes 8388992 | tf_op jit(solution)/shard_map/gather | solution.py:263
  131.3 4.0 %fusion.64 = (f32[32,8,16,128]{3,2,1,0:T(8,128)}, f32[32,8,16,128]{3,2,1,0:T(8,128)S(1)}) fusion(f32[32,16,16,128]{3,2,1,0:T(8,128)} %gather_fusion), kind=kLoop, calls=%fused_computation.229 | loop fusion | bytes 8388608 | tf_op jit(solution)/shard_map/slice | solution.py:266
  135.3 59.7 %all_to_all.10 = f32[32,8,16,128]{3,2,1,0:T(8,128)S(1)} all-to-all(f32[32,8,16,128]{3,2,1,0:T(8,128)S(1)} %get-tuple-element.12), channel_id=1, replica_groups=mesh['group'=8,'dev'=32] {'dev'}, dimensions={0} | all-to-all | bytes 4194304 | tf_op jit(solution)/shard_map/all_to_all | solution.py:265
  195.0 8.2 %all-to-all-start = ((f32[32,8,16,128]{3,2,1,0:T(8,128)}), f32[32,8,16,128]{3,2,1,0:T(8,128)}, u32[]{:S(2)}, u32[]{:S(2)}) async-start(f32[32,8,16,128]{3,2,1,0:T(8,128)} %get-tuple-element.11), calls=%async_computation | async-start | bytes 4194304 | tf_op jit(solution)/shard_map/all_to_all | solution.py:265
  203.3 49.2 %all-to-all-done = f32[32,8,16,128]{3,2,1,0:T(8,128)} async-done(((f32[32,8,16,128]{3,2,1,0:T(8,128)}), f32[32,8,16,128]{3,2,1,0:T(8,128)}, u32[]{:S(2)}, u32[]{:S(2)}) %all-to-all-start) | async-done | bytes 2097184 | tf_op jit(solution)/shard_map/all_to_all | solution.py:265
  252.5 4.0 %pad_maximum_fusion = f32[32,16,16,128]{3,2,1,0:T(8,128)} fusion(f32[32,8,16,128]{3,2,1,0:T(8,128)S(1)} %all_to_all.10, f32[32,8,16,128]{3,2,1,0:T(8,128)} %all-to-all-done), kind=kLoop, calls=%fused_computation.38 | loop fusion | flops 1048576 | bytes 8388608 | tf_op jit(solution)/shard_map/concatenate | solution.py:268
  256.5 2.8 %gather_fusion.1 = f32[8,16,16,128]{3,2,1,0:T(8,128)S(1)} fusion(f32[32,16,16,128]{3,2,1,0:T(8,128)} %pad_maximum_fusion, s32[1024]{0:T(1024)S(1)} %pad_clamp_fusion), kind=kCustom, calls=%fused_computation.1 | custom fusion | bytes 2097184 | tf_op jit(solution)/shard_map/jit(_take)/gather | solution.py:269
  259.3 1.1 broadcast_select_fusion
  (89 shorter events, 3.0 us)
Async XLA Ops:
  0.0 17.0 %copy-start.12 = (s32[16,6]{0,1:T(8,128)S(1)}, s32[16,6]{0,1:T(8,128)}, u32[]{:S(2)}) copy-start(s32[16,6]{0,1:T(8,128)} %param.11) | copy-start | bytes 1156
  0.0 10.3 %copy-start.5 = (bf16[32,32,512]{2,1,0:T(8,128)(2,1)S(1)}, bf16[32,32,512]{2,1,0:T(8,128)(2,1)}, u32[]{:S(2)}) copy-start(bf16[32,32,512]{2,1,0:T(8,128)(2,1)} %param.7) | copy-start | bytes 3145732
  3.1 25.1 %collective-permute-start.1 = (f32[65592]{0:T(1024)S(1)}, f32[65592]{0:T(1024)S(1)}, u32[]{:S(2)}, u32[]{:S(2)}) collective-permute-start(f32[65592]{0:T(1024)S(1)} %pad_maximum_fusion.5), channel_id=1, source_target_pairs={{32,0},{64,32},{96,64},{128,96},{160,128},{192,160},{224,192},{33,... | collective-permute-start | bytes 787112 | tf_op jit(solution)/shard_map/ppermute | solution.py:169
  8.4 19.9 %collective-permute-start = (f32[65592]{0:T(1024)S(1)}, f32[65592]{0:T(1024)S(1)}, u32[]{:S(2)}, u32[]{:S(2)}) collective-permute-start(f32[65592]{0:T(1024)S(1)} %pad_maximum_fusion.4), channel_id=1, source_target_pairs={{0,32},{32,64},{64,96},{96,128},{128,160},{160,192},{192,224},{1,3... | collective-permute-start | bytes 787112 | tf_op jit(solution)/shard_map/ppermute | solution.py:169
  10.3 9.5 %collective-permute-start.4 = (bf16[7,32,512]{2,1,0:T(8,128)(2,1)S(1)}, bf16[7,32,512]{2,1,0:T(8,128)(2,1)S(1)}, u32[]{:S(2)}, u32[]{:S(2)}) collective-permute-start(bf16[7,32,512]{2,1,0:T(8,128)(2,1)S(1)} %get-tuple-element.36), channel_id=1, source_target_pairs={{0,32},{32,64},{64,96},{96,128},{128,160},{160,192},{192,224},{1,3... | collective-permute-start | bytes 688136 | tf_op jit(solution)/shard_map/ppermute | solution.py:167
  12.3 7.7 %collective-permute-start.5 = (bf16[7,32,512]{2,1,0:T(8,128)(2,1)S(1)}, bf16[7,32,512]{2,1,0:T(8,128)(2,1)S(1)}, u32[]{:S(2)}, u32[]{:S(2)}) collective-permute-start(bf16[7,32,512]{2,1,0:T(8,128)(2,1)S(1)} %get-tuple-element.35), channel_id=1, source_target_pairs={{32,0},{64,32},{96,64},{128,96},{160,128},{192,160},{224,192},{33,... | collective-permute-start | bytes 688136 | tf_op jit(solution)/shard_map/ppermute | solution.py:167
  19.7 8.8 %copy-start.6 = (f32[2,2,4,1]{3,2,1,0:T(4,128)}, f32[2,2,4,1]{3,2,1,0:T(4,128)S(1)}, u32[]{:S(2)}) copy-start(f32[2,2,4,1]{3,2,1,0:T(4,128)S(1)} %concatenate.130) | copy-start | bytes 196
  20.0 1.2 copy-start.2
  22.1 16.2 %collective-permute-start.7 = (bf16[46,7,512]{2,1,0:T(8,128)(2,1)}, bf16[46,7,512]{2,1,0:T(8,128)(2,1)}, u32[]{:S(2)}, u32[]{:S(2)}) collective-permute-start(bf16[46,7,512]{2,1,0:T(8,128)(2,1)} %get-tuple-element.34), channel_id=1, source_target_pairs={{1,0},{2,1},{3,2},{4,3},{5,4},{6,5},{7,6},{8,7},{9,8},{10,9},{11,1... | collective-permute-start | bytes 989192 | tf_op jit(solution)/shard_map/ppermute | solution.py:167
  23.4 15.0 %collective-permute-start.6 = (bf16[46,7,512]{2,1,0:T(8,128)(2,1)}, bf16[46,7,512]{2,1,0:T(8,128)(2,1)}, u32[]{:S(2)}, u32[]{:S(2)}) collective-permute-start(bf16[46,7,512]{2,1,0:T(8,128)(2,1)} %get-tuple-element.33), channel_id=1, source_target_pairs={{0,1},{1,2},{2,3},{3,4},{4,5},{5,6},{6,7},{7,8},{8,9},{9,10},{10,1... | collective-permute-start | bytes 989192 | tf_op jit(solution)/shard_map/ppermute | solution.py:167
  28.2 0.6 copy-start.8
  28.3 0.6 copy-start.10
  30.9 11.3 %copy-start.1 = (f32[40,32,512]{2,1,0:T(8,128)}, f32[40,32,512]{2,1,0:T(8,128)S(1)}, u32[]{:S(2)}) copy-start(f32[40,32,512]{2,1,0:T(8,128)S(1)} %constant_dynamic-update-slice_fusion) | copy-start | bytes 7864324
  32.1 27.2 %collective-permute-start.3 = (f32[82032]{0:T(1024)}, f32[82032]{0:T(1024)}, u32[]{:S(2)}, u32[]{:S(2)}) collective-permute-start(f32[82032]{0:T(1024)} %pad_maximum_fusion.3), channel_id=1, source_target_pairs={{1,0},{2,1},{3,2},{4,3},{5,4},{6,5},{7,6},{8,7},{9,8},{10,9},{11,1... | collective-permute-start | bytes 984392 | tf_op jit(solution)/shard_map/ppermute | solution.py:169
  33.6 27.5 %collective-permute-start.2 = (f32[82032]{0:T(1024)S(1)}, f32[82032]{0:T(1024)}, u32[]{:S(2)}, u32[]{:S(2)}) collective-permute-start(f32[82032]{0:T(1024)S(1)} %pad_maximum_fusion.2), channel_id=1, source_target_pairs={{0,1},{1,2},{2,3},{3,4},{4,5},{5,6},{6,7},{7,8},{8,9},{9,10},{10,1... | collective-permute-start | bytes 984392 | tf_op jit(solution)/shard_map/ppermute | solution.py:169
  69.4 3.0 %copy-start.7 = (f32[2,2,4,1]{3,2,1,0:T(4,128)S(1)}, f32[2,2,4,1]{3,2,1,0:T(4,128)}, u32[]{:S(2)}) copy-start(f32[2,2,4,1]{3,2,1,0:T(4,128)} %copy-done.6) | copy-start | bytes 196
  69.4 3.0 %copy-start.9 = (f32[1,2,4,7]{3,2,1,0:T(4,128)S(1)}, f32[1,2,4,7]{3,2,1,0:T(4,128)}, u32[]{:S(2)}) copy-start(f32[1,2,4,7]{3,2,1,0:T(4,128)} %copy-done.8) | copy-start | bytes 676
  69.4 3.0 %copy-start.11 = (f32[1,2,4,7]{3,2,1,0:T(4,128)S(1)}, f32[1,2,4,7]{3,2,1,0:T(4,128)}, u32[]{:S(2)}) copy-start(f32[1,2,4,7]{3,2,1,0:T(4,128)} %copy-done.10) | copy-start | bytes 676
  69.4 3.0 %copy-start.18 = (s32[7]{0:T(128)S(1)}, s32[7]{0:T(128)}, u32[]{:S(2)}) copy-start(s32[7]{0:T(128)} %constant.240.clone) | copy-start | bytes 88
  70.8 10.9 %copy-start.15 = (pred[40]{0:T(512)(128)(4,1)S(1)}, pred[40]{0:T(512)(128)(4,1)}, u32[]{:S(2)}) copy-start(pred[40]{0:T(512)(128)(4,1)} %get-tuple-element.53) | copy-start | bytes 124
  77.7 6.1 %copy-start.13 = (s32[512]{0:T(512)S(1)}, s32[512]{0:T(512)}, u32[]{:S(2)}) copy-start(s32[512]{0:T(512)} %get-tuple-element.57) | copy-start | bytes 6148
  77.7 6.1 %copy-start.14 = (s32[512]{0:T(512)S(1)}, s32[512]{0:T(512)}, u32[]{:S(2)}) copy-start(s32[512]{0:T(512)} %get-tuple-element.58) | copy-start | bytes 6148
  77.7 6.1 %copy-start.16 = (pred[40]{0:T(512)(128)(4,1)S(1)}, pred[40]{0:T(512)(128)(4,1)}, u32[]{:S(2)}) copy-start(pred[40]{0:T(512)(128)(4,1)} %get-tuple-element.54) | copy-start | bytes 124
  77.7 6.1 %copy-start.17 = (pred[40]{0:T(512)(128)(4,1)S(1)}, pred[40]{0:T(512)(128)(4,1)}, u32[]{:S(2)}) copy-start(pred[40]{0:T(512)(128)(4,1)} %get-tuple-element.60) | copy-start | bytes 124
  81.8 7.2 %copy-start = (f32[40,40,512]{2,1,0:T(8,128)S(1)}, f32[40,40,512]{2,1,0:T(8,128)}, u32[]{:S(2)}) copy-start(f32[40,40,512]{2,1,0:T(8,128)} %fusion.18) | copy-start | bytes 9830404
  81.8 7.2 %copy-start.3 = (f32[38,38,1]{2,1,0:T(8,128)S(1)}, f32[38,38,1]{2,1,0:T(8,128)}, u32[]{:S(2)}) copy-start(f32[38,38,1]{2,1,0:T(8,128)} %get-tuple-element.15) | copy-start | bytes 17332
  81.8 7.2 %copy-start.4 = (f32[38,38,1]{2,1,0:T(8,128)S(1)}, f32[38,38,1]{2,1,0:T(8,128)}, u32[]{:S(2)}) copy-start(f32[38,38,1]{2,1,0:T(8,128)} %get-tuple-element.16) | copy-start | bytes 17332
  195.0 8.2 %copy-start.19 = (s32[8]{0:T(128)S(1)}, s32[8]{0:T(128)}, u32[]{:S(2)}) copy-start(s32[8]{0:T(128)} %param.10) | copy-start | bytes 100
  195.0 57.5 %all-to-all-start = ((f32[32,8,16,128]{3,2,1,0:T(8,128)}), f32[32,8,16,128]{3,2,1,0:T(8,128)}, u32[]{:S(2)}, u32[]{:S(2)}) async-start(f32[32,8,16,128]{3,2,1,0:T(8,128)} %get-tuple-element.11), calls=%async_computation | async-start | bytes 4194304 | tf_op jit(solution)/shard_map/all_to_all | solution.py:265

commit v3 on v1

--- a/solution.py
+++ b/solution.py
@@ -152,7 +152,7 @@
 
 def extended_packed(em_image, level_set, info):
     cells = [em_image, level_set, info]
-    widths = [3 + STEPS, STEPS, 1]
+    widths = [2 + STEPS, STEPS, 1]
     for axis, dim in (("group", 0), ("dev", 1)):
         count = lax.axis_size(axis)
         ends = count - 1
@@ -216,26 +216,27 @@
     window = jnp.pad(margin.astype(jnp.float32), ((0, 0), (0, 0), (3, 3)))
     edge = edge_map(window)
     span_x, span_y, span_z = wide_level.shape
-    lead = BX - STEPS
+    lead = BX - STEPS + 1
+    inner_shape = (span_x - 2, span_y - 2, span_z)
     weights = jnp.asarray([1 << side for side in range(6)] + [0], jnp.int32)
     brick_code = jnp.sum(jnp.where(wide_info > 0.5, weights, 0), axis=-1)
     def planes(per_brick):
         spread = jnp.broadcast_to(
             per_brick.reshape(BXN + 2, BYN + 2, 1, BZN, 1), (BXN + 2, BYN + 2, BY, BZN, BZ)
         ).reshape(BXN + 2, (BYN + 2) * BY, BZN * BZ)
-        return spread[:, lead : lead + span_y]
+        return spread[:, lead : lead + span_y - 2]
     def across_x(per_brick):
         table = planes(per_brick)
-        xe = lax.broadcasted_iota(jnp.int32, wide_level.shape, 0) + lead
+        xe = lax.broadcasted_iota(jnp.int32, inner_shape, 0) + lead
         value = table[BXN + 1][None]
         for bx in range(BXN, -1, -1):
             value = jnp.where(xe < (bx + 1) * BX, table[bx][None], value)
         return value
     rate = across_x(wide_info[..., 6])
     place = (
-        lax.broadcasted_iota(jnp.int32, wide_level.shape, 0) + lead,
-        lax.broadcasted_iota(jnp.int32, wide_level.shape, 1) + lead,
-        lax.broadcasted_iota(jnp.int32, wide_level.shape, 2),
+        lax.broadcasted_iota(jnp.int32, inner_shape, 0) + lead,
+        lax.broadcasted_iota(jnp.int32, inner_shape, 1) + lead,
+        lax.broadcasted_iota(jnp.int32, inner_shape, 2),
     )
     sizes = (BX, BX, BY, BY, BZ, BZ)
     code = across_x(brick_code)
@@ -248,7 +249,8 @@
         lo = repeat + 1
         hi_x = span_x - repeat - 1
         hi_y = span_y - repeat - 1
-        lvl = region_step(lvl, edge[lo:hi_x, lo:hi_y], rate[lo:hi_x, lo:hi_y], code[lo:hi_x, lo:hi_y])
+        cut = (slice(lo - 1, hi_x - 1), slice(lo - 1, hi_y - 1))
+        lvl = region_step(lvl, edge[cut], rate[cut], code[cut])
     band_here = brick_of_band.shape[0]
     lower = jnp.concatenate([neighbours[1:, 4], neighbours[:1, 4]])
     upper = jnp.concatenate([neighbours[-1:, 5], neighbours[:-1, 5]])

time: 245 us -> 247 us (level)
    add x4, other arithmetic: 31 us -> 41.3 us  [region_step(): return centre + time_step * edge * force * jnp.sqrt(1.0 + gradient)]
    div x1 -> x0, other arithmetic: 6.09 us -> none  [edge_map(): 1.0 / (1.0 + (grad_x * grad_x + grad_y * grad_y + grad_z * grad_z) / cont...]
  transfers between devices with their start and end apart: 9 -> 9, of which waited for: 1 -> 2; matrix products, arithmetic and copies ran while one was open for 14% -> 11% of each run, Pallas kernels for 0% -> 0%
where the time goes in v3:
time: 247 us; the launch traced here: 246 us
  waiting for transfers between devices  96 us (39%)
  other arithmetic  70.2 us (28%)
  local copies, waits for them, and re-layouts  42.3 us (17%)
  starting transfers between devices  36.4 us (15%)
    all_to_all x1, waiting for transfers between devices, per_device(): lax.all_to_all(sending, 'dev', split_axis=0, concat_axis=0, tiled=True)  95.6 us
    add x4, other arithmetic, region_step(): return centre + time_step * edge * force * jnp.sqrt(1.0 + gradient)  41.3 us
    all_to_all x1, starting transfers between devices, per_device(): lax.all_to_all(sending, 'dev', split_axis=0, concat_axis=0, tiled=True)  12.9 us
    ppermute x4, starting transfers between devices, sent(): flat = lax.ppermute(flat, axis, pairs)  12.4 us
    ppermute x4, starting transfers between devices, sent(): image_part = lax.ppermute(pieces[0], axis, pairs)  11.1 us
    add x3, other arithmetic, smooth_axis(): summed + gauss_taps[offset] * lax.slice_in_dim(values, offset, offset + l...  10.4 us
    slice x4, local copies, waits for them, and re-layouts, region_step(): centre[:, :, 1:]  8.12 us
  transfers between devices with their start and end apart: 9, of which 2 were waited for; matrix products, arithmetic and copies ran while one was open for 11% of the time, Pallas kernels for 0%

profile of v3, /device:TPU:1, one launch (start us, length us, event | category | flops | bytes accessed | tf_op | source)
XLA Modules:
  0.0 245.6 jit_solution(15665189602767775825)
XLA Ops:
  0.0 0.9 copy.24
  0.9 0.8 select_reduce_fusion.2
  1.9 1.1 fusion.70
  3.1 4.5 %collective-permute-start = (f32[65592]{0:T(1024)S(1)}, f32[65592]{0:T(1024)S(1)}, u32[]{:S(2)}, u32[]{:S(2)}) collective-permute-start(f32[65592]{0:T(1024)S(1)} %pad_maximum_fusion.3), channel_id=1, source_target_pairs={{0,32},{32,64},{64,96},{96,128},{128,160},{160,192},{192,224},{1,3... | collective-permute-start | bytes 787112 | tf_op jit(solution)/shard_map/ppermute | solution.py:169
  7.7 1.9 collective-permute-start.1
  9.7 3.6 %collective-permute-start.4 = (bf16[6,32,512]{2,1,0:T(8,128)(2,1)S(1)}, bf16[6,32,512]{2,1,0:T(8,128)(2,1)S(1)}, u32[]{:S(2)}, u32[]{:S(2)}) collective-permute-start(bf16[6,32,512]{2,1,0:T(8,128)(2,1)S(1)} %get-tuple-element.36), channel_id=1, source_target_pairs={{0,32},{32,64},{64,96},{96,128},{128,160},{160,192},{192,224},{1,3... | collective-permute-start | bytes 589832 | tf_op jit(solution)/shard_map/ppermute | solution.py:167
  13.4 1.9 collective-permute-start.5
  15.4 0.6 compare_and_fusion
  16.0 0.6 fusion.59
  16.6 0.6 compare_select_fusion.8
  17.1 0.5 fusion.44
  17.7 0.6 fusion.74
  18.3 1.3 broadcast_compare_fusion
  20.0 0.4 collective-permute-done.5
  20.4 1.1 copy-done.1
  21.5 0.8 fusion.71
  22.4 4.3 %collective-permute-start.6 = (bf16[44,6,512]{2,1,0:T(8,128)(2,1)}, bf16[44,6,512]{2,1,0:T(8,128)(2,1)}, u32[]{:S(2)}, u32[]{:S(2)}) collective-permute-start(bf16[44,6,512]{2,1,0:T(8,128)(2,1)} %get-tuple-element.33), channel_id=1, source_target_pairs={{0,1},{1,2},{2,3},{3,4},{4,5},{5,6},{6,7},{7,8},{8,9},{9,10},{10,1... | collective-permute-start | bytes 811016 | tf_op jit(solution)/shard_map/ppermute | solution.py:167
  26.6 1.3 collective-permute-start.7
  28.2 0.7 reshape.344
  29.0 1.8 constant_dynamic-update-slice_fusion.1
  31.0 0.1 slice_bitcast_fusion.1
  31.2 1.4 pad_maximum_fusion.1
  32.7 4.7 %collective-permute-start.2 = (f32[82032]{0:T(1024)}, f32[82032]{0:T(1024)}, u32[]{:S(2)}, u32[]{:S(2)}) collective-permute-start(f32[82032]{0:T(1024)} %pad_maximum_fusion.1), channel_id=1, source_target_pairs={{0,1},{1,2},{2,3},{3,4},{4,5},{5,6},{6,7},{7,8},{8,9},{9,10},{10,1... | collective-permute-start | bytes 984392 | tf_op jit(solution)/shard_map/ppermute | solution.py:169
  37.6 1.3 collective-permute-start.3
  38.9 3.7 %fusion.35 = f32[44,44,518]{2,1,0:T(8,128)S(1)} fusion(bf16[44,6,512]{2,1,0:T(8,128)(2,1)} %collective-permute-done.7, bf16[44,32,512]{2,1,0:T(8,128)(2,1)} %copy-done.1, bf16[44,6,512]{2,1,0:T(8,128)(2,1)} %collective-permute-done.6), kind=kLoop, calls=%fused_computation.107 | loop fusion | flops 12034176 | bytes 5993856 | tf_op jit(solution)/shard_map/jit(_pad)/pad | solution.py:216
  42.6 2.4 fusion.1
  45.0 2.3 fusion.9
  47.3 5.7 %fusion.5 = f32[40,40,514]{2,1,0:T(8,128)} fusion(f32[40,40,518]{2,1,0:T(8,128)S(1)} %fusion.9), kind=kLoop, calls=%fused_computation.21 | loop fusion | flops 7401600 | bytes 19737600 | tf_op jit(solution)/shard_map/add | solution.py:49
  53.0 1.0 slice.437
  54.0 0.8 reshape.345
  54.9 1.0 slice.440
  55.9 0.8 reshape.348
  56.7 2.3 pad_maximum_fusion
  59.1 4.1 %fusion.62 = (f32[38,38,511]{2,1,0:T(8,128)}, f32[38,38,511]{2,1,0:T(8,128)}) fusion(f32[40,40,512]{2,1,0:T(8,128)S(1)} %pad_maximum_fusion), kind=kLoop, calls=%fused_computation.224 | loop fusion | bytes 11806144 | tf_op jit(solution)/shard_map/slice | solution.py:193
  63.1 1.4 fusion.63
  64.6 0.7 slice.465
  65.3 0.7 slice.466
  66.1 0.4 select_reduce_fusion
  66.5 0.2 slice_reduce_fusion
  66.7 0.9 broadcast_in_dim.159
  67.7 2.1 reshape.352
  69.7 1.7 slice_bitcast_fusion.5
  71.4 0.9 broadcast_in_dim.149
  72.4 2.0 reshape.351
  74.4 1.1 slice_bitcast_fusion.9
  75.5 20.6 %multiply_add_fusion = (f32[38,38,512]{2,1,0:T(8,128)S(1)}, f32[38,38,512]{2,1,0:T(8,128)S(1)}) fusion(f32[38,38,511]{2,1,0:T(8,128)} %get-tuple-element.14, f32[38,38,1]{2,1,0:T(8,128)} %get-tuple-element.16, f32[38,38,1]{2,1,0:T(8,128)} %get-tuple-element.15, f32[38,38,511]{2,1,0:T(8,128)} %get-tuple-element.13, f32[40,40,512]{2,1,0:T(8,128)S(1)} %pad_maximum_fusion, ...), kind=kLoop, calls=%fused_computation.62 | loop fusion | flops 72454144 | bytes 48604160 | tf_op jit(solution)/shard_map/add | solution.py:204
  96.1 1.5 fusion.64
  97.6 0.3 fusion.65
  98.0 3.8 %shift-left_or_fusion = s32[38,38,512]{2,1,0:T(8,128)S(1)} fusion(s32[512]{0:T(512)S(1)} %get-tuple-element.55, s32[512]{0:T(512)S(1)} %get-tuple-element.56, s32[38]{0:T(128)S(1)} %copy-done.7, s32[38]{0:T(128)S(1)} %copy-done.8, s32[38,512]{1,0:T(8,128)S(1)} %get-tuple-element.38, s32[38,512]{1,0:T(8,128)S(1)} %get-tuple-element.39, ...), kind=kLoop, calls=%fused_computation.70 | loop fusion | flops 22179840 | bytes 3273672 | tf_op jit(solution)/shard_map/or | solution.py:246
  101.8 0.9 select_select_fusion
  102.7 7.5 %fusion.29 = f32[36,36,512]{2,1,0:T(8,128)S(1)} fusion(f32[38,38,512]{2,1,0:T(8,128)S(1)} %select_select_fusion, f32[38,38,512]{2,1,0:T(8,128)S(1)} %get-tuple-element.10, f32[36,36,511]{2,1,0:T(8,128)S(1)} %get-tuple-element.18, f32[36,36,1]{2,1,0:T(8,128)S(1)} %get-tuple-element.20, f32[36,36,1]{2,1,0:T(8,128)S(1)} %get-tuple-element.19, ...), kind=kLoop, calls=%fused_computation.74 | loop fusion | flops 33841152 | bytes 29196288 | tf_op jit(solution)/shard_map/add | solution.py:204
  110.2 1.4 fusion.66
  111.6 0.3 fusion.67
  111.9 7.9 %fusion.32 = f32[34,34,512]{2,1,0:T(8,128)S(1)} fusion(f32[38,38,512]{2,1,0:T(8,128)S(1)} %select_select_fusion, f32[38,38,512]{2,1,0:T(8,128)S(1)} %get-tuple-element.10, f32[34,34,511]{2,1,0:T(8,128)S(1)} %get-tuple-element.22, f32[34,34,1]{2,1,0:T(8,128)S(1)} %get-tuple-element.24, f32[34,34,1]{2,1,0:T(8,128)S(1)} %get-tuple-element.23, ...), kind=kLoop, calls=%fused_computation.91 | loop fusion | flops 30185472 | bytes 26042368 | tf_op jit(solution)/shard_map/add | solution.py:204
  119.8 1.1 fusion.68
  120.9 0.3 fusion.69
  121.2 5.4 %fusion.38 = f32[32,32,512]{2,1,0:T(8,128)S(1)} fusion(f32[38,38,512]{2,1,0:T(8,128)S(1)} %select_select_fusion, f32[38,38,512]{2,1,0:T(8,128)S(1)} %get-tuple-element.10, f32[32,32,511]{2,1,0:T(8,128)S(1)} %get-tuple-element.26, f32[32,32,1]{2,1,0:T(8,128)S(1)} %get-tuple-element.28, f32[32,32,1]{2,1,0:T(8,128)S(1)} %get-tuple-element.27, ...), kind=kLoop, calls=%fused_computation.111 | loop fusion | flops 26738688 | bytes 23068672 | tf_op jit(solution)/shard_map/add | solution.py:204
  126.6 1.7 reshape.353
  128.4 1.8 copy.29
  130.2 2.9 %gather_fusion = f32[32,16,16,128]{3,2,1,0:T(8,128)} fusion(f32[2,16,2,16,4,128]{5,3,4,2,1,0:T(8,128)S(1)} %copy.29, s32[32]{0:T(128)S(1)} %fusion.57), kind=kCustom, calls=%fused_computation | custom fusion | bytes 8388992 | tf_op jit(solution)/shard_map/gather | solution.py:265
  133.1 12.9 %all-to-all-start = ((f32[32,16,16,128]{3,2,1,0:T(8,128)}), f32[32,16,16,128]{3,2,1,0:T(8,128)}, u32[]{:S(2)}, u32[]{:S(2)}) async-start(f32[32,16,16,128]{3,2,1,0:T(8,128)} %gather_fusion), calls=%async_computation | async-start | bytes 8388608 | tf_op jit(solution)/shard_map/all_to_all | solution.py:266
  146.0 95.6 %all-to-all-done = f32[32,16,16,128]{3,2,1,0:T(8,128)} async-done(((f32[32,16,16,128]{3,2,1,0:T(8,128)}), f32[32,16,16,128]{3,2,1,0:T(8,128)}, u32[]{:S(2)}, u32[]{:S(2)}) %all-to-all-start) | async-done | bytes 4194336 | tf_op jit(solution)/shard_map/all_to_all | solution.py:266
  241.6 2.8 %gather_fusion.1 = f32[8,16,16,128]{3,2,1,0:T(8,128)S(1)} fusion(f32[32,16,16,128]{3,2,1,0:T(8,128)} %all-to-all-done, s32[1024]{0:T(1024)S(1)} %pad_clamp_fusion), kind=kCustom, calls=%fused_computation.1 | custom fusion | bytes 2097184 | tf_op jit(solution)/shard_map/jit(_take)/gather | solution.py:267
  244.4 1.1 broadcast_select_fusion
  (75 shorter events, 2.0 us)
Async XLA Ops:
  0.0 17.7 %copy-start.6 = (s32[16,6]{0,1:T(8,128)S(1)}, s32[16,6]{0,1:T(8,128)}, u32[]{:S(2)}) copy-start(s32[16,6]{0,1:T(8,128)} %param.11) | copy-start | bytes 1156
  0.0 9.7 %copy-start.2 = (bf16[32,32,512]{2,1,0:T(8,128)(2,1)S(1)}, bf16[32,32,512]{2,1,0:T(8,128)(2,1)}, u32[]{:S(2)}) copy-start(bf16[32,32,512]{2,1,0:T(8,128)(2,1)} %param.7) | copy-start | bytes 3145732
  3.1 24.9 %collective-permute-start = (f32[65592]{0:T(1024)S(1)}, f32[65592]{0:T(1024)S(1)}, u32[]{:S(2)}, u32[]{:S(2)}) collective-permute-start(f32[65592]{0:T(1024)S(1)} %pad_maximum_fusion.3), channel_id=1, source_target_pairs={{0,32},{32,64},{64,96},{96,128},{128,160},{160,192},{192,224},{1,3... | collective-permute-start | bytes 787112 | tf_op jit(solution)/shard_map/ppermute | solution.py:169
  7.7 20.3 %collective-permute-start.1 = (f32[65592]{0:T(1024)S(1)}, f32[65592]{0:T(1024)S(1)}, u32[]{:S(2)}, u32[]{:S(2)}) collective-permute-start(f32[65592]{0:T(1024)S(1)} %pad_maximum_fusion.4), channel_id=1, source_target_pairs={{32,0},{64,32},{96,64},{128,96},{160,128},{192,160},{224,192},{33,... | collective-permute-start | bytes 787112 | tf_op jit(solution)/shard_map/ppermute | solution.py:169
  9.7 10.1 %collective-permute-start.4 = (bf16[6,32,512]{2,1,0:T(8,128)(2,1)S(1)}, bf16[6,32,512]{2,1,0:T(8,128)(2,1)S(1)}, u32[]{:S(2)}, u32[]{:S(2)}) collective-permute-start(bf16[6,32,512]{2,1,0:T(8,128)(2,1)S(1)} %get-tuple-element.36), channel_id=1, source_target_pairs={{0,32},{32,64},{64,96},{96,128},{128,160},{160,192},{192,224},{1,3... | collective-permute-start | bytes 589832 | tf_op jit(solution)/shard_map/ppermute | solution.py:167
  13.4 7.0 %collective-permute-start.5 = (bf16[6,32,512]{2,1,0:T(8,128)(2,1)S(1)}, bf16[6,32,512]{2,1,0:T(8,128)(2,1)S(1)}, u32[]{:S(2)}, u32[]{:S(2)}) collective-permute-start(bf16[6,32,512]{2,1,0:T(8,128)(2,1)S(1)} %get-tuple-element.35), channel_id=1, source_target_pairs={{32,0},{64,32},{96,64},{128,96},{160,128},{192,160},{224,192},{33,... | collective-permute-start | bytes 589832 | tf_op jit(solution)/shard_map/ppermute | solution.py:167
  20.4 1.2 copy-start.1
  22.4 16.6 %collective-permute-start.6 = (bf16[44,6,512]{2,1,0:T(8,128)(2,1)}, bf16[44,6,512]{2,1,0:T(8,128)(2,1)}, u32[]{:S(2)}, u32[]{:S(2)}) collective-permute-start(bf16[44,6,512]{2,1,0:T(8,128)(2,1)} %get-tuple-element.33), channel_id=1, source_target_pairs={{0,1},{1,2},{2,3},{3,4},{4,5},{5,6},{6,7},{7,8},{8,9},{9,10},{10,1... | collective-permute-start | bytes 811016 | tf_op jit(solution)/shard_map/ppermute | solution.py:167
  26.6 12.3 %collective-permute-start.7 = (bf16[44,6,512]{2,1,0:T(8,128)(2,1)S(1)}, bf16[44,6,512]{2,1,0:T(8,128)(2,1)}, u32[]{:S(2)}, u32[]{:S(2)}) collective-permute-start(bf16[44,6,512]{2,1,0:T(8,128)(2,1)S(1)} %get-tuple-element.34), channel_id=1, source_target_pairs={{1,0},{2,1},{3,2},{4,3},{5,4},{6,5},{7,6},{8,7},{9,8},{10,9},{11,1... | collective-permute-start | bytes 811016 | tf_op jit(solution)/shard_map/ppermute | solution.py:167
  28.0 0.9 copy-start.4
  29.0 1.9 copy-start.5
  31.0 11.6 %copy-start = (f32[40,32,512]{2,1,0:T(8,128)}, f32[40,32,512]{2,1,0:T(8,128)S(1)}, u32[]{:S(2)}) copy-start(f32[40,32,512]{2,1,0:T(8,128)S(1)} %constant_dynamic-update-slice_fusion) | copy-start | bytes 7864324
  32.7 20.4 %collective-permute-start.2 = (f32[82032]{0:T(1024)}, f32[82032]{0:T(1024)}, u32[]{:S(2)}, u32[]{:S(2)}) collective-permute-start(f32[82032]{0:T(1024)} %pad_maximum_fusion.1), channel_id=1, source_target_pairs={{0,1},{1,2},{2,3},{3,4},{4,5},{5,6},{6,7},{7,8},{8,9},{9,10},{10,1... | collective-permute-start | bytes 984392 | tf_op jit(solution)/shard_map/ppermute | solution.py:169
  37.6 17.3 %collective-permute-start.3 = (f32[82032]{0:T(1024)S(1)}, f32[82032]{0:T(1024)}, u32[]{:S(2)}, u32[]{:S(2)}) collective-permute-start(f32[82032]{0:T(1024)S(1)} %pad_maximum_fusion.2), channel_id=1, source_target_pairs={{1,0},{2,1},{3,2},{4,3},{5,4},{6,5},{7,6},{8,7},{9,8},{10,9},{11,1... | collective-permute-start | bytes 984392 | tf_op jit(solution)/shard_map/ppermute | solution.py:169
  63.1 3.0 %copy-start.13 = (s32[7]{0:T(128)S(1)}, s32[7]{0:T(128)}, u32[]{:S(2)}) copy-start(s32[7]{0:T(128)} %constant.232.clone) | copy-start | bytes 88
  96.0 1.9 copy-start.7
  96.1 1.9 copy-start.8
  96.1 1.9 copy-start.9
  96.1 1.9 copy-start.10
  96.1 1.9 copy-start.11
  96.1 1.9 copy-start.12
  97.6 4.2 %copy-start.3 = (f32[38,512]{1,0:T(8,128)S(1)}, f32[38,512]{1,0:T(8,128)}, u32[]{:S(2)}) copy-start(f32[38,512]{1,0:T(8,128)} %get-tuple-element.44) | copy-start | bytes 233476
  133.1 12.9 %copy-start.14 = (s32[8]{0:T(128)S(1)}, s32[8]{0:T(128)}, u32[]{:S(2)}) copy-start(s32[8]{0:T(128)} %param.10) | copy-start | bytes 100
  133.1 108.6 %all-to-all-start = ((f32[32,16,16,128]{3,2,1,0:T(8,128)}), f32[32,16,16,128]{3,2,1,0:T(8,128)}, u32[]{:S(2)}, u32[]{:S(2)}) async-start(f32[32,16,16,128]{3,2,1,0:T(8,128)} %gather_fusion), calls=%async_computation | async-start | bytes 8388608 | tf_op jit(solution)/shard_map/all_to_all | solution.py:266

commit v4 on v1

--- a/solution.py
+++ b/solution.py
@@ -164,15 +164,14 @@
                 pieces.append(lax.slice_in_dim(c, start, start + w, axis=dim))
             parts.append(pieces)
         def sent(pieces, pairs):
-            image_part = lax.ppermute(pieces[0], axis, pairs)
-            flat = jnp.concatenate([pieces[1].reshape(-1), pieces[2].reshape(-1)])
+            flat = jnp.concatenate([p.astype(jnp.float32).reshape(-1) for p in pieces])
             flat = lax.ppermute(flat, axis, pairs)
-            size = pieces[1].size
-            return [
-                image_part,
-                flat[:size].reshape(pieces[1].shape),
-                flat[size:].reshape(pieces[2].shape),
-            ]
+            out = []
+            start = 0
+            for p in pieces:
+                out.append(flat[start : start + p.size].reshape(p.shape).astype(p.dtype))
+                start += p.size
+            return out
         from_below = sent(parts[1], [(i, i + 1) for i in range(ends)])
         from_above = sent(parts[0], [(i + 1, i) for i in range(ends)])
         cells = [

time: 245 us -> 275 us (1.12)
  waiting for transfers between devices: 94.2 us -> 114 us
  local copies, waits for them, and re-layouts: 42.2 us -> 60.7 us
  starting transfers between devices: 35.8 us -> 23.6 us
    ppermute x4, waiting for transfers between devices: 0.01 us -> 19.1 us  [sent(): flat = lax.ppermute(flat, axis, pairs)]
    ppermute x4 -> x0, starting transfers between devices: 10.4 us -> none  [sent(): image_part = lax.ppermute(pieces[0], axis, pairs)]
    slice x8 -> x14, local copies, waits for them, and re-layouts: 3.4 us -> 10.2 us  [sent(): out.append(flat[start:start + p.size].reshape(p.shape).astype(p.dtype))]
    convert_element_type x0 -> x4, local copies, waits for them, and re-layouts: none -> 5.81 us  [sent(): out.append(flat[start:start + p.size].reshape(p.shape).astype(p.dtype))]
    unnamed x50 -> x48, local copies, waits for them, and re-layouts: 4.86 us -> 8.26 us
  transfers between devices with their start and end apart: 9 -> 5, of which waited for: 1 -> 4; matrix products, arithmetic and copies ran while one was open for 14% -> 3% of each run, Pallas kernels for 0% -> 0%
where the time goes in v4:
time: 275 us; the launch traced here: 271 us
  waiting for transfers between devices  114 us (41%)
  other arithmetic  71.8 us (26%)
  local copies, waits for them, and re-layouts  60.7 us (22%)
  starting transfers between devices  23.6 us (9%)
    all_to_all x1, waiting for transfers between devices, per_device(): lax.all_to_all(sending, 'dev', split_axis=0, concat_axis=0, tiled=True)  95.4 us
    add x4, other arithmetic, region_step(): return centre + time_step * edge * force * jnp.sqrt(1.0 + gradient)  31.1 us
    ppermute x4, waiting for transfers between devices, sent(): flat = lax.ppermute(flat, axis, pairs)  19.1 us
    ppermute x4, starting transfers between devices, sent(): flat = lax.ppermute(flat, axis, pairs)  12.4 us
    all_to_all x1, starting transfers between devices, per_device(): lax.all_to_all(sending, 'dev', split_axis=0, concat_axis=0, tiled=True)  11.2 us
    add x3, other arithmetic, smooth_axis(): summed + gauss_taps[offset] * lax.slice_in_dim(values, offset, offset + l...  11 us
    slice x14, local copies, waits for them, and re-layouts, sent(): out.append(flat[start:start + p.size].reshape(p.shape).astype(p.dtype))  10.2 us
    unnamed x48, local copies, waits for them, and re-layouts  8.26 us
  transfers between devices with their start and end apart: 5, of which 4 were waited for; matrix products, arithmetic and copies ran while one was open for 3% of the time, Pallas kernels for 0%

profile of v4, /device:TPU:1, one launch (start us, length us, event | category | flops | bytes accessed | tf_op | source)
XLA Modules:
  0.0 271.3 jit_solution(10507296086455768765)
XLA Ops:
  0.0 0.8 copy.24
  0.8 0.8 select_reduce_fusion.2
  1.8 1.1 fusion.72
  2.9 1.1 slice_convert_fusion.7
  4.2 5.1 %collective-permute-start.1 = (f32[180280]{0:T(1024)S(1)}, f32[180280]{0:T(1024)S(1)}, u32[]{:S(2)}, u32[]{:S(2)}) collective-permute-start(f32[180280]{0:T(1024)S(1)} %pad_maximum_fusion.4), channel_id=1, source_target_pairs={{32,0},{64,32},{96,64},{128,96},{160,128},{192,160},{224,192},{33,... | collective-permute-start | bytes 2163368 | tf_op jit(solution)/shard_map/ppermute | solution.py:168
  9.7 1.9 collective-permute-start
  14.0 1.4 fusion.74
  15.4 2.3 collective-permute-done.1
  17.8 2.0 collective-permute-done
  21.3 0.7 reshape.387
  22.0 1.0 slice.466
  23.1 1.8 constant_dynamic-update-slice_fusion.4
  25.3 1.4 slice.780
  26.7 0.8 convert_element_type.45
  27.5 1.6 constant_dynamic-update-slice_fusion.2
  29.2 2.3 constant_dynamic-update-slice_fusion.1
  31.5 1.7 slice.779
  33.2 1.1 convert_element_type.46
  34.3 0.7 constant_dynamic-update-slice_fusion
  35.0 1.3 slice_convert_fusion.5
  36.4 1.0 pad_maximum_fusion.2
  37.4 1.3 collective-permute-start.3
  39.1 4.1 %collective-permute-start.2 = (f32[246896]{0:T(1024)S(1)}, f32[246896]{0:T(1024)S(1)}, u32[]{:S(2)}, u32[]{:S(2)}) collective-permute-start(f32[246896]{0:T(1024)S(1)} %pad_maximum_fusion.1), channel_id=1, source_target_pairs={{0,1},{1,2},{2,3},{3,4},{4,5},{5,6},{6,7},{7,8},{8,9},{9,10},{10,1... | collective-permute-start | bytes 2962760 | tf_op jit(solution)/shard_map/ppermute | solution.py:168
  43.1 0.8 slice_bitcast_fusion.11
  44.0 1.3 broadcast_compare_fusion
  46.0 14.8 %collective-permute-done.3 = f32[246896]{0:T(1024)} collective-permute-done((f32[246896]{0:T(1024)}, f32[246896]{0:T(1024)}, u32[]{:S(2)}, u32[]{:S(2)}) %collective-permute-start.3) | collective-permute-done | bytes 987616 | tf_op jit(solution)/shard_map/ppermute | solution.py:168
  60.8 1.0 slice.476
  61.8 0.8 reshape.388
  62.6 0.9 copy-done.5
  63.6 0.8 reshape.383
  64.4 2.3 pad_maximum_fusion
  66.7 4.0 %fusion.64 = (f32[38,38,511]{2,1,0:T(8,128)}, f32[38,38,511]{2,1,0:T(8,128)}) fusion(f32[40,40,512]{2,1,0:T(8,128)S(1)} %pad_maximum_fusion), kind=kLoop, calls=%fused_computation.236 | loop fusion | bytes 11806144 | tf_op jit(solution)/shard_map/slice | solution.py:192
  70.8 1.5 fusion.65
  73.7 1.0 broadcast_in_dim.159
  74.7 2.0 reshape.392
  76.7 1.7 slice_bitcast_fusion.5
  78.4 1.8 slice.777
  80.3 1.9 convert_element_type.48
  82.2 1.8 slice.778
  84.1 1.9 convert_element_type.47
  86.0 3.8 %fusion.35 = f32[46,46,518]{2,1,0:T(8,128)S(1)} fusion(bf16[46,7,512]{2,1,0:T(8,128)(2,1)} %convert_element_type.48, bf16[46,32,512]{2,1,0:T(8,128)(2,1)} %constant_dynamic-update-slice_fusion, bf16[46,7,512]{2,1,0:T(8,128)(2,1)} %convert_element_type.47), kind=kLoop, calls=%fused_computation.94 | loop fusion | flops 13153056 | bytes 6551136 | tf_op jit(solution)/shard_map/jit(_pad)/pad | solution.py:215
  89.9 2.6 fusion.9
  92.5 2.9 %fusion.5 = f32[42,42,518]{2,1,0:T(8,128)S(1)} fusion(f32[42,46,518]{2,1,0:T(8,128)S(1)} %fusion.9), kind=kLoop, calls=%fused_computation.15 | loop fusion | flops 8223768 | bytes 21930048 | tf_op jit(solution)/shard_map/add | solution.py:49
  95.4 5.5 %fusion.1 = f32[42,42,514]{2,1,0:T(8,128)S(1)} fusion(f32[42,42,518]{2,1,0:T(8,128)S(1)} %fusion.5), kind=kLoop, calls=%fused_computation.6 | loop fusion | flops 8160264 | bytes 21760704 | tf_op jit(solution)/shard_map/add | solution.py:49
  100.9 6.1 %fusion.18 = f32[40,40,512]{2,1,0:T(8,128)} fusion(f32[42,42,514]{2,1,0:T(8,128)S(1)} %fusion.1), kind=kLoop, calls=%fused_computation.44 | loop fusion | flops 11468800 | bytes 22937600 | tf_op jit(solution)/shard_map/div | solution.py:60
  107.0 0.9 broadcast_in_dim.149
  107.9 2.1 reshape.391
  110.0 1.1 slice_bitcast_fusion.9
  111.1 1.9 select_select_fusion
  113.0 5.2 %shift-left_or_fusion = s32[40,40,512]{2,1,0:T(8,128)S(1)} fusion(s32[512]{0:T(512)S(1)} %get-tuple-element.55, s32[512]{0:T(512)S(1)} %copy-done.11, s32[40]{0:T(128)} %get-tuple-element.53, s32[40]{0:T(128)} %get-tuple-element.54, s32[40,512]{1,0:T(8,128)S(1)} %get-tuple-element.36, s32[40,512]{1,0:T(8,128)S(1)} %get-tuple-element.37, ...), kind=kLoop, calls=%fused_computation.54 | loop fusion | flops 24576000 | bytes 3609568 | tf_op jit(solution)/shard_map/or | solution.py:244
  118.3 10.0 %fusion.29 = f32[38,38,512]{2,1,0:T(8,128)S(1)} fusion(f32[40,40,512]{2,1,0:T(8,128)S(1)} %select_select_fusion, f32[40,40,512]{2,1,0:T(8,128)S(1)} %copy-done, f32[38,38,511]{2,1,0:T(8,128)} %get-tuple-element.12, f32[38,38,1]{2,1,0:T(8,128)S(1)} %copy-done.3, f32[38,38,1]{2,1,0:T(8,128)S(1)} %copy-done.2, f32[38,38,511]{2,1,0:T(8,128)} %get-tuple-element.11, ...), kind=kLoop, calls=%fused_computation.61 | loop fusion | flops 37705728 | bytes 32530432 | tf_op jit(solution)/shard_map/add | solution.py:203
  128.3 1.5 fusion.66
  130.2 7.6 %fusion.32 = f32[36,36,512]{2,1,0:T(8,128)S(1)} fusion(f32[40,40,512]{2,1,0:T(8,128)S(1)} %select_select_fusion, f32[40,40,512]{2,1,0:T(8,128)S(1)} %copy-done, f32[36,36,511]{2,1,0:T(8,128)S(1)} %get-tuple-element.16, f32[36,36,1]{2,1,0:T(8,128)S(1)} %get-tuple-element.18, f32[36,36,1]{2,1,0:T(8,128)S(1)} %get-tuple-element.17, ...), kind=kLoop, calls=%fused_computation.78 | loop fusion | flops 33841152 | bytes 29196288 | tf_op jit(solution)/shard_map/add | solution.py:203
  137.8 1.4 fusion.68
  139.5 8.0 %fusion.38 = f32[34,34,512]{2,1,0:T(8,128)S(1)} fusion(f32[40,40,512]{2,1,0:T(8,128)S(1)} %select_select_fusion, f32[40,40,512]{2,1,0:T(8,128)S(1)} %copy-done, f32[34,34,511]{2,1,0:T(8,128)S(1)} %get-tuple-element.20, f32[34,34,1]{2,1,0:T(8,128)S(1)} %get-tuple-element.22, f32[34,34,1]{2,1,0:T(8,128)S(1)} %get-tuple-element.21, ...), kind=kLoop, calls=%fused_computation.98 | loop fusion | flops 30185472 | bytes 26042368 | tf_op jit(solution)/shard_map/add | solution.py:203
  147.5 1.0 fusion.70
  148.8 5.4 %fusion.41 = f32[32,32,512]{2,1,0:T(8,128)S(1)} fusion(f32[40,40,512]{2,1,0:T(8,128)S(1)} %select_select_fusion, f32[40,40,512]{2,1,0:T(8,128)S(1)} %copy-done, f32[32,32,511]{2,1,0:T(8,128)S(1)} %get-tuple-element.24, f32[32,32,1]{2,1,0:T(8,128)S(1)} %get-tuple-element.26, f32[32,32,1]{2,1,0:T(8,128)S(1)} %get-tuple-element.25, ...), kind=kLoop, calls=%fused_computation.115 | loop fusion | flops 26738688 | bytes 23068672 | tf_op jit(solution)/shard_map/add | solution.py:203
  154.2 1.7 reshape.393
  155.9 1.8 copy.29
  157.7 2.9 %gather_fusion = f32[32,16,16,128]{3,2,1,0:T(8,128)} fusion(f32[2,16,2,16,4,128]{5,3,4,2,1,0:T(8,128)S(1)} %copy.29, s32[32]{0:T(128)S(1)} %fusion.60), kind=kCustom, calls=%fused_computation | custom fusion | bytes 8388992 | tf_op jit(solution)/shard_map/gather | solution.py:262
  160.7 11.2 %all-to-all-start = ((f32[32,16,16,128]{3,2,1,0:T(8,128)}), f32[32,16,16,128]{3,2,1,0:T(8,128)}, u32[]{:S(2)}, u32[]{:S(2)}) async-start(f32[32,16,16,128]{3,2,1,0:T(8,128)} %gather_fusion), calls=%async_computation | async-start | bytes 8388608 | tf_op jit(solution)/shard_map/all_to_all | solution.py:263
  172.0 95.4 %all-to-all-done = f32[32,16,16,128]{3,2,1,0:T(8,128)} async-done(((f32[32,16,16,128]{3,2,1,0:T(8,128)}), f32[32,16,16,128]{3,2,1,0:T(8,128)}, u32[]{:S(2)}, u32[]{:S(2)}) %all-to-all-start) | async-done | bytes 4194336 | tf_op jit(solution)/shard_map/all_to_all | solution.py:263
  267.3 2.8 %gather_fusion.1 = f32[8,16,16,128]{3,2,1,0:T(8,128)S(1)} fusion(f32[32,16,16,128]{3,2,1,0:T(8,128)} %all-to-all-done, s32[1024]{0:T(1024)S(1)} %pad_clamp_fusion), kind=kCustom, calls=%fused_computation.1 | custom fusion | bytes 2097184 | tf_op jit(solution)/shard_map/jit(_take)/gather | solution.py:264
  270.1 1.1 broadcast_select_fusion
  (88 shorter events, 8.6 us)
Async XLA Ops:
  4.2 13.5 %collective-permute-start.1 = (f32[180280]{0:T(1024)S(1)}, f32[180280]{0:T(1024)S(1)}, u32[]{:S(2)}, u32[]{:S(2)}) collective-permute-start(f32[180280]{0:T(1024)S(1)} %pad_maximum_fusion.4), channel_id=1, source_target_pairs={{32,0},{64,32},{96,64},{128,96},{160,128},{192,160},{224,192},{33,... | collective-permute-start | bytes 2163368 | tf_op jit(solution)/shard_map/ppermute | solution.py:168
  9.7 10.2 %collective-permute-start = (f32[180280]{0:T(1024)S(1)}, f32[180280]{0:T(1024)}, u32[]{:S(2)}, u32[]{:S(2)}) collective-permute-start(f32[180280]{0:T(1024)S(1)} %pad_maximum_fusion.3), channel_id=1, source_target_pairs={{0,32},{32,64},{64,96},{96,128},{128,160},{160,192},{192,224},{1,3... | collective-permute-start | bytes 2163368 | tf_op jit(solution)/shard_map/ppermute | solution.py:168
  17.7 5.3 %copy-start.4 = (f32[180280]{0:T(1024)}, f32[180280]{0:T(1024)S(1)}, u32[]{:S(2)}) copy-start(f32[180280]{0:T(1024)S(1)} %collective-permute-done.1) | copy-start | bytes 2163364
  17.8 3.5 %copy-start.6 = (f32[1,2,4,7]{3,2,1,0:T(4,128)}, f32[1,2,4,7]{3,2,1,0:T(4,128)S(1)}, u32[]{:S(2)}) copy-start(f32[1,2,4,7]{3,2,1,0:T(4,128)S(1)} %reshape.381) | copy-start | bytes 676
  20.7 0.7 copy-start.8
  23.1 1.9 slice-start
  25.0 8.2 %copy-start.1 = (f32[40,32,512]{2,1,0:T(8,128)}, f32[40,32,512]{2,1,0:T(8,128)S(1)}, u32[]{:S(2)}) copy-start(f32[40,32,512]{2,1,0:T(8,128)S(1)} %constant_dynamic-update-slice_fusion.3) | copy-start | bytes 7864324
  31.5 4.9 %copy-start.15 = (f32[112]{0:T(128)S(1)}, f32[112]{0:T(128)}, u32[]{:S(2)}) copy-start(f32[112]{0:T(128)} %reshape.387) | copy-start | bytes 1348
  34.3 4.4 %copy-start.10 = (f32[4,1,4,7]{3,2,1,0:T(4,128)S(1)}, f32[4,1,4,7]{3,2,1,0:T(4,128)}, u32[]{:S(2)}) copy-start(f32[4,1,4,7]{3,2,1,0:T(4,128)} %get-tuple-element.43) | copy-start | bytes 1348
  37.4 23.4 %collective-permute-start.3 = (f32[246896]{0:T(1024)}, f32[246896]{0:T(1024)}, u32[]{:S(2)}, u32[]{:S(2)}) collective-permute-start(f32[246896]{0:T(1024)} %pad_maximum_fusion.2), channel_id=1, source_target_pairs={{1,0},{2,1},{3,2},{4,3},{5,4},{6,5},{7,6},{8,7},{9,8},{10,9},{11,1... | collective-permute-start | bytes 2962760 | tf_op jit(solution)/shard_map/ppermute | solution.py:168
  39.1 23.5 %collective-permute-start.2 = (f32[246896]{0:T(1024)S(1)}, f32[246896]{0:T(1024)S(1)}, u32[]{:S(2)}, u32[]{:S(2)}) collective-permute-start(f32[246896]{0:T(1024)S(1)} %pad_maximum_fusion.1), channel_id=1, source_target_pairs={{0,1},{1,2},{2,3},{3,4},{4,5},{5,6},{6,7},{7,8},{8,9},{9,10},{10,1... | collective-permute-start | bytes 2962760 | tf_op jit(solution)/shard_map/ppermute | solution.py:168
  62.6 0.9 copy-start.5
  70.8 2.3 slice-start.1
  70.8 2.4 copy-start.7
  70.8 2.4 copy-start.9
  70.8 2.4 copy-start.16
  100.9 10.2 %copy-start.12 = (pred[40]{0:T(512)(128)(4,1)S(1)}, pred[40]{0:T(512)(128)(4,1)}, u32[]{:S(2)}) copy-start(pred[40]{0:T(512)(128)(4,1)} %get-tuple-element.51) | copy-start | bytes 124
  100.9 10.2 %copy-start.13 = (pred[40]{0:T(512)(128)(4,1)S(1)}, pred[40]{0:T(512)(128)(4,1)}, u32[]{:S(2)}) copy-start(pred[40]{0:T(512)(128)(4,1)} %get-tuple-element.52) | copy-start | bytes 124
  100.9 10.2 %copy-start.14 = (pred[40]{0:T(512)(128)(4,1)S(1)}, pred[40]{0:T(512)(128)(4,1)}, u32[]{:S(2)}) copy-start(pred[40]{0:T(512)(128)(4,1)} %get-tuple-element.58) | copy-start | bytes 124
  107.0 6.1 %copy-start.11 = (s32[512]{0:T(512)S(1)}, s32[512]{0:T(512)}, u32[]{:S(2)}) copy-start(s32[512]{0:T(512)} %get-tuple-element.56) | copy-start | bytes 6148
  111.1 7.2 %copy-start = (f32[40,40,512]{2,1,0:T(8,128)S(1)}, f32[40,40,512]{2,1,0:T(8,128)}, u32[]{:S(2)}) copy-start(f32[40,40,512]{2,1,0:T(8,128)} %fusion.18) | copy-start | bytes 9830404
  111.1 7.2 %copy-start.2 = (f32[38,38,1]{2,1,0:T(8,128)S(1)}, f32[38,38,1]{2,1,0:T(8,128)}, u32[]{:S(2)}) copy-start(f32[38,38,1]{2,1,0:T(8,128)} %get-tuple-element.13) | copy-start | bytes 17332
  111.1 7.2 %copy-start.3 = (f32[38,38,1]{2,1,0:T(8,128)S(1)}, f32[38,38,1]{2,1,0:T(8,128)}, u32[]{:S(2)}) copy-start(f32[38,38,1]{2,1,0:T(8,128)} %get-tuple-element.14) | copy-start | bytes 17332
  160.7 11.2 %copy-start.17 = (s32[8]{0:T(128)S(1)}, s32[8]{0:T(128)}, u32[]{:S(2)}) copy-start(s32[8]{0:T(128)} %param.10) | copy-start | bytes 100
  160.7 106.6 %all-to-all-start = ((f32[32,16,16,128]{3,2,1,0:T(8,128)}), f32[32,16,16,128]{3,2,1,0:T(8,128)}, u32[]{:S(2)}, u32[]{:S(2)}) async-start(f32[32,16,16,128]{3,2,1,0:T(8,128)} %gather_fusion), calls=%async_computation | async-start | bytes 8388608 | tf_op jit(solution)/shard_map/all_to_all | solution.py:263

commit v5 on v1

--- a/solution.py
+++ b/solution.py
@@ -260,9 +260,11 @@
     matches = (owner_dev[None, :] == jnp.arange(partners)[:, None]) & in_band[None, :]
     chosen = jnp.sum(jnp.where(matches, jnp.arange(bricks_here)[None, :], 0), axis=1)
     view = lvl.reshape(BXN, BX, BYN, BY, BZN, BZ)
-    sending = view[chosen // (BYN * BZN), :, chosen // BZN % BYN, :, chosen % BZN, :]
+    sending = view.at[chosen // (BYN * BZN), :, chosen // BZN % BYN, :, chosen % BZN, :].get(
+        mode="promise_in_bounds"
+    )
     arrived = lax.all_to_all(sending, "dev", split_axis=0, concat_axis=0, tiled=True)
-    return jnp.take(arrived, source_dev, axis=0)
+    return arrived.at[source_dev].get(mode="promise_in_bounds")
 
 
 def solution(mesh):

time: 245 us -> 245 us (level)
  no operation moved by 1% of the time
where the time goes in v5:
time: 245 us; the launch traced here: 242 us
  waiting for transfers between devices  94.2 us (38%)
  other arithmetic  68.2 us (28%)
  local copies, waits for them, and re-layouts  43.2 us (18%)
  starting transfers between devices  35.8 us (15%)
    all_to_all x1, waiting for transfers between devices, per_device(): lax.all_to_all(sending, 'dev', split_axis=0, concat_axis=0, tiled=True)  94.2 us
    add x4, other arithmetic, region_step(): return centre + time_step * edge * force * jnp.sqrt(1.0 + gradient)  31 us
    ppermute x4, starting transfers between devices, sent(): flat = lax.ppermute(flat, axis, pairs)  13 us
    all_to_all x1, starting transfers between devices, per_device(): lax.all_to_all(sending, 'dev', split_axis=0, concat_axis=0, tiled=True)  12.4 us
    add x3, other arithmetic, smooth_axis(): summed + gauss_taps[offset] * lax.slice_in_dim(values, offset, offset + l...  11 us
    ppermute x4, starting transfers between devices, sent(): image_part = lax.ppermute(pieces[0], axis, pairs)  10.3 us
    slice x4, local copies, waits for them, and re-layouts, region_step(): centre[:, :, 1:]  8 us
    div x1, other arithmetic, edge_map(): 1.0 / (1.0 + (grad_x * grad_x + grad_y * grad_y + grad_z * grad_z) / cont...  6.1 us
  transfers between devices with their start and end apart: 9, of which 1 were waited for; matrix products, arithmetic and copies ran while one was open for 14% of the time, Pallas kernels for 0%

profile of v5, /device:TPU:1, one launch (start us, length us, event | category | flops | bytes accessed | tf_op | source)
XLA Modules:
  0.0 241.9 jit_solution(11240471688630576338)
XLA Ops:
  0.0 0.9 copy.24
  0.9 0.8 select_reduce_fusion.2
  1.9 1.1 fusion.72
  3.1 5.1 %collective-permute-start.1 = (f32[65592]{0:T(1024)S(1)}, f32[65592]{0:T(1024)S(1)}, u32[]{:S(2)}, u32[]{:S(2)}) collective-permute-start(f32[65592]{0:T(1024)S(1)} %pad_maximum_fusion.4), channel_id=1, source_target_pairs={{32,0},{64,32},{96,64},{128,96},{160,128},{192,160},{224,192},{33,... | collective-permute-start | bytes 787112 | tf_op jit(solution)/shard_map/ppermute | solution.py:169
  8.4 1.9 collective-permute-start
  10.3 1.9 collective-permute-start.4
  12.3 2.4 collective-permute-start.5
  14.7 0.6 fusion.61
  15.3 0.6 compare_and_fusion
  15.9 0.6 iota_and_fusion
  16.5 0.6 compare_select_fusion.10
  17.1 0.6 fusion.76
  17.7 1.3 broadcast_compare_fusion
  19.1 0.6 fusion.47
  20.0 1.2 copy-done.2
  21.2 1.0 fusion.73
  22.2 1.3 collective-permute-start.7
  23.5 4.7 %collective-permute-start.6 = (bf16[46,7,512]{2,1,0:T(8,128)(2,1)}, bf16[46,7,512]{2,1,0:T(8,128)(2,1)}, u32[]{:S(2)}, u32[]{:S(2)}) collective-permute-start(bf16[46,7,512]{2,1,0:T(8,128)(2,1)} %get-tuple-element.29), channel_id=1, source_target_pairs={{0,1},{1,2},{2,3},{3,4},{4,5},{5,6},{6,7},{7,8},{8,9},{9,10},{10,1... | collective-permute-start | bytes 989192 | tf_op jit(solution)/shard_map/ppermute | solution.py:167
  28.6 0.3 copy-done.8
  29.1 1.8 constant_dynamic-update-slice_fusion.1
  31.0 0.1 slice_bitcast_fusion.1
  31.2 1.0 pad_maximum_fusion.2
  32.2 1.3 collective-permute-start.3
  33.7 4.7 %collective-permute-start.2 = (f32[82032]{0:T(1024)S(1)}, f32[82032]{0:T(1024)}, u32[]{:S(2)}, u32[]{:S(2)}) collective-permute-start(f32[82032]{0:T(1024)S(1)} %pad_maximum_fusion.1), channel_id=1, source_target_pairs={{0,1},{1,2},{2,3},{3,4},{4,5},{5,6},{6,7},{7,8},{8,9},{9,10},{10,1... | collective-permute-start | bytes 984392 | tf_op jit(solution)/shard_map/ppermute | solution.py:169
  38.5 3.8 %fusion.35 = f32[46,46,518]{2,1,0:T(8,128)S(1)} fusion(bf16[46,7,512]{2,1,0:T(8,128)(2,1)} %collective-permute-done.7, bf16[46,32,512]{2,1,0:T(8,128)(2,1)} %copy-done.2, bf16[46,7,512]{2,1,0:T(8,128)(2,1)} %collective-permute-done.6), kind=kLoop, calls=%fused_computation.94 | loop fusion | flops 13153056 | bytes 6551136 | tf_op jit(solution)/shard_map/jit(_pad)/pad | solution.py:216
  42.3 2.6 %fusion.9 = f32[42,46,518]{2,1,0:T(8,128)S(1)} fusion(f32[46,46,518]{2,1,0:T(8,128)S(1)} %fusion.35), kind=kLoop, calls=%fused_computation.24 | loop fusion | flops 9006984 | bytes 24018624 | tf_op jit(solution)/shard_map/add | solution.py:49
  44.9 2.9 %fusion.5 = f32[42,42,518]{2,1,0:T(8,128)S(1)} fusion(f32[42,46,518]{2,1,0:T(8,128)S(1)} %fusion.9), kind=kLoop, calls=%fused_computation.15 | loop fusion | flops 8223768 | bytes 21930048 | tf_op jit(solution)/shard_map/add | solution.py:49
  47.8 5.5 %fusion.1 = f32[42,42,514]{2,1,0:T(8,128)S(1)} fusion(f32[42,42,518]{2,1,0:T(8,128)S(1)} %fusion.5), kind=kLoop, calls=%fused_computation.6 | loop fusion | flops 8160264 | bytes 21760704 | tf_op jit(solution)/shard_map/add | solution.py:49
  53.3 6.1 %fusion.18 = f32[40,40,512]{2,1,0:T(8,128)} fusion(f32[42,42,514]{2,1,0:T(8,128)S(1)} %fusion.1), kind=kLoop, calls=%fused_computation.44 | loop fusion | flops 11468800 | bytes 22937600 | tf_op jit(solution)/shard_map/div | solution.py:60
  59.4 1.0 slice.452
  60.4 0.8 reshape.343
  61.2 1.0 slice.449
  62.2 0.9 reshape.340
  63.1 2.3 pad_maximum_fusion
  65.4 4.1 %fusion.64 = (f32[38,38,511]{2,1,0:T(8,128)}, f32[38,38,511]{2,1,0:T(8,128)}) fusion(f32[40,40,512]{2,1,0:T(8,128)S(1)} %pad_maximum_fusion), kind=kLoop, calls=%fused_computation.226 | loop fusion | bytes 11806144 | tf_op jit(solution)/shard_map/slice | solution.py:193
  69.5 1.4 fusion.65
  70.9 0.7 slice.479
  71.7 0.7 slice.478
  72.5 0.4 select_reduce_fusion
  72.9 0.2 slice_reduce_fusion
  73.1 0.9 broadcast_in_dim.149
  74.0 2.1 reshape.347
  76.1 1.7 slice_bitcast_fusion.5
  77.8 1.0 broadcast_in_dim.139
  78.8 2.0 reshape.346
  80.8 1.1 slice_bitcast_fusion.9
  81.9 1.9 select_select_fusion
  83.9 5.2 %shift-left_or_fusion = s32[40,40,512]{2,1,0:T(8,128)S(1)} fusion(s32[512]{0:T(512)S(1)} %copy-done.13, s32[512]{0:T(512)S(1)} %copy-done.14, s32[40]{0:T(128)} %get-tuple-element.51, s32[40]{0:T(128)} %get-tuple-element.52, s32[40,512]{1,0:T(8,128)S(1)} %get-tuple-element.34, s32[40,512]{1,0:T(8,128)S(1)} %get-tuple-element.35, ...), kind=kLoop, calls=%fused_computation.54 | loop fusion | flops 24576000 | bytes 3609568 | tf_op jit(solution)/shard_map/or | solution.py:245
  89.1 10.3 %fusion.29 = f32[38,38,512]{2,1,0:T(8,128)S(1)} fusion(f32[40,40,512]{2,1,0:T(8,128)S(1)} %select_select_fusion, f32[40,40,512]{2,1,0:T(8,128)S(1)} %copy-done, f32[38,38,511]{2,1,0:T(8,128)} %get-tuple-element.10, f32[38,38,1]{2,1,0:T(8,128)S(1)} %copy-done.4, f32[38,38,1]{2,1,0:T(8,128)S(1)} %copy-done.3, f32[38,38,511]{2,1,0:T(8,128)} %get-tuple-element.9, ...), kind=kLoop, calls=%fused_computation.61 | loop fusion | flops 37705728 | bytes 32530432 | tf_op jit(solution)/shard_map/add | solution.py:204
  99.4 1.5 fusion.66
  100.9 0.3 fusion.67
  101.3 7.4 %fusion.32 = f32[36,36,512]{2,1,0:T(8,128)S(1)} fusion(f32[40,40,512]{2,1,0:T(8,128)S(1)} %select_select_fusion, f32[40,40,512]{2,1,0:T(8,128)S(1)} %copy-done, f32[36,36,511]{2,1,0:T(8,128)S(1)} %get-tuple-element.14, f32[36,36,1]{2,1,0:T(8,128)S(1)} %get-tuple-element.16, f32[36,36,1]{2,1,0:T(8,128)S(1)} %get-tuple-element.15, ...), kind=kLoop, calls=%fused_computation.78 | loop fusion | flops 33841152 | bytes 29196288 | tf_op jit(solution)/shard_map/add | solution.py:204
  108.6 1.4 fusion.68
  110.1 0.3 fusion.69
  110.4 8.0 %fusion.38 = f32[34,34,512]{2,1,0:T(8,128)S(1)} fusion(f32[40,40,512]{2,1,0:T(8,128)S(1)} %select_select_fusion, f32[40,40,512]{2,1,0:T(8,128)S(1)} %copy-done, f32[34,34,511]{2,1,0:T(8,128)S(1)} %get-tuple-element.18, f32[34,34,1]{2,1,0:T(8,128)S(1)} %get-tuple-element.20, f32[34,34,1]{2,1,0:T(8,128)S(1)} %get-tuple-element.19, ...), kind=kLoop, calls=%fused_computation.98 | loop fusion | flops 30185472 | bytes 26042368 | tf_op jit(solution)/shard_map/add | solution.py:204
  118.3 1.0 fusion.70
  119.3 0.3 fusion.71
  119.6 5.4 %fusion.41 = f32[32,32,512]{2,1,0:T(8,128)S(1)} fusion(f32[40,40,512]{2,1,0:T(8,128)S(1)} %select_select_fusion, f32[40,40,512]{2,1,0:T(8,128)S(1)} %copy-done, f32[32,32,511]{2,1,0:T(8,128)S(1)} %get-tuple-element.22, f32[32,32,1]{2,1,0:T(8,128)S(1)} %get-tuple-element.24, f32[32,32,1]{2,1,0:T(8,128)S(1)} %get-tuple-element.23, ...), kind=kLoop, calls=%fused_computation.115 | loop fusion | flops 26738688 | bytes 23068672 | tf_op jit(solution)/shard_map/add | solution.py:204
  125.1 1.7 reshape.348
  126.8 1.8 copy.29
  128.6 2.9 %gather_fusion = f32[32,16,16,128]{3,2,1,0:T(8,128)} fusion(f32[2,16,2,16,4,128]{5,3,4,2,1,0:T(8,128)S(1)} %copy.29, s32[32]{0:T(128)S(1)} %fusion.60), kind=kCustom, calls=%fused_computation | custom fusion | bytes 8388992 | tf_op jit(solution)/shard_map/gather | solution.py:263
  131.5 12.4 %all-to-all-start = ((f32[32,16,16,128]{3,2,1,0:T(8,128)}), f32[32,16,16,128]{3,2,1,0:T(8,128)}, u32[]{:S(2)}, u32[]{:S(2)}) async-start(f32[32,16,16,128]{3,2,1,0:T(8,128)} %gather_fusion), calls=%async_computation | async-start | bytes 8388608 | tf_op jit(solution)/shard_map/all_to_all | solution.py:266
  143.9 94.2 %all-to-all-done = f32[32,16,16,128]{3,2,1,0:T(8,128)} async-done(((f32[32,16,16,128]{3,2,1,0:T(8,128)}), f32[32,16,16,128]{3,2,1,0:T(8,128)}, u32[]{:S(2)}, u32[]{:S(2)}) %all-to-all-start) | async-done | bytes 4194336 | tf_op jit(solution)/shard_map/all_to_all | solution.py:266
  238.1 3.8 %gather_fusion.1 = f32[8,16,16,128]{3,2,1,0:T(8,128)} fusion(f32[32,16,16,128]{3,2,1,0:T(8,128)} %all-to-all-done, s32[1024]{0:T(1024)S(1)} %pad_clamp_fusion), kind=kCustom, calls=%fused_computation.1 | custom fusion | bytes 2097184 | tf_op jit(solution)/shard_map/gather | solution.py:267
  (85 shorter events, 2.2 us)
Async XLA Ops:
  0.0 17.1 %copy-start.12 = (s32[16,6]{0,1:T(8,128)S(1)}, s32[16,6]{0,1:T(8,128)}, u32[]{:S(2)}) copy-start(s32[16,6]{0,1:T(8,128)} %param.11) | copy-start | bytes 1156
  0.0 10.3 %copy-start.5 = (bf16[32,32,512]{2,1,0:T(8,128)(2,1)S(1)}, bf16[32,32,512]{2,1,0:T(8,128)(2,1)}, u32[]{:S(2)}) copy-start(bf16[32,32,512]{2,1,0:T(8,128)(2,1)} %param.7) | copy-start | bytes 3145732
  3.1 25.1 %collective-permute-start.1 = (f32[65592]{0:T(1024)S(1)}, f32[65592]{0:T(1024)S(1)}, u32[]{:S(2)}, u32[]{:S(2)}) collective-permute-start(f32[65592]{0:T(1024)S(1)} %pad_maximum_fusion.4), channel_id=1, source_target_pairs={{32,0},{64,32},{96,64},{128,96},{160,128},{192,160},{224,192},{33,... | collective-permute-start | bytes 787112 | tf_op jit(solution)/shard_map/ppermute | solution.py:169
  8.4 19.9 %collective-permute-start = (f32[65592]{0:T(1024)S(1)}, f32[65592]{0:T(1024)S(1)}, u32[]{:S(2)}, u32[]{:S(2)}) collective-permute-start(f32[65592]{0:T(1024)S(1)} %pad_maximum_fusion.3), channel_id=1, source_target_pairs={{0,32},{32,64},{64,96},{96,128},{128,160},{160,192},{192,224},{1,3... | collective-permute-start | bytes 787112 | tf_op jit(solution)/shard_map/ppermute | solution.py:169
  10.3 9.5 %collective-permute-start.4 = (bf16[7,32,512]{2,1,0:T(8,128)(2,1)S(1)}, bf16[7,32,512]{2,1,0:T(8,128)(2,1)S(1)}, u32[]{:S(2)}, u32[]{:S(2)}) collective-permute-start(bf16[7,32,512]{2,1,0:T(8,128)(2,1)S(1)} %get-tuple-element.32), channel_id=1, source_target_pairs={{0,32},{32,64},{64,96},{96,128},{128,160},{160,192},{192,224},{1,3... | collective-permute-start | bytes 688136 | tf_op jit(solution)/shard_map/ppermute | solution.py:167
  12.3 7.7 %collective-permute-start.5 = (bf16[7,32,512]{2,1,0:T(8,128)(2,1)S(1)}, bf16[7,32,512]{2,1,0:T(8,128)(2,1)S(1)}, u32[]{:S(2)}, u32[]{:S(2)}) collective-permute-start(bf16[7,32,512]{2,1,0:T(8,128)(2,1)S(1)} %get-tuple-element.31), channel_id=1, source_target_pairs={{32,0},{64,32},{96,64},{128,96},{160,128},{192,160},{224,192},{33,... | collective-permute-start | bytes 688136 | tf_op jit(solution)/shard_map/ppermute | solution.py:167
  19.8 8.8 %copy-start.6 = (f32[2,2,4,1]{3,2,1,0:T(4,128)}, f32[2,2,4,1]{3,2,1,0:T(4,128)S(1)}, u32[]{:S(2)}) copy-start(f32[2,2,4,1]{3,2,1,0:T(4,128)S(1)} %concatenate.126) | copy-start | bytes 196
  20.0 1.2 copy-start.2
  22.2 16.3 %collective-permute-start.7 = (bf16[46,7,512]{2,1,0:T(8,128)(2,1)}, bf16[46,7,512]{2,1,0:T(8,128)(2,1)}, u32[]{:S(2)}, u32[]{:S(2)}) collective-permute-start(bf16[46,7,512]{2,1,0:T(8,128)(2,1)} %get-tuple-element.30), channel_id=1, source_target_pairs={{1,0},{2,1},{3,2},{4,3},{5,4},{6,5},{7,6},{8,7},{9,8},{10,9},{11,1... | collective-permute-start | bytes 989192 | tf_op jit(solution)/shard_map/ppermute | solution.py:167
  23.5 15.0 %collective-permute-start.6 = (bf16[46,7,512]{2,1,0:T(8,128)(2,1)}, bf16[46,7,512]{2,1,0:T(8,128)(2,1)}, u32[]{:S(2)}, u32[]{:S(2)}) collective-permute-start(bf16[46,7,512]{2,1,0:T(8,128)(2,1)} %get-tuple-element.29), channel_id=1, source_target_pairs={{0,1},{1,2},{2,3},{3,4},{4,5},{5,6},{6,7},{7,8},{8,9},{9,10},{10,1... | collective-permute-start | bytes 989192 | tf_op jit(solution)/shard_map/ppermute | solution.py:167
  28.3 0.6 copy-start.8
  28.4 0.6 copy-start.10
  31.0 11.3 %copy-start.1 = (f32[40,32,512]{2,1,0:T(8,128)}, f32[40,32,512]{2,1,0:T(8,128)S(1)}, u32[]{:S(2)}) copy-start(f32[40,32,512]{2,1,0:T(8,128)S(1)} %constant_dynamic-update-slice_fusion) | copy-start | bytes 7864324
  32.2 27.2 %collective-permute-start.3 = (f32[82032]{0:T(1024)}, f32[82032]{0:T(1024)}, u32[]{:S(2)}, u32[]{:S(2)}) collective-permute-start(f32[82032]{0:T(1024)} %pad_maximum_fusion.2), channel_id=1, source_target_pairs={{1,0},{2,1},{3,2},{4,3},{5,4},{6,5},{7,6},{8,7},{9,8},{10,9},{11,1... | collective-permute-start | bytes 984392 | tf_op jit(solution)/shard_map/ppermute | solution.py:169
  33.7 27.5 %collective-permute-start.2 = (f32[82032]{0:T(1024)S(1)}, f32[82032]{0:T(1024)}, u32[]{:S(2)}, u32[]{:S(2)}) collective-permute-start(f32[82032]{0:T(1024)S(1)} %pad_maximum_fusion.1), channel_id=1, source_target_pairs={{0,1},{1,2},{2,3},{3,4},{4,5},{5,6},{6,7},{7,8},{8,9},{9,10},{10,1... | collective-permute-start | bytes 984392 | tf_op jit(solution)/shard_map/ppermute | solution.py:169
  69.5 3.0 %copy-start.7 = (f32[2,2,4,1]{3,2,1,0:T(4,128)S(1)}, f32[2,2,4,1]{3,2,1,0:T(4,128)}, u32[]{:S(2)}) copy-start(f32[2,2,4,1]{3,2,1,0:T(4,128)} %copy-done.6) | copy-start | bytes 196
  69.5 3.0 %copy-start.9 = (f32[1,2,4,7]{3,2,1,0:T(4,128)S(1)}, f32[1,2,4,7]{3,2,1,0:T(4,128)}, u32[]{:S(2)}) copy-start(f32[1,2,4,7]{3,2,1,0:T(4,128)} %copy-done.8) | copy-start | bytes 676
  69.5 3.0 %copy-start.11 = (f32[1,2,4,7]{3,2,1,0:T(4,128)S(1)}, f32[1,2,4,7]{3,2,1,0:T(4,128)}, u32[]{:S(2)}) copy-start(f32[1,2,4,7]{3,2,1,0:T(4,128)} %copy-done.10) | copy-start | bytes 676
  69.5 3.0 %copy-start.18 = (s32[7]{0:T(128)S(1)}, s32[7]{0:T(128)}, u32[]{:S(2)}) copy-start(s32[7]{0:T(128)} %constant.229.clone) | copy-start | bytes 88
  70.9 11.0 %copy-start.15 = (pred[40]{0:T(512)(128)(4,1)S(1)}, pred[40]{0:T(512)(128)(4,1)}, u32[]{:S(2)}) copy-start(pred[40]{0:T(512)(128)(4,1)} %get-tuple-element.49) | copy-start | bytes 124
  77.8 6.1 %copy-start.13 = (s32[512]{0:T(512)S(1)}, s32[512]{0:T(512)}, u32[]{:S(2)}) copy-start(s32[512]{0:T(512)} %get-tuple-element.53) | copy-start | bytes 6148
  77.8 6.1 %copy-start.14 = (s32[512]{0:T(512)S(1)}, s32[512]{0:T(512)}, u32[]{:S(2)}) copy-start(s32[512]{0:T(512)} %get-tuple-element.54) | copy-start | bytes 6148
  77.8 6.1 %copy-start.16 = (pred[40]{0:T(512)(128)(4,1)S(1)}, pred[40]{0:T(512)(128)(4,1)}, u32[]{:S(2)}) copy-start(pred[40]{0:T(512)(128)(4,1)} %get-tuple-element.50) | copy-start | bytes 124
  77.8 6.1 %copy-start.17 = (pred[40]{0:T(512)(128)(4,1)S(1)}, pred[40]{0:T(512)(128)(4,1)}, u32[]{:S(2)}) copy-start(pred[40]{0:T(512)(128)(4,1)} %get-tuple-element.56) | copy-start | bytes 124
  81.9 7.2 %copy-start = (f32[40,40,512]{2,1,0:T(8,128)S(1)}, f32[40,40,512]{2,1,0:T(8,128)}, u32[]{:S(2)}) copy-start(f32[40,40,512]{2,1,0:T(8,128)} %fusion.18) | copy-start | bytes 9830404
  81.9 7.2 %copy-start.3 = (f32[38,38,1]{2,1,0:T(8,128)S(1)}, f32[38,38,1]{2,1,0:T(8,128)}, u32[]{:S(2)}) copy-start(f32[38,38,1]{2,1,0:T(8,128)} %get-tuple-element.11) | copy-start | bytes 17332
  81.9 7.2 %copy-start.4 = (f32[38,38,1]{2,1,0:T(8,128)S(1)}, f32[38,38,1]{2,1,0:T(8,128)}, u32[]{:S(2)}) copy-start(f32[38,38,1]{2,1,0:T(8,128)} %get-tuple-element.12) | copy-start | bytes 17332
  131.5 12.4 %copy-start.19 = (s32[8]{0:T(128)S(1)}, s32[8]{0:T(128)}, u32[]{:S(2)}) copy-start(s32[8]{0:T(128)} %param.10) | copy-start | bytes 100
  131.5 106.6 %all-to-all-start = ((f32[32,16,16,128]{3,2,1,0:T(8,128)}), f32[32,16,16,128]{3,2,1,0:T(8,128)}, u32[]{:S(2)}, u32[]{:S(2)}) async-start(f32[32,16,16,128]{3,2,1,0:T(8,128)} %gather_fusion), calls=%async_computation | async-start | bytes 8388608 | tf_op jit(solution)/shard_map/all_to_all | solution.py:266

commit v6 on v5

--- a/solution.py
+++ b/solution.py
@@ -243,6 +243,7 @@
         pos = place[side // 2] % sizes[side]
         inner = pos != (0 if side % 2 == 0 else sizes[side] - 1)
         code = code | (inner.astype(jnp.int32) << side)
+    code = code.astype(jnp.int8)
     lvl = wide_level
     for repeat in range(STEPS):
         lo = repeat + 1

time: 245 us -> 249 us (1.016)
  other arithmetic: 68.2 us -> 72.3 us
    or x1 -> x0, other arithmetic: 5.18 us -> none  [per_device(): code = code | inner.astype(jnp.int32) << side]
    add x4, other arithmetic: 31 us -> 36 us  [region_step(): return centre + time_step * edge * force * jnp.sqrt(1.0 + gradient)]
    convert_element_type x0 -> x1, other arithmetic: none -> 4.1 us  [per_device(): code = code.astype(jnp.int8)]
  transfers between devices with their start and end apart: 9 -> 9, of which waited for: 1 -> 1; matrix products, arithmetic and copies ran while one was open for 14% -> 13% of each run, Pallas kernels for 0% -> 0%
where the time goes in v6:
time: 249 us; the launch traced here: 246 us
  waiting for transfers between devices  94.2 us (38%)
  other arithmetic  72.3 us (29%)
  local copies, waits for them, and re-layouts  43.3 us (17%)
  starting transfers between devices  35.8 us (14%)
    all_to_all x1, waiting for transfers between devices, per_device(): lax.all_to_all(sending, 'dev', split_axis=0, concat_axis=0, tiled=True)  94.2 us
    add x4, other arithmetic, region_step(): return centre + time_step * edge * force * jnp.sqrt(1.0 + gradient)  36 us
    ppermute x4, starting transfers between devices, sent(): flat = lax.ppermute(flat, axis, pairs)  13 us
    all_to_all x1, starting transfers between devices, per_device(): lax.all_to_all(sending, 'dev', split_axis=0, concat_axis=0, tiled=True)  12.4 us
    add x3, other arithmetic, smooth_axis(): summed + gauss_taps[offset] * lax.slice_in_dim(values, offset, offset + l...  11 us
    ppermute x4, starting transfers between devices, sent(): image_part = lax.ppermute(pieces[0], axis, pairs)  10.4 us
    slice x4, local copies, waits for them, and re-layouts, region_step(): centre[:, :, 1:]  7.96 us
    div x1, other arithmetic, edge_map(): 1.0 / (1.0 + (grad_x * grad_x + grad_y * grad_y + grad_z * grad_z) / cont...  6.1 us
  transfers between devices with their start and end apart: 9, of which 1 were waited for; matrix products, arithmetic and copies ran while one was open for 13% of the time, Pallas kernels for 0%

profile of v6, /device:TPU:1, one launch (start us, length us, event | category | flops | bytes accessed | tf_op | source)
XLA Modules:
  0.0 246.1 jit_solution(17279955272992925626)
XLA Ops:
  0.0 0.9 copy.24
  0.9 0.8 select_reduce_fusion.2
  1.9 1.1 fusion.72
  3.1 5.1 %collective-permute-start.1 = (f32[65592]{0:T(1024)S(1)}, f32[65592]{0:T(1024)S(1)}, u32[]{:S(2)}, u32[]{:S(2)}) collective-permute-start(f32[65592]{0:T(1024)S(1)} %pad_maximum_fusion.4), channel_id=1, source_target_pairs={{32,0},{64,32},{96,64},{128,96},{160,128},{192,160},{224,192},{33,... | collective-permute-start | bytes 787112 | tf_op jit(solution)/shard_map/ppermute | solution.py:169
  8.4 1.9 collective-permute-start
  10.3 1.9 collective-permute-start.4
  12.3 2.4 collective-permute-start.5
  14.7 0.6 fusion.61
  15.3 0.6 compare_and_fusion
  15.9 0.6 iota_and_fusion
  16.5 0.6 compare_select_fusion.10
  17.1 0.6 fusion.76
  17.7 1.3 broadcast_compare_fusion
  19.1 0.6 fusion.47
  20.0 1.2 copy-done.2
  21.2 1.0 fusion.73
  22.2 1.3 collective-permute-start.7
  23.5 4.7 %collective-permute-start.6 = (bf16[46,7,512]{2,1,0:T(8,128)(2,1)}, bf16[46,7,512]{2,1,0:T(8,128)(2,1)}, u32[]{:S(2)}, u32[]{:S(2)}) collective-permute-start(bf16[46,7,512]{2,1,0:T(8,128)(2,1)} %get-tuple-element.29), channel_id=1, source_target_pairs={{0,1},{1,2},{2,3},{3,4},{4,5},{5,6},{6,7},{7,8},{8,9},{9,10},{10,1... | collective-permute-start | bytes 989192 | tf_op jit(solution)/shard_map/ppermute | solution.py:167
  28.6 0.3 copy-done.8
  29.1 1.8 constant_dynamic-update-slice_fusion.1
  31.0 0.1 slice_bitcast_fusion.1
  31.2 1.0 pad_maximum_fusion.2
  32.2 1.3 collective-permute-start.3
  33.7 4.7 %collective-permute-start.2 = (f32[82032]{0:T(1024)S(1)}, f32[82032]{0:T(1024)}, u32[]{:S(2)}, u32[]{:S(2)}) collective-permute-start(f32[82032]{0:T(1024)S(1)} %pad_maximum_fusion.1), channel_id=1, source_target_pairs={{0,1},{1,2},{2,3},{3,4},{4,5},{5,6},{6,7},{7,8},{8,9},{9,10},{10,1... | collective-permute-start | bytes 984392 | tf_op jit(solution)/shard_map/ppermute | solution.py:169
  38.5 3.8 %fusion.35 = f32[46,46,518]{2,1,0:T(8,128)S(1)} fusion(bf16[46,7,512]{2,1,0:T(8,128)(2,1)} %collective-permute-done.7, bf16[46,32,512]{2,1,0:T(8,128)(2,1)} %copy-done.2, bf16[46,7,512]{2,1,0:T(8,128)(2,1)} %collective-permute-done.6), kind=kLoop, calls=%fused_computation.82 | loop fusion | flops 13153056 | bytes 6551136 | tf_op jit(solution)/shard_map/jit(_pad)/pad | solution.py:216
  42.3 2.6 %fusion.9 = f32[42,46,518]{2,1,0:T(8,128)S(1)} fusion(f32[46,46,518]{2,1,0:T(8,128)S(1)} %fusion.35), kind=kLoop, calls=%fused_computation.24 | loop fusion | flops 9006984 | bytes 24018624 | tf_op jit(solution)/shard_map/add | solution.py:49
  44.9 2.9 %fusion.5 = f32[42,42,518]{2,1,0:T(8,128)S(1)} fusion(f32[42,46,518]{2,1,0:T(8,128)S(1)} %fusion.9), kind=kLoop, calls=%fused_computation.15 | loop fusion | flops 8223768 | bytes 21930048 | tf_op jit(solution)/shard_map/add | solution.py:49
  47.8 5.5 %fusion.1 = f32[42,42,514]{2,1,0:T(8,128)S(1)} fusion(f32[42,42,518]{2,1,0:T(8,128)S(1)} %fusion.5), kind=kLoop, calls=%fused_computation.6 | loop fusion | flops 8160264 | bytes 21760704 | tf_op jit(solution)/shard_map/add | solution.py:49
  53.3 6.1 %fusion.18 = f32[40,40,512]{2,1,0:T(8,128)} fusion(f32[42,42,514]{2,1,0:T(8,128)S(1)} %fusion.1), kind=kLoop, calls=%fused_computation.44 | loop fusion | flops 11468800 | bytes 22937600 | tf_op jit(solution)/shard_map/div | solution.py:60
  59.4 1.0 slice.452
  60.4 0.8 reshape.343
  61.2 1.0 slice.449
  62.2 0.9 reshape.340
  63.1 2.3 pad_maximum_fusion
  65.4 4.1 %fusion.64 = (f32[38,38,511]{2,1,0:T(8,128)}, f32[38,38,511]{2,1,0:T(8,128)}) fusion(f32[40,40,512]{2,1,0:T(8,128)S(1)} %pad_maximum_fusion), kind=kLoop, calls=%fused_computation.202 | loop fusion | bytes 11806144 | tf_op jit(solution)/shard_map/slice | solution.py:193
  69.5 1.4 fusion.65
  70.9 0.7 slice.479
  71.7 0.7 slice.478
  72.5 0.4 select_reduce_fusion
  72.9 0.2 slice_reduce_fusion
  73.1 0.9 broadcast_in_dim.149
  74.0 2.1 reshape.347
  76.1 1.7 slice_bitcast_fusion.5
  77.8 1.0 broadcast_in_dim.139
  78.8 2.0 reshape.346
  80.8 1.2 slice_bitcast_fusion.9
  82.1 2.2 select_select_fusion
  84.3 4.1 %or_convert_fusion = s8[40,40,512]{2,1,0:T(8,128)(4,1)S(1)} fusion(s32[512]{0:T(512)S(1)} %copy-done.13, s32[512]{0:T(512)S(1)} %copy-done.14, s32[40]{0:T(128)} %get-tuple-element.51, s32[40]{0:T(128)} %get-tuple-element.52, s32[40,512]{1,0:T(8,128)S(1)} %get-tuple-element.34, s32[40,512]{1,0:T(8,128)S(1)} %get-tuple-element.35, ...), kind=kLoop, calls=%fused_computation.54 | loop fusion | flops 25395200 | bytes 1151968 | tf_op jit(solution)/shard_map/convert_element_type | solution.py:246
  88.4 11.6 %fusion.29 = f32[38,38,512]{2,1,0:T(8,128)S(1)} fusion(f32[40,40,512]{2,1,0:T(8,128)S(1)} %select_select_fusion, f32[40,40,512]{2,1,0:T(8,128)S(1)} %copy-done, f32[38,38,511]{2,1,0:T(8,128)} %get-tuple-element.10, f32[38,38,1]{2,1,0:T(8,128)S(1)} %copy-done.4, f32[38,38,1]{2,1,0:T(8,128)S(1)} %copy-done.3, f32[38,38,511]{2,1,0:T(8,128)} %get-tuple-element.9, ...), kind=kLoop, calls=%fused_computation.61 | loop fusion | flops 37705728 | bytes 30312448 | tf_op jit(solution)/shard_map/add | solution.py:204
  100.1 1.5 fusion.66
  101.6 0.3 fusion.67
  101.9 9.0 %fusion.32 = f32[36,36,512]{2,1,0:T(8,128)S(1)} fusion(f32[40,40,512]{2,1,0:T(8,128)S(1)} %select_select_fusion, f32[40,40,512]{2,1,0:T(8,128)S(1)} %copy-done, f32[36,36,511]{2,1,0:T(8,128)S(1)} %get-tuple-element.14, f32[36,36,1]{2,1,0:T(8,128)S(1)} %get-tuple-element.16, f32[36,36,1]{2,1,0:T(8,128)S(1)} %get-tuple-element.15, ...), kind=kLoop, calls=%fused_computation.72 | loop fusion | flops 33841152 | bytes 27205632 | tf_op jit(solution)/shard_map/add | solution.py:204
  110.8 1.4 fusion.68
  112.2 0.3 fusion.69
  112.5 9.3 %fusion.38 = f32[34,34,512]{2,1,0:T(8,128)S(1)} fusion(f32[40,40,512]{2,1,0:T(8,128)S(1)} %select_select_fusion, f32[40,40,512]{2,1,0:T(8,128)S(1)} %copy-done, f32[34,34,511]{2,1,0:T(8,128)S(1)} %get-tuple-element.18, f32[34,34,1]{2,1,0:T(8,128)S(1)} %get-tuple-element.20, f32[34,34,1]{2,1,0:T(8,128)S(1)} %get-tuple-element.19, ...), kind=kLoop, calls=%fused_computation.86 | loop fusion | flops 30185472 | bytes 24266752 | tf_op jit(solution)/shard_map/add | solution.py:204
  121.8 1.0 fusion.70
  122.9 0.3 fusion.71
  123.1 6.1 %fusion.41 = f32[32,32,512]{2,1,0:T(8,128)S(1)} fusion(f32[40,40,512]{2,1,0:T(8,128)S(1)} %select_select_fusion, f32[40,40,512]{2,1,0:T(8,128)S(1)} %copy-done, f32[32,32,511]{2,1,0:T(8,128)S(1)} %get-tuple-element.22, f32[32,32,1]{2,1,0:T(8,128)S(1)} %get-tuple-element.24, f32[32,32,1]{2,1,0:T(8,128)S(1)} %get-tuple-element.23, ...), kind=kLoop, calls=%fused_computation.97 | loop fusion | flops 26738688 | bytes 21495808 | tf_op jit(solution)/shard_map/add | solution.py:204
  129.3 1.7 reshape.348
  131.0 1.8 copy.29
  132.8 2.9 %gather_fusion = f32[32,16,16,128]{3,2,1,0:T(8,128)} fusion(f32[2,16,2,16,4,128]{5,3,4,2,1,0:T(8,128)S(1)} %copy.29, s32[32]{0:T(128)S(1)} %fusion.60), kind=kCustom, calls=%fused_computation | custom fusion | bytes 8388992 | tf_op jit(solution)/shard_map/gather | solution.py:264
  135.7 12.4 %all-to-all-start = ((f32[32,16,16,128]{3,2,1,0:T(8,128)}), f32[32,16,16,128]{3,2,1,0:T(8,128)}, u32[]{:S(2)}, u32[]{:S(2)}) async-start(f32[32,16,16,128]{3,2,1,0:T(8,128)} %gather_fusion), calls=%async_computation | async-start | bytes 8388608 | tf_op jit(solution)/shard_map/all_to_all | solution.py:267
  148.1 94.2 %all-to-all-done = f32[32,16,16,128]{3,2,1,0:T(8,128)} async-done(((f32[32,16,16,128]{3,2,1,0:T(8,128)}), f32[32,16,16,128]{3,2,1,0:T(8,128)}, u32[]{:S(2)}, u32[]{:S(2)}) %all-to-all-start) | async-done | bytes 4194336 | tf_op jit(solution)/shard_map/all_to_all | solution.py:267
  242.3 3.8 %gather_fusion.1 = f32[8,16,16,128]{3,2,1,0:T(8,128)} fusion(f32[32,16,16,128]{3,2,1,0:T(8,128)} %all-to-all-done, s32[1024]{0:T(1024)S(1)} %pad_clamp_fusion), kind=kCustom, calls=%fused_computation.1 | custom fusion | bytes 2097184 | tf_op jit(solution)/shard_map/gather | solution.py:268
  (85 shorter events, 2.2 us)
Async XLA Ops:
  0.0 17.1 %copy-start.12 = (s32[16,6]{0,1:T(8,128)S(1)}, s32[16,6]{0,1:T(8,128)}, u32[]{:S(2)}) copy-start(s32[16,6]{0,1:T(8,128)} %param.11) | copy-start | bytes 1156
  0.0 10.3 %copy-start.5 = (bf16[32,32,512]{2,1,0:T(8,128)(2,1)S(1)}, bf16[32,32,512]{2,1,0:T(8,128)(2,1)}, u32[]{:S(2)}) copy-start(bf16[32,32,512]{2,1,0:T(8,128)(2,1)} %param.7) | copy-start | bytes 3145732
  3.1 25.1 %collective-permute-start.1 = (f32[65592]{0:T(1024)S(1)}, f32[65592]{0:T(1024)S(1)}, u32[]{:S(2)}, u32[]{:S(2)}) collective-permute-start(f32[65592]{0:T(1024)S(1)} %pad_maximum_fusion.4), channel_id=1, source_target_pairs={{32,0},{64,32},{96,64},{128,96},{160,128},{192,160},{224,192},{33,... | collective-permute-start | bytes 787112 | tf_op jit(solution)/shard_map/ppermute | solution.py:169
  8.4 19.9 %collective-permute-start = (f32[65592]{0:T(1024)S(1)}, f32[65592]{0:T(1024)S(1)}, u32[]{:S(2)}, u32[]{:S(2)}) collective-permute-start(f32[65592]{0:T(1024)S(1)} %pad_maximum_fusion.3), channel_id=1, source_target_pairs={{0,32},{32,64},{64,96},{96,128},{128,160},{160,192},{192,224},{1,3... | collective-permute-start | bytes 787112 | tf_op jit(solution)/shard_map/ppermute | solution.py:169
  10.3 9.5 %collective-permute-start.4 = (bf16[7,32,512]{2,1,0:T(8,128)(2,1)S(1)}, bf16[7,32,512]{2,1,0:T(8,128)(2,1)S(1)}, u32[]{:S(2)}, u32[]{:S(2)}) collective-permute-start(bf16[7,32,512]{2,1,0:T(8,128)(2,1)S(1)} %get-tuple-element.32), channel_id=1, source_target_pairs={{0,32},{32,64},{64,96},{96,128},{128,160},{160,192},{192,224},{1,3... | collective-permute-start | bytes 688136 | tf_op jit(solution)/shard_map/ppermute | solution.py:167
  12.3 7.7 %collective-permute-start.5 = (bf16[7,32,512]{2,1,0:T(8,128)(2,1)S(1)}, bf16[7,32,512]{2,1,0:T(8,128)(2,1)S(1)}, u32[]{:S(2)}, u32[]{:S(2)}) collective-permute-start(bf16[7,32,512]{2,1,0:T(8,128)(2,1)S(1)} %get-tuple-element.31), channel_id=1, source_target_pairs={{32,0},{64,32},{96,64},{128,96},{160,128},{192,160},{224,192},{33,... | collective-permute-start | bytes 688136 | tf_op jit(solution)/shard_map/ppermute | solution.py:167
  19.8 8.8 %copy-start.6 = (f32[2,2,4,1]{3,2,1,0:T(4,128)}, f32[2,2,4,1]{3,2,1,0:T(4,128)S(1)}, u32[]{:S(2)}) copy-start(f32[2,2,4,1]{3,2,1,0:T(4,128)S(1)} %concatenate.126) | copy-start | bytes 196
  20.0 1.2 copy-start.2
  22.2 16.3 %collective-permute-start.7 = (bf16[46,7,512]{2,1,0:T(8,128)(2,1)}, bf16[46,7,512]{2,1,0:T(8,128)(2,1)}, u32[]{:S(2)}, u32[]{:S(2)}) collective-permute-start(bf16[46,7,512]{2,1,0:T(8,128)(2,1)} %get-tuple-element.30), channel_id=1, source_target_pairs={{1,0},{2,1},{3,2},{4,3},{5,4},{6,5},{7,6},{8,7},{9,8},{10,9},{11,1... | collective-permute-start | bytes 989192 | tf_op jit(solution)/shard_map/ppermute | solution.py:167
  23.5 15.0 %collective-permute-start.6 = (bf16[46,7,512]{2,1,0:T(8,128)(2,1)}, bf16[46,7,512]{2,1,0:T(8,128)(2,1)}, u32[]{:S(2)}, u32[]{:S(2)}) collective-permute-start(bf16[46,7,512]{2,1,0:T(8,128)(2,1)} %get-tuple-element.29), channel_id=1, source_target_pairs={{0,1},{1,2},{2,3},{3,4},{4,5},{5,6},{6,7},{7,8},{8,9},{9,10},{10,1... | collective-permute-start | bytes 989192 | tf_op jit(solution)/shard_map/ppermute | solution.py:167
  28.3 0.6 copy-start.8
  28.4 0.6 copy-start.10
  31.0 11.3 %copy-start.1 = (f32[40,32,512]{2,1,0:T(8,128)}, f32[40,32,512]{2,1,0:T(8,128)S(1)}, u32[]{:S(2)}) copy-start(f32[40,32,512]{2,1,0:T(8,128)S(1)} %constant_dynamic-update-slice_fusion) | copy-start | bytes 7864324
  32.2 27.2 %collective-permute-start.3 = (f32[82032]{0:T(1024)}, f32[82032]{0:T(1024)}, u32[]{:S(2)}, u32[]{:S(2)}) collective-permute-start(f32[82032]{0:T(1024)} %pad_maximum_fusion.2), channel_id=1, source_target_pairs={{1,0},{2,1},{3,2},{4,3},{5,4},{6,5},{7,6},{8,7},{9,8},{10,9},{11,1... | collective-permute-start | bytes 984392 | tf_op jit(solution)/shard_map/ppermute | solution.py:169
  33.7 27.5 %collective-permute-start.2 = (f32[82032]{0:T(1024)S(1)}, f32[82032]{0:T(1024)}, u32[]{:S(2)}, u32[]{:S(2)}) collective-permute-start(f32[82032]{0:T(1024)S(1)} %pad_maximum_fusion.1), channel_id=1, source_target_pairs={{0,1},{1,2},{2,3},{3,4},{4,5},{5,6},{6,7},{7,8},{8,9},{9,10},{10,1... | collective-permute-start | bytes 984392 | tf_op jit(solution)/shard_map/ppermute | solution.py:169
  69.5 3.0 %copy-start.7 = (f32[2,2,4,1]{3,2,1,0:T(4,128)S(1)}, f32[2,2,4,1]{3,2,1,0:T(4,128)}, u32[]{:S(2)}) copy-start(f32[2,2,4,1]{3,2,1,0:T(4,128)} %copy-done.6) | copy-start | bytes 196
  69.5 3.0 %copy-start.9 = (f32[1,2,4,7]{3,2,1,0:T(4,128)S(1)}, f32[1,2,4,7]{3,2,1,0:T(4,128)}, u32[]{:S(2)}) copy-start(f32[1,2,4,7]{3,2,1,0:T(4,128)} %copy-done.8) | copy-start | bytes 676
  69.5 3.0 %copy-start.11 = (f32[1,2,4,7]{3,2,1,0:T(4,128)S(1)}, f32[1,2,4,7]{3,2,1,0:T(4,128)}, u32[]{:S(2)}) copy-start(f32[1,2,4,7]{3,2,1,0:T(4,128)} %copy-done.10) | copy-start | bytes 676
  69.5 3.0 %copy-start.18 = (s32[7]{0:T(128)S(1)}, s32[7]{0:T(128)}, u32[]{:S(2)}) copy-start(s32[7]{0:T(128)} %constant.235.clone) | copy-start | bytes 88
  69.5 12.6 %copy-start.15 = (pred[40]{0:T(512)(128)(4,1)S(1)}, pred[40]{0:T(512)(128)(4,1)}, u32[]{:S(2)}) copy-start(pred[40]{0:T(512)(128)(4,1)} %get-tuple-element.49) | copy-start | bytes 124
  76.1 8.2 %copy-start.13 = (s32[512]{0:T(512)S(1)}, s32[512]{0:T(512)}, u32[]{:S(2)}) copy-start(s32[512]{0:T(512)} %get-tuple-element.53) | copy-start | bytes 6148
  76.1 8.2 %copy-start.14 = (s32[512]{0:T(512)S(1)}, s32[512]{0:T(512)}, u32[]{:S(2)}) copy-start(s32[512]{0:T(512)} %get-tuple-element.54) | copy-start | bytes 6148
  76.1 8.2 %copy-start.16 = (pred[40]{0:T(512)(128)(4,1)S(1)}, pred[40]{0:T(512)(128)(4,1)}, u32[]{:S(2)}) copy-start(pred[40]{0:T(512)(128)(4,1)} %get-tuple-element.50) | copy-start | bytes 124
  76.1 8.2 %copy-start.17 = (pred[40]{0:T(512)(128)(4,1)S(1)}, pred[40]{0:T(512)(128)(4,1)}, u32[]{:S(2)}) copy-start(pred[40]{0:T(512)(128)(4,1)} %get-tuple-element.56) | copy-start | bytes 124
  80.8 7.6 %copy-start = (f32[40,40,512]{2,1,0:T(8,128)S(1)}, f32[40,40,512]{2,1,0:T(8,128)}, u32[]{:S(2)}) copy-start(f32[40,40,512]{2,1,0:T(8,128)} %fusion.18) | copy-start | bytes 9830404
  80.8 7.6 %copy-start.3 = (f32[38,38,1]{2,1,0:T(8,128)S(1)}, f32[38,38,1]{2,1,0:T(8,128)}, u32[]{:S(2)}) copy-start(f32[38,38,1]{2,1,0:T(8,128)} %get-tuple-element.11) | copy-start | bytes 17332
  80.8 7.6 %copy-start.4 = (f32[38,38,1]{2,1,0:T(8,128)S(1)}, f32[38,38,1]{2,1,0:T(8,128)}, u32[]{:S(2)}) copy-start(f32[38,38,1]{2,1,0:T(8,128)} %get-tuple-element.12) | copy-start | bytes 17332
  135.7 12.4 %copy-start.19 = (s32[8]{0:T(128)S(1)}, s32[8]{0:T(128)}, u32[]{:S(2)}) copy-start(s32[8]{0:T(128)} %param.10) | copy-start | bytes 100
  135.7 106.6 %all-to-all-start = ((f32[32,16,16,128]{3,2,1,0:T(8,128)}), f32[32,16,16,128]{3,2,1,0:T(8,128)}, u32[]{:S(2)}, u32[]{:S(2)}) async-start(f32[32,16,16,128]{3,2,1,0:T(8,128)} %gather_fusion), calls=%async_computation | async-start | bytes 8388608 | tf_op jit(solution)/shard_map/all_to_all | solution.py:267

commit v7 on v5

--- a/solution.py
+++ b/solution.py
@@ -219,26 +219,22 @@
     lead = BX - STEPS
     weights = jnp.asarray([1 << side for side in range(6)] + [0], jnp.int32)
     brick_code = jnp.sum(jnp.where(wide_info > 0.5, weights, 0), axis=-1)
-    def planes(per_brick):
-        spread = jnp.broadcast_to(
-            per_brick.reshape(BXN + 2, BYN + 2, 1, BZN, 1), (BXN + 2, BYN + 2, BY, BZN, BZ)
-        ).reshape(BXN + 2, (BYN + 2) * BY, BZN * BZ)
-        return spread[:, lead : lead + span_y]
-    def across_x(per_brick):
-        table = planes(per_brick)
-        xe = lax.broadcasted_iota(jnp.int32, wide_level.shape, 0) + lead
-        value = table[BXN + 1][None]
-        for bx in range(BXN, -1, -1):
-            value = jnp.where(xe < (bx + 1) * BX, table[bx][None], value)
-        return value
-    rate = across_x(wide_info[..., 6])
+    def spread(per_brick):
+        table = jnp.broadcast_to(
+            per_brick.reshape(BXN + 2, 1, BYN + 2, 1, BZN), (BXN + 2, BX, BYN + 2, BY, BZN)
+        ).reshape((BXN + 2) * BX, (BYN + 2) * BY, BZN)
+        table = table[lead : lead + span_x, lead : lead + span_y]
+        return jnp.broadcast_to(table[..., None], (span_x, span_y, BZN, BZ)).reshape(
+            span_x, span_y, BZN * BZ
+        )
+    rate = spread(wide_info[..., 6])
     place = (
         lax.broadcasted_iota(jnp.int32, wide_level.shape, 0) + lead,
         lax.broadcasted_iota(jnp.int32, wide_level.shape, 1) + lead,
         lax.broadcasted_iota(jnp.int32, wide_level.shape, 2),
     )
     sizes = (BX, BX, BY, BY, BZ, BZ)
-    code = across_x(brick_code)
+    code = spread(brick_code)
     for side in range(6):
         pos = place[side // 2] % sizes[side]
         inner = pos != (0 if side % 2 == 0 else sizes[side] - 1)

time: 245 us -> 253 us (1.033)
  local copies, waits for them, and re-layouts: 43.2 us -> 58.2 us
  other arithmetic: 68.2 us -> 62.5 us
    reshape x2, local copies, waits for them, and re-layouts: 4.12 us -> 10.2 us  [spread(): jnp.broadcast_to(table[..., None], (span_x, span_y, BZN, BZ))]
    broadcast_in_dim x4, local copies, waits for them, and re-layouts: 4.66 us -> 9.64 us  [the longest x2 9.17 us: spread(): jnp.broadcast_to(table[..., None], (span_x, span_y, BZN, BZ))]
    unnamed x50 -> x42, local copies, waits for them, and re-layouts: 4.86 us -> 5.9 us
  transfers between devices with their start and end apart: 9 -> 9, of which waited for: 1 -> 1; matrix products, arithmetic and copies ran while one was open for 14% -> 15% of each run, Pallas kernels for 0% -> 0%
where the time goes in v7:
time: 253 us; the launch traced here: 250 us
  waiting for transfers between devices  93.7 us (37%)
  other arithmetic  62.5 us (25%)
  local copies, waits for them, and re-layouts  58.2 us (23%)
  starting transfers between devices  34.7 us (14%)
    all_to_all x1, waiting for transfers between devices, per_device(): lax.all_to_all(sending, 'dev', split_axis=0, concat_axis=0, tiled=True)  93.7 us
    add x4, other arithmetic, region_step(): return centre + time_step * edge * force * jnp.sqrt(1.0 + gradient)  30.8 us
    ppermute x4, starting transfers between devices, sent(): image_part = lax.ppermute(pieces[0], axis, pairs)  12 us
    ppermute x4, starting transfers between devices, sent(): flat = lax.ppermute(flat, axis, pairs)  11.7 us
    all_to_all x1, starting transfers between devices, per_device(): lax.all_to_all(sending, 'dev', split_axis=0, concat_axis=0, tiled=True)  11 us
    add x3, other arithmetic, smooth_axis(): summed + gauss_taps[offset] * lax.slice_in_dim(values, offset, offset + l...  11 us
    reshape x2, local copies, waits for them, and re-layouts, spread(): jnp.broadcast_to(table[..., None], (span_x, span_y, BZN, BZ))  10.2 us
    broadcast_in_dim x2, local copies, waits for them, and re-layouts, spread(): jnp.broadcast_to(table[..., None], (span_x, span_y, BZN, BZ))  9.17 us
  transfers between devices with their start and end apart: 9, of which 1 were waited for; matrix products, arithmetic and copies ran while one was open for 15% of the time, Pallas kernels for 0%

profile of v7, /device:TPU:1, one launch (start us, length us, event | category | flops | bytes accessed | tf_op | source)
XLA Modules:
  0.0 249.6 jit_solution(11167044032611465114)
XLA Ops:
  0.0 1.2 fusion.71
  1.2 5.1 %collective-permute-start.5 = (bf16[7,32,512]{2,1,0:T(8,128)(2,1)S(1)}, bf16[7,32,512]{2,1,0:T(8,128)(2,1)S(1)}, u32[]{:S(2)}, u32[]{:S(2)}) collective-permute-start(bf16[7,32,512]{2,1,0:T(8,128)(2,1)S(1)} %get-tuple-element.31), channel_id=1, source_target_pairs={{32,0},{64,32},{96,64},{128,96},{160,128},{192,160},{224,192},{33,... | collective-permute-start | bytes 688136 | tf_op jit(solution)/shard_map/ppermute | solution.py:167
  6.3 1.9 collective-permute-start.4
  8.2 0.8 select_reduce_fusion.2
  9.1 0.8 copy.24
  10.0 1.1 fusion.69
  11.2 1.9 collective-permute-start
  13.3 0.7 pad_maximum_fusion.4
  14.0 3.1 %collective-permute-start.1 = (f32[65592]{0:T(1024)}, f32[65592]{0:T(1024)}, u32[]{:S(2)}, u32[]{:S(2)}) collective-permute-start(f32[65592]{0:T(1024)} %pad_maximum_fusion.4), channel_id=1, source_target_pairs={{32,0},{64,32},{96,64},{128,96},{160,128},{192,160},{224,192},{33,... | collective-permute-start | bytes 787112 | tf_op jit(solution)/shard_map/ppermute | solution.py:169
  17.2 0.6 compare_and_fusion
  17.7 0.6 fusion.73
  18.4 0.6 compare_select_fusion.10
  19.0 0.6 iota_and_fusion
  19.6 1.3 broadcast_compare_fusion
  21.0 0.6 fusion.47
  21.7 1.0 constant_dynamic-update-slice_fusion.5
  22.9 3.6 %collective-permute-start.6 = (bf16[46,7,512]{2,1,0:T(8,128)(2,1)S(1)}, bf16[46,7,512]{2,1,0:T(8,128)(2,1)}, u32[]{:S(2)}, u32[]{:S(2)}) collective-permute-start(bf16[46,7,512]{2,1,0:T(8,128)(2,1)S(1)} %get-tuple-element.29), channel_id=1, source_target_pairs={{0,1},{1,2},{2,3},{3,4},{4,5},{5,6},{6,7},{7,8},{8,9},{9,10},{10,1... | collective-permute-start | bytes 989192 | tf_op jit(solution)/shard_map/ppermute | solution.py:167
  26.6 1.3 collective-permute-start.7
  27.9 1.0 slice.409
  28.9 0.7 slice.412
  29.7 1.0 slice.410
  30.7 0.7 slice.413
  31.8 1.8 constant_dynamic-update-slice_fusion.1
  34.0 1.3 collective-permute-start.3
  35.3 5.3 %collective-permute-start.2 = (f32[82032]{0:T(1024)S(1)}, f32[82032]{0:T(1024)}, u32[]{:S(2)}, u32[]{:S(2)}) collective-permute-start(f32[82032]{0:T(1024)S(1)} %pad_maximum_fusion.1), channel_id=1, source_target_pairs={{0,1},{1,2},{2,3},{3,4},{4,5},{5,6},{6,7},{7,8},{8,9},{9,10},{10,1... | collective-permute-start | bytes 984392 | tf_op jit(solution)/shard_map/ppermute | solution.py:169
  40.7 3.6 %fusion.35 = f32[46,46,518]{2,1,0:T(8,128)S(1)} fusion(bf16[46,7,512]{2,1,0:T(8,128)(2,1)} %collective-permute-done.7, bf16[46,32,512]{2,1,0:T(8,128)(2,1)S(1)} %constant_dynamic-update-slice_fusion.3, bf16[46,7,512]{2,1,0:T(8,128)(2,1)} %collective-permute-done.6), kind=kLoop, calls=%fused_computation.93 | loop fusion | flops 13153056 | bytes 6551136 | tf_op jit(solution)/shard_map/jit(_pad)/pad | solution.py:216
  44.3 2.6 %fusion.9 = f32[42,46,518]{2,1,0:T(8,128)S(1)} fusion(f32[46,46,518]{2,1,0:T(8,128)S(1)} %fusion.35), kind=kLoop, calls=%fused_computation.24 | loop fusion | flops 9006984 | bytes 24018624 | tf_op jit(solution)/shard_map/add | solution.py:49
  46.9 2.9 %fusion.5 = f32[42,42,518]{2,1,0:T(8,128)S(1)} fusion(f32[42,46,518]{2,1,0:T(8,128)S(1)} %fusion.9), kind=kLoop, calls=%fused_computation.15 | loop fusion | flops 8223768 | bytes 21930048 | tf_op jit(solution)/shard_map/add | solution.py:49
  49.8 5.5 %fusion.1 = f32[42,42,514]{2,1,0:T(8,128)S(1)} fusion(f32[42,42,518]{2,1,0:T(8,128)S(1)} %fusion.5), kind=kLoop, calls=%fused_computation.6 | loop fusion | flops 8160264 | bytes 21760704 | tf_op jit(solution)/shard_map/add | solution.py:49
  55.3 6.1 %fusion.18 = f32[40,40,512]{2,1,0:T(8,128)} fusion(f32[42,42,514]{2,1,0:T(8,128)S(1)} %fusion.1), kind=kLoop, calls=%fused_computation.44 | loop fusion | flops 11468800 | bytes 22937600 | tf_op jit(solution)/shard_map/div | solution.py:60
  61.4 0.7 copy-done.4
  62.1 0.8 reshape.351
  63.0 1.0 slice.415
  64.0 0.8 reshape.348
  64.8 2.3 pad_maximum_fusion
  67.2 1.4 fusion.62
  68.6 4.0 %fusion.61 = (f32[38,38,511]{2,1,0:T(8,128)}, f32[38,38,511]{2,1,0:T(8,128)}) fusion(f32[40,40,512]{2,1,0:T(8,128)S(1)} %pad_maximum_fusion), kind=kLoop, calls=%fused_computation.213 | loop fusion | bytes 11806144 | tf_op jit(solution)/shard_map/slice | solution.py:193
  72.7 0.7 slice.444
  73.5 0.4 select_reduce_fusion
  74.1 0.2 broadcast_in_dim.80
  74.3 1.0 slice.457
  75.3 0.2 broadcast_in_dim.77
  75.6 4.5 %broadcast_in_dim.78 = s32[40,40,4,128]{3,2,1,0:T(4,128)} broadcast(s32[40,40,4]{2,1,0:T(8,128)S(1)} %slice.446), dimensions={0,1,2} | broadcast | bytes 3302400 | tf_op jit(solution)/shard_map/broadcast_in_dim | solution.py:227
  80.1 5.1 %reshape.355 = s32[40,40,512]{2,1,0:T(8,128)} reshape(s32[40,40,4,128]{3,2,1,0:T(4,128)} %broadcast_in_dim.78) | data formatting | bytes 6553600 | tf_op jit(solution)/shard_map/reshape | solution.py:227
  85.2 4.7 %broadcast_in_dim.81 = f32[40,40,4,128]{3,2,1,0:T(4,128)} broadcast(f32[40,40,4]{2,1,0:T(8,128)} %slice.457), dimensions={0,1,2} | broadcast | bytes 3302400 | tf_op jit(solution)/shard_map/broadcast_in_dim | solution.py:227
  89.9 5.1 %reshape.357 = f32[40,40,512]{2,1,0:T(8,128)} reshape(f32[40,40,4,128]{3,2,1,0:T(4,128)} %broadcast_in_dim.81) | data formatting | bytes 6553600 | tf_op jit(solution)/shard_map/reshape | solution.py:227
  95.1 2.8 %shift-left_or_fusion = s32[40,40,512]{2,1,0:T(8,128)S(1)} fusion(s32[40,40,512]{2,1,0:T(8,128)} %reshape.355, s32[512]{0:T(512)S(1)} %copy-done.8, s32[512]{0:T(512)S(1)} %copy-done.9, s32[40]{0:T(128)S(1)} %copy-done.11, s32[40]{0:T(128)S(1)} %copy-done.12, pred[40]{0:T(512)(128)(4,1)S(1)} %copy-done.10, pred[512]{0:T(512)(128)(4,1)S(1)} %copy-done.14), kind=kLoop, calls=%fused_computation.53 | loop fusion | flops 22118400 | bytes 6558568 | tf_op jit(solution)/shard_map/or | solution.py:241
  98.0 1.0 copy-done.1
  99.0 9.8 %fusion.29 = f32[38,38,512]{2,1,0:T(8,128)S(1)} fusion(f32[40,40,512]{2,1,0:T(8,128)S(1)} %copy-done, f32[40,40,512]{2,1,0:T(8,128)S(1)} %copy-done.1, f32[38,38,511]{2,1,0:T(8,128)} %get-tuple-element.10, f32[38,38,1]{2,1,0:T(8,128)} %get-tuple-element.12, f32[38,38,1]{2,1,0:T(8,128)} %get-tuple-element.11, f32[38,38,511]{2,1,0:T(8,128)} %get-tuple-element.9, ...), kind=kLoop, calls=%fused_computation.60 | loop fusion | flops 37705728 | bytes 32530432 | tf_op jit(solution)/shard_map/add | solution.py:204
  108.8 0.3 fusion.64
  109.1 1.5 fusion.63
  110.7 7.6 %fusion.32 = f32[36,36,512]{2,1,0:T(8,128)S(1)} fusion(f32[40,40,512]{2,1,0:T(8,128)S(1)} %copy-done, f32[40,40,512]{2,1,0:T(8,128)S(1)} %copy-done.1, f32[36,36,511]{2,1,0:T(8,128)S(1)} %get-tuple-element.14, f32[36,36,1]{2,1,0:T(8,128)S(1)} %get-tuple-element.16, f32[36,36,1]{2,1,0:T(8,128)S(1)} %get-tuple-element.15, ...), kind=kLoop, calls=%fused_computation.77 | loop fusion | flops 33841152 | bytes 29196288 | tf_op jit(solution)/shard_map/add | solution.py:204
  118.3 0.3 fusion.66
  118.6 1.4 fusion.65
  120.0 8.0 %fusion.38 = f32[34,34,512]{2,1,0:T(8,128)S(1)} fusion(f32[40,40,512]{2,1,0:T(8,128)S(1)} %copy-done, f32[40,40,512]{2,1,0:T(8,128)S(1)} %copy-done.1, f32[34,34,511]{2,1,0:T(8,128)S(1)} %get-tuple-element.18, f32[34,34,1]{2,1,0:T(8,128)S(1)} %get-tuple-element.20, f32[34,34,1]{2,1,0:T(8,128)S(1)} %get-tuple-element.19, ...), kind=kLoop, calls=%fused_computation.97 | loop fusion | flops 30185472 | bytes 26042368 | tf_op jit(solution)/shard_map/add | solution.py:204
  127.9 0.3 fusion.68
  128.2 1.0 fusion.67
  129.2 5.4 %fusion.41 = f32[32,32,512]{2,1,0:T(8,128)S(1)} fusion(f32[40,40,512]{2,1,0:T(8,128)S(1)} %copy-done, f32[40,40,512]{2,1,0:T(8,128)S(1)} %copy-done.1, f32[32,32,511]{2,1,0:T(8,128)S(1)} %get-tuple-element.22, f32[32,32,1]{2,1,0:T(8,128)S(1)} %get-tuple-element.24, f32[32,32,1]{2,1,0:T(8,128)S(1)} %get-tuple-element.23, ...), kind=kLoop, calls=%fused_computation.114 | loop fusion | flops 26738688 | bytes 23068672 | tf_op jit(solution)/shard_map/add | solution.py:204
  134.7 1.7 reshape.358
  136.4 1.8 copy.29
  138.2 2.9 %gather_fusion = f32[32,16,16,128]{3,2,1,0:T(8,128)} fusion(f32[2,16,2,16,4,128]{5,3,4,2,1,0:T(8,128)S(1)} %copy.29, s32[32]{0:T(128)S(1)} %fusion.60), kind=kCustom, calls=%fused_computation | custom fusion | bytes 8388992 | tf_op jit(solution)/shard_map/gather | solution.py:259
  141.1 11.0 %all-to-all-start = ((f32[32,16,16,128]{3,2,1,0:T(8,128)}), f32[32,16,16,128]{3,2,1,0:T(8,128)}, u32[]{:S(2)}, u32[]{:S(2)}) async-start(f32[32,16,16,128]{3,2,1,0:T(8,128)} %gather_fusion), calls=%async_computation | async-start | bytes 8388608 | tf_op jit(solution)/shard_map/all_to_all | solution.py:262
  152.2 93.7 %all-to-all-done = f32[32,16,16,128]{3,2,1,0:T(8,128)} async-done(((f32[32,16,16,128]{3,2,1,0:T(8,128)}), f32[32,16,16,128]{3,2,1,0:T(8,128)}, u32[]{:S(2)}, u32[]{:S(2)}) %all-to-all-start) | async-done | bytes 4194336 | tf_op jit(solution)/shard_map/all_to_all | solution.py:262
  245.9 3.8 %gather_fusion.1 = f32[8,16,16,128]{3,2,1,0:T(8,128)} fusion(f32[32,16,16,128]{3,2,1,0:T(8,128)} %all-to-all-done, s32[1024]{0:T(1024)S(1)} %pad_clamp_fusion), kind=kCustom, calls=%fused_computation.1 | custom fusion | bytes 2097184 | tf_op jit(solution)/shard_map/gather | solution.py:263
  (78 shorter events, 2.6 us)
Async XLA Ops:
  0.0 22.7 %copy-start.3 = (bf16[32,32,512]{2,1,0:T(8,128)(2,1)S(1)}, bf16[32,32,512]{2,1,0:T(8,128)(2,1)}, u32[]{:S(2)}) copy-start(bf16[32,32,512]{2,1,0:T(8,128)(2,1)} %param.7) | copy-start | bytes 3145732
  0.0 17.7 %copy-start.7 = (s32[16,6]{0,1:T(8,128)S(1)}, s32[16,6]{0,1:T(8,128)}, u32[]{:S(2)}) copy-start(s32[16,6]{0,1:T(8,128)} %param.11) | copy-start | bytes 1156
  1.2 21.6 %collective-permute-start.5 = (bf16[7,32,512]{2,1,0:T(8,128)(2,1)S(1)}, bf16[7,32,512]{2,1,0:T(8,128)(2,1)S(1)}, u32[]{:S(2)}, u32[]{:S(2)}) collective-permute-start(bf16[7,32,512]{2,1,0:T(8,128)(2,1)S(1)} %get-tuple-element.31), channel_id=1, source_target_pairs={{32,0},{64,32},{96,64},{128,96},{160,128},{192,160},{224,192},{33,... | collective-permute-start | bytes 688136 | tf_op jit(solution)/shard_map/ppermute | solution.py:167
  6.3 15.4 %collective-permute-start.4 = (bf16[7,32,512]{2,1,0:T(8,128)(2,1)S(1)}, bf16[7,32,512]{2,1,0:T(8,128)(2,1)}, u32[]{:S(2)}, u32[]{:S(2)}) collective-permute-start(bf16[7,32,512]{2,1,0:T(8,128)(2,1)S(1)} %get-tuple-element.32), channel_id=1, source_target_pairs={{0,32},{32,64},{64,96},{96,128},{128,160},{160,192},{192,224},{1,3... | collective-permute-start | bytes 688136 | tf_op jit(solution)/shard_map/ppermute | solution.py:167
  11.2 16.7 %collective-permute-start = (f32[65592]{0:T(1024)S(1)}, f32[65592]{0:T(1024)}, u32[]{:S(2)}, u32[]{:S(2)}) collective-permute-start(f32[65592]{0:T(1024)S(1)} %pad_maximum_fusion.3), channel_id=1, source_target_pairs={{0,32},{32,64},{64,96},{96,128},{128,160},{160,192},{192,224},{1,3... | collective-permute-start | bytes 787112 | tf_op jit(solution)/shard_map/ppermute | solution.py:169
  14.0 15.7 %collective-permute-start.1 = (f32[65592]{0:T(1024)}, f32[65592]{0:T(1024)}, u32[]{:S(2)}, u32[]{:S(2)}) collective-permute-start(f32[65592]{0:T(1024)} %pad_maximum_fusion.4), channel_id=1, source_target_pairs={{32,0},{64,32},{96,64},{128,96},{160,128},{192,160},{224,192},{33,... | collective-permute-start | bytes 787112 | tf_op jit(solution)/shard_map/ppermute | solution.py:169
  21.7 9.8 %copy-start.5 = (f32[2,2,4,1]{3,2,1,0:T(4,128)}, f32[2,2,4,1]{3,2,1,0:T(4,128)S(1)}, u32[]{:S(2)}) copy-start(f32[2,2,4,1]{3,2,1,0:T(4,128)S(1)} %concatenate.126) | copy-start | bytes 196
  22.9 17.7 %collective-permute-start.6 = (bf16[46,7,512]{2,1,0:T(8,128)(2,1)S(1)}, bf16[46,7,512]{2,1,0:T(8,128)(2,1)}, u32[]{:S(2)}, u32[]{:S(2)}) collective-permute-start(bf16[46,7,512]{2,1,0:T(8,128)(2,1)S(1)} %get-tuple-element.29), channel_id=1, source_target_pairs={{0,1},{1,2},{2,3},{3,4},{4,5},{5,6},{6,7},{7,8},{8,9},{9,10},{10,1... | collective-permute-start | bytes 989192 | tf_op jit(solution)/shard_map/ppermute | solution.py:167
  26.6 14.1 %collective-permute-start.7 = (bf16[46,7,512]{2,1,0:T(8,128)(2,1)S(1)}, bf16[46,7,512]{2,1,0:T(8,128)(2,1)}, u32[]{:S(2)}, u32[]{:S(2)}) collective-permute-start(bf16[46,7,512]{2,1,0:T(8,128)(2,1)S(1)} %get-tuple-element.30), channel_id=1, source_target_pairs={{1,0},{2,1},{3,2},{4,3},{5,4},{6,5},{7,6},{8,7},{9,8},{10,9},{11,1... | collective-permute-start | bytes 989192 | tf_op jit(solution)/shard_map/ppermute | solution.py:167
  33.6 7.1 %copy-start.2 = (f32[40,32,512]{2,1,0:T(8,128)}, f32[40,32,512]{2,1,0:T(8,128)S(1)}, u32[]{:S(2)}) copy-start(f32[40,32,512]{2,1,0:T(8,128)S(1)} %constant_dynamic-update-slice_fusion) | copy-start | bytes 7864324
  34.0 27.4 %collective-permute-start.3 = (f32[82032]{0:T(1024)S(1)}, f32[82032]{0:T(1024)S(1)}, u32[]{:S(2)}, u32[]{:S(2)}) collective-permute-start(f32[82032]{0:T(1024)S(1)} %pad_maximum_fusion.2), channel_id=1, source_target_pairs={{1,0},{2,1},{3,2},{4,3},{5,4},{6,5},{7,6},{8,7},{9,8},{10,9},{11,1... | collective-permute-start | bytes 984392 | tf_op jit(solution)/shard_map/ppermute | solution.py:169
  35.3 27.6 %collective-permute-start.2 = (f32[82032]{0:T(1024)S(1)}, f32[82032]{0:T(1024)}, u32[]{:S(2)}, u32[]{:S(2)}) collective-permute-start(f32[82032]{0:T(1024)S(1)} %pad_maximum_fusion.1), channel_id=1, source_target_pairs={{0,1},{1,2},{2,3},{3,4},{4,5},{5,6},{6,7},{7,8},{8,9},{9,10},{10,1... | collective-permute-start | bytes 984392 | tf_op jit(solution)/shard_map/ppermute | solution.py:169
  61.4 0.7 copy-start.4
  68.6 4.0 %slice-start = ((f32[82032]{0:T(1024)}), f32[112]{0:T(128)S(1)}, s32[]{:S(2)}) async-start(f32[82032]{0:T(1024)} %copy-done.4), calls=%async_computation.1 | async-start | bytes 1024 | tf_op jit(solution)/shard_map/slice | solution.py:174
  68.6 4.9 %copy-start.6 = (f32[2,2,4,1]{3,2,1,0:T(4,128)S(1)}, f32[2,2,4,1]{3,2,1,0:T(4,128)}, u32[]{:S(2)}) copy-start(f32[2,2,4,1]{3,2,1,0:T(4,128)} %copy-done.5) | copy-start | bytes 196
  68.6 4.9 %copy-start.13 = (s32[7]{0:T(128)S(1)}, s32[7]{0:T(128)}, u32[]{:S(2)}) copy-start(s32[7]{0:T(128)} %constant.225.clone) | copy-start | bytes 88
  89.9 5.1 %copy-start.8 = (s32[512]{0:T(512)S(1)}, s32[512]{0:T(512)}, u32[]{:S(2)}) copy-start(s32[512]{0:T(512)} %get-tuple-element.43) | copy-start | bytes 6148
  89.9 5.1 %copy-start.9 = (s32[512]{0:T(512)S(1)}, s32[512]{0:T(512)}, u32[]{:S(2)}) copy-start(s32[512]{0:T(512)} %get-tuple-element.44) | copy-start | bytes 6148
  89.9 5.1 %copy-start.10 = (pred[40]{0:T(512)(128)(4,1)S(1)}, pred[40]{0:T(512)(128)(4,1)}, u32[]{:S(2)}) copy-start(pred[40]{0:T(512)(128)(4,1)} %compare_and_fusion) | copy-start | bytes 124
  89.9 5.1 %copy-start.11 = (s32[40]{0:T(128)S(1)}, s32[40]{0:T(128)}, u32[]{:S(2)}) copy-start(s32[40]{0:T(128)} %get-tuple-element.41) | copy-start | bytes 484
  89.9 5.1 %copy-start.12 = (s32[40]{0:T(128)S(1)}, s32[40]{0:T(128)}, u32[]{:S(2)}) copy-start(s32[40]{0:T(128)} %get-tuple-element.42) | copy-start | bytes 484
  89.9 5.1 %copy-start.14 = (pred[512]{0:T(512)(128)(4,1)S(1)}, pred[512]{0:T(512)(128)(4,1)}, u32[]{:S(2)}) copy-start(pred[512]{0:T(512)(128)(4,1)} %fusion.47) | copy-start | bytes 1540
  95.1 2.9 %copy-start = (f32[40,40,512]{2,1,0:T(8,128)S(1)}, f32[40,40,512]{2,1,0:T(8,128)}, u32[]{:S(2)}) copy-start(f32[40,40,512]{2,1,0:T(8,128)} %reshape.357) | copy-start | bytes 9830404
  95.1 3.9 %copy-start.1 = (f32[40,40,512]{2,1,0:T(8,128)S(1)}, f32[40,40,512]{2,1,0:T(8,128)}, u32[]{:S(2)}) copy-start(f32[40,40,512]{2,1,0:T(8,128)} %fusion.18) | copy-start | bytes 9830404
  141.1 11.0 %copy-start.15 = (s32[8]{0:T(128)S(1)}, s32[8]{0:T(128)}, u32[]{:S(2)}) copy-start(s32[8]{0:T(128)} %param.10) | copy-start | bytes 100
  141.1 104.8 %all-to-all-start = ((f32[32,16,16,128]{3,2,1,0:T(8,128)}), f32[32,16,16,128]{3,2,1,0:T(8,128)}, u32[]{:S(2)}, u32[]{:S(2)}) async-start(f32[32,16,16,128]{3,2,1,0:T(8,128)} %gather_fusion), calls=%async_computation | async-start | bytes 8388608 | tf_op jit(solution)/shard_map/all_to_all | solution.py:262

commit v8 on v7

--- a/solution.py
+++ b/solution.py
@@ -224,9 +224,11 @@
             per_brick.reshape(BXN + 2, 1, BYN + 2, 1, BZN), (BXN + 2, BX, BYN + 2, BY, BZN)
         ).reshape((BXN + 2) * BX, (BYN + 2) * BY, BZN)
         table = table[lead : lead + span_x, lead : lead + span_y]
-        return jnp.broadcast_to(table[..., None], (span_x, span_y, BZN, BZ)).reshape(
-            span_x, span_y, BZN * BZ
-        )
+        zi = lax.broadcasted_iota(jnp.int32, wide_level.shape, 2)
+        value = table[:, :, BZN - 1][..., None]
+        for bz in range(BZN - 2, -1, -1):
+            value = jnp.where(zi < (bz + 1) * BZ, table[:, :, bz][..., None], value)
+        return value
     rate = spread(wide_info[..., 6])
     place = (
         lax.broadcasted_iota(jnp.int32, wide_level.shape, 0) + lead,

time: 253 us -> 237 us (0.937)
  local copies, waits for them, and re-layouts: 58.2 us -> 39.2 us
    broadcast_in_dim x2, local copies, waits for them, and re-layouts: 9.17 us -> 0.17 us  [spread(): value = jnp.where(zi < (bz + 1) * BZ, table[:, :, bz][..., None], value)]
    reshape x2, local copies, waits for them, and re-layouts: 10.2 us -> 2.59 us  [spread(): table = jnp.broadcast_to(per_brick.reshape(BXN + 2, 1, BYN + 2, 1, BZN),...]
    unnamed x42 -> x58, local copies, waits for them, and re-layouts: 5.9 us -> 4.85 us
  transfers between devices with their start and end apart: 9 -> 9, of which waited for: 1 -> 1; matrix products, arithmetic and copies ran while one was open for 15% -> 14% of each run, Pallas kernels for 0% -> 0%
where the time goes in v8:
time: 237 us; the launch traced here: 233 us
  waiting for transfers between devices  94.3 us (40%)
  other arithmetic  63.4 us (27%)
  local copies, waits for them, and re-layouts  39.2 us (17%)
  starting transfers between devices  35.8 us (15%)
    all_to_all x1, waiting for transfers between devices, per_device(): lax.all_to_all(sending, 'dev', split_axis=0, concat_axis=0, tiled=True)  94.3 us
    add x4, other arithmetic, region_step(): return centre + time_step * edge * force * jnp.sqrt(1.0 + gradient)  31 us
    ppermute x4, starting transfers between devices, sent(): flat = lax.ppermute(flat, axis, pairs)  13 us
    all_to_all x1, starting transfers between devices, per_device(): lax.all_to_all(sending, 'dev', split_axis=0, concat_axis=0, tiled=True)  12.4 us
    add x3, other arithmetic, smooth_axis(): summed + gauss_taps[offset] * lax.slice_in_dim(values, offset, offset + l...  11 us
    ppermute x4, starting transfers between devices, sent(): image_part = lax.ppermute(pieces[0], axis, pairs)  10.4 us
    slice x4, local copies, waits for them, and re-layouts, region_step(): centre[:, :, 1:]  8 us
    div x1, other arithmetic, edge_map(): 1.0 / (1.0 + (grad_x * grad_x + grad_y * grad_y + grad_z * grad_z) / cont...  6.09 us
  transfers between devices with their start and end apart: 9, of which 1 were waited for; matrix products, arithmetic and copies ran while one was open for 14% of the time, Pallas kernels for 0%

profile of v8, /device:TPU:1, one launch (start us, length us, event | category | flops | bytes accessed | tf_op | source)
XLA Modules:
  0.0 233.5 jit_solution(13589578763237295725)
XLA Ops:
  0.0 0.9 copy.35
  0.9 0.8 select_reduce_fusion.2
  1.9 1.1 fusion.69
  3.1 5.1 %collective-permute-start.1 = (f32[65592]{0:T(1024)S(1)}, f32[65592]{0:T(1024)S(1)}, u32[]{:S(2)}, u32[]{:S(2)}) collective-permute-start(f32[65592]{0:T(1024)S(1)} %pad_maximum_fusion.4), channel_id=1, source_target_pairs={{32,0},{64,32},{96,64},{128,96},{160,128},{192,160},{224,192},{33,... | collective-permute-start | bytes 787112 | tf_op jit(solution)/shard_map/ppermute | solution.py:169
  8.4 1.9 collective-permute-start
  10.3 1.9 collective-permute-start.4
  12.3 2.4 %collective-permute-start.5 = (bf16[7,32,512]{2,1,0:T(8,128)(2,1)S(1)}, bf16[7,32,512]{2,1,0:T(8,128)(2,1)S(1)}, u32[]{:S(2)}, u32[]{:S(2)}) collective-permute-start(bf16[7,32,512]{2,1,0:T(8,128)(2,1)S(1)} %get-tuple-element.31), channel_id=1, source_target_pairs={{32,0},{64,32},{96,64},{128,96},{160,128},{192,160},{224,192},{33,... | collective-permute-start | bytes 688136 | tf_op jit(solution)/shard_map/ppermute | solution.py:167
  14.7 0.5 iota_compare_fusion.4
  15.2 0.6 iota_compare_fusion.6
  15.8 0.6 iota_and_fusion
  16.4 0.5 compare_select_fusion.10
  17.0 0.6 fusion.73
  17.6 1.4 broadcast_compare_fusion
  19.1 0.6 compare_and_fusion
  19.8 0.1 constant_dynamic-update-slice_fusion.4
  20.0 1.1 copy-done.2
  21.1 1.0 fusion.70
  22.1 1.3 collective-permute-start.7
  23.4 4.8 %collective-permute-start.6 = (bf16[46,7,512]{2,1,0:T(8,128)(2,1)}, bf16[46,7,512]{2,1,0:T(8,128)(2,1)}, u32[]{:S(2)}, u32[]{:S(2)}) collective-permute-start(bf16[46,7,512]{2,1,0:T(8,128)(2,1)} %get-tuple-element.29), channel_id=1, source_target_pairs={{0,1},{1,2},{2,3},{3,4},{4,5},{5,6},{6,7},{7,8},{8,9},{9,10},{10,1... | collective-permute-start | bytes 989192 | tf_op jit(solution)/shard_map/ppermute | solution.py:167
  28.5 0.3 copy-done.8
  29.0 1.8 constant_dynamic-update-slice_fusion.1
  30.9 0.1 slice_bitcast_fusion.1
  31.1 1.0 pad_maximum_fusion.2
  32.1 1.3 collective-permute-start.3
  33.6 4.7 %collective-permute-start.2 = (f32[82032]{0:T(1024)S(1)}, f32[82032]{0:T(1024)}, u32[]{:S(2)}, u32[]{:S(2)}) collective-permute-start(f32[82032]{0:T(1024)S(1)} %pad_maximum_fusion.1), channel_id=1, source_target_pairs={{0,1},{1,2},{2,3},{3,4},{4,5},{5,6},{6,7},{7,8},{8,9},{9,10},{10,1... | collective-permute-start | bytes 984392 | tf_op jit(solution)/shard_map/ppermute | solution.py:169
  38.4 3.8 %fusion.35 = f32[46,46,518]{2,1,0:T(8,128)S(1)} fusion(bf16[46,7,512]{2,1,0:T(8,128)(2,1)} %collective-permute-done.7, bf16[46,32,512]{2,1,0:T(8,128)(2,1)} %copy-done.2, bf16[46,7,512]{2,1,0:T(8,128)(2,1)} %collective-permute-done.6), kind=kLoop, calls=%fused_computation.94 | loop fusion | flops 13153056 | bytes 6551136 | tf_op jit(solution)/shard_map/jit(_pad)/pad | solution.py:216
  42.2 2.6 %fusion.9 = f32[42,46,518]{2,1,0:T(8,128)S(1)} fusion(f32[46,46,518]{2,1,0:T(8,128)S(1)} %fusion.35), kind=kLoop, calls=%fused_computation.24 | loop fusion | flops 9006984 | bytes 24018624 | tf_op jit(solution)/shard_map/add | solution.py:49
  44.8 2.9 %fusion.5 = f32[42,42,518]{2,1,0:T(8,128)S(1)} fusion(f32[42,46,518]{2,1,0:T(8,128)S(1)} %fusion.9), kind=kLoop, calls=%fused_computation.15 | loop fusion | flops 8223768 | bytes 21930048 | tf_op jit(solution)/shard_map/add | solution.py:49
  47.7 5.5 %fusion.1 = f32[42,42,514]{2,1,0:T(8,128)S(1)} fusion(f32[42,42,518]{2,1,0:T(8,128)S(1)} %fusion.5), kind=kLoop, calls=%fused_computation.6 | loop fusion | flops 8160264 | bytes 21760704 | tf_op jit(solution)/shard_map/add | solution.py:49
  53.2 6.1 %fusion.18 = f32[40,40,512]{2,1,0:T(8,128)} fusion(f32[42,42,514]{2,1,0:T(8,128)S(1)} %fusion.1), kind=kLoop, calls=%fused_computation.44 | loop fusion | flops 11468800 | bytes 22937600 | tf_op jit(solution)/shard_map/div | solution.py:60
  59.3 1.0 slice.452
  60.3 0.8 reshape.343
  61.1 1.0 slice.449
  62.1 0.8 reshape.340
  63.0 2.3 %pad_maximum_fusion = f32[40,40,512]{2,1,0:T(8,128)S(1)} fusion(f32[40,4,512]{2,1,0:T(4,128)} %reshape.343, f32[40,32,512]{2,1,0:T(8,128)} %copy-done.1, f32[40,4,512]{2,1,0:T(4,128)} %reshape.340), kind=kLoop, calls=%fused_computation.52 | loop fusion | flops 1638400 | bytes 6553600 | tf_op jit(solution)/shard_map/concatenate | solution.py:179
  65.3 4.1 %fusion.61 = (f32[38,38,511]{2,1,0:T(8,128)}, f32[38,38,511]{2,1,0:T(8,128)}) fusion(f32[40,40,512]{2,1,0:T(8,128)S(1)} %pad_maximum_fusion), kind=kLoop, calls=%fused_computation.224 | loop fusion | bytes 11806144 | tf_op jit(solution)/shard_map/slice | solution.py:193
  69.4 1.4 fusion.62
  70.8 0.7 slice.479
  71.6 0.7 slice.478
  72.4 0.4 select_reduce_fusion
  72.9 0.2 copy.43
  73.2 0.9 broadcast_in_dim.149
  74.1 1.3 reshape.347
  75.5 0.1 copy.40
  75.6 0.9 broadcast_in_dim.139
  76.5 1.3 reshape.346
  78.0 0.9 select_select_fusion
  78.9 1.6 shift-left_or_fusion
  80.6 10.0 %fusion.29 = f32[38,38,512]{2,1,0:T(8,128)S(1)} fusion(f32[40,40,512]{2,1,0:T(8,128)S(1)} %select_select_fusion, f32[40,40,512]{2,1,0:T(8,128)S(1)} %copy-done, f32[38,38,511]{2,1,0:T(8,128)} %get-tuple-element.10, f32[38,38,1]{2,1,0:T(8,128)S(1)} %copy-done.4, f32[38,38,1]{2,1,0:T(8,128)S(1)} %copy-done.3, f32[38,38,511]{2,1,0:T(8,128)} %get-tuple-element.9, ...), kind=kLoop, calls=%fused_computation.61 | loop fusion | flops 37705728 | bytes 32530432 | tf_op jit(solution)/shard_map/add | solution.py:204
  90.6 1.5 fusion.63
  92.1 0.3 fusion.64
  92.4 7.6 %fusion.32 = f32[36,36,512]{2,1,0:T(8,128)S(1)} fusion(f32[40,40,512]{2,1,0:T(8,128)S(1)} %select_select_fusion, f32[40,40,512]{2,1,0:T(8,128)S(1)} %copy-done, f32[36,36,511]{2,1,0:T(8,128)S(1)} %get-tuple-element.14, f32[36,36,1]{2,1,0:T(8,128)S(1)} %get-tuple-element.16, f32[36,36,1]{2,1,0:T(8,128)S(1)} %get-tuple-element.15, ...), kind=kLoop, calls=%fused_computation.78 | loop fusion | flops 33841152 | bytes 29196288 | tf_op jit(solution)/shard_map/add | solution.py:204
  100.1 1.4 fusion.65
  101.5 0.3 fusion.66
  101.8 8.0 %fusion.38 = f32[34,34,512]{2,1,0:T(8,128)S(1)} fusion(f32[40,40,512]{2,1,0:T(8,128)S(1)} %select_select_fusion, f32[40,40,512]{2,1,0:T(8,128)S(1)} %copy-done, f32[34,34,511]{2,1,0:T(8,128)S(1)} %get-tuple-element.18, f32[34,34,1]{2,1,0:T(8,128)S(1)} %get-tuple-element.20, f32[34,34,1]{2,1,0:T(8,128)S(1)} %get-tuple-element.19, ...), kind=kLoop, calls=%fused_computation.98 | loop fusion | flops 30185472 | bytes 26042368 | tf_op jit(solution)/shard_map/add | solution.py:204
  109.7 1.0 fusion.67
  110.8 0.3 fusion.68
  111.0 5.4 %fusion.41 = f32[32,32,512]{2,1,0:T(8,128)S(1)} fusion(f32[40,40,512]{2,1,0:T(8,128)S(1)} %select_select_fusion, f32[40,40,512]{2,1,0:T(8,128)S(1)} %copy-done, f32[32,32,511]{2,1,0:T(8,128)S(1)} %get-tuple-element.22, f32[32,32,1]{2,1,0:T(8,128)S(1)} %get-tuple-element.24, f32[32,32,1]{2,1,0:T(8,128)S(1)} %get-tuple-element.23, ...), kind=kLoop, calls=%fused_computation.115 | loop fusion | flops 26738688 | bytes 23068672 | tf_op jit(solution)/shard_map/add | solution.py:204
  116.5 1.8 reshape.348
  118.2 1.8 copy.42
  120.0 2.9 %gather_fusion = f32[32,16,16,128]{3,2,1,0:T(8,128)} fusion(f32[2,16,2,16,4,128]{5,3,4,2,1,0:T(8,128)S(1)} %copy.42, s32[32]{0:T(128)S(1)} %fusion.60), kind=kCustom, calls=%fused_computation | custom fusion | bytes 8388992 | tf_op jit(solution)/shard_map/gather | solution.py:261
  122.9 12.4 %all-to-all-start = ((f32[32,16,16,128]{3,2,1,0:T(8,128)}), f32[32,16,16,128]{3,2,1,0:T(8,128)}, u32[]{:S(2)}, u32[]{:S(2)}) async-start(f32[32,16,16,128]{3,2,1,0:T(8,128)} %gather_fusion), calls=%async_computation | async-start | bytes 8388608 | tf_op jit(solution)/shard_map/all_to_all | solution.py:264
  135.4 94.3 %all-to-all-done = f32[32,16,16,128]{3,2,1,0:T(8,128)} async-done(((f32[32,16,16,128]{3,2,1,0:T(8,128)}), f32[32,16,16,128]{3,2,1,0:T(8,128)}, u32[]{:S(2)}, u32[]{:S(2)}) %all-to-all-start) | async-done | bytes 4194336 | tf_op jit(solution)/shard_map/all_to_all | solution.py:264
  229.7 3.8 %gather_fusion.1 = f32[8,16,16,128]{3,2,1,0:T(8,128)} fusion(f32[32,16,16,128]{3,2,1,0:T(8,128)} %all-to-all-done, s32[1024]{0:T(1024)S(1)} %pad_clamp_fusion), kind=kCustom, calls=%fused_computation.1 | custom fusion | bytes 2097184 | tf_op jit(solution)/shard_map/gather | solution.py:265
  (95 shorter events, 2.3 us)
Async XLA Ops:
  0.0 16.9 %copy-start.12 = (s32[16,6]{0,1:T(8,128)S(1)}, s32[16,6]{0,1:T(8,128)}, u32[]{:S(2)}) copy-start(s32[16,6]{0,1:T(8,128)} %param.11) | copy-start | bytes 1156
  0.0 10.3 %copy-start.5 = (bf16[32,32,512]{2,1,0:T(8,128)(2,1)S(1)}, bf16[32,32,512]{2,1,0:T(8,128)(2,1)}, u32[]{:S(2)}) copy-start(bf16[32,32,512]{2,1,0:T(8,128)(2,1)} %param.7) | copy-start | bytes 3145732
  3.1 25.1 %collective-permute-start.1 = (f32[65592]{0:T(1024)S(1)}, f32[65592]{0:T(1024)S(1)}, u32[]{:S(2)}, u32[]{:S(2)}) collective-permute-start(f32[65592]{0:T(1024)S(1)} %pad_maximum_fusion.4), channel_id=1, source_target_pairs={{32,0},{64,32},{96,64},{128,96},{160,128},{192,160},{224,192},{33,... | collective-permute-start | bytes 787112 | tf_op jit(solution)/shard_map/ppermute | solution.py:169
  8.4 19.8 %collective-permute-start = (f32[65592]{0:T(1024)S(1)}, f32[65592]{0:T(1024)S(1)}, u32[]{:S(2)}, u32[]{:S(2)}) collective-permute-start(f32[65592]{0:T(1024)S(1)} %pad_maximum_fusion.3), channel_id=1, source_target_pairs={{0,32},{32,64},{64,96},{96,128},{128,160},{160,192},{192,224},{1,3... | collective-permute-start | bytes 787112 | tf_op jit(solution)/shard_map/ppermute | solution.py:169
  10.3 9.4 %collective-permute-start.4 = (bf16[7,32,512]{2,1,0:T(8,128)(2,1)S(1)}, bf16[7,32,512]{2,1,0:T(8,128)(2,1)S(1)}, u32[]{:S(2)}, u32[]{:S(2)}) collective-permute-start(bf16[7,32,512]{2,1,0:T(8,128)(2,1)S(1)} %get-tuple-element.32), channel_id=1, source_target_pairs={{0,32},{32,64},{64,96},{96,128},{128,160},{160,192},{192,224},{1,3... | collective-permute-start | bytes 688136 | tf_op jit(solution)/shard_map/ppermute | solution.py:167
  12.3 7.6 %collective-permute-start.5 = (bf16[7,32,512]{2,1,0:T(8,128)(2,1)S(1)}, bf16[7,32,512]{2,1,0:T(8,128)(2,1)S(1)}, u32[]{:S(2)}, u32[]{:S(2)}) collective-permute-start(bf16[7,32,512]{2,1,0:T(8,128)(2,1)S(1)} %get-tuple-element.31), channel_id=1, source_target_pairs={{32,0},{64,32},{96,64},{128,96},{160,128},{192,160},{224,192},{33,... | collective-permute-start | bytes 688136 | tf_op jit(solution)/shard_map/ppermute | solution.py:167
  19.7 8.8 %copy-start.6 = (f32[2,2,4,1]{3,2,1,0:T(4,128)}, f32[2,2,4,1]{3,2,1,0:T(4,128)S(1)}, u32[]{:S(2)}) copy-start(f32[2,2,4,1]{3,2,1,0:T(4,128)S(1)} %concatenate.126) | copy-start | bytes 196
  19.9 1.2 copy-start.2
  22.1 16.3 %collective-permute-start.7 = (bf16[46,7,512]{2,1,0:T(8,128)(2,1)}, bf16[46,7,512]{2,1,0:T(8,128)(2,1)}, u32[]{:S(2)}, u32[]{:S(2)}) collective-permute-start(bf16[46,7,512]{2,1,0:T(8,128)(2,1)} %get-tuple-element.30), channel_id=1, source_target_pairs={{1,0},{2,1},{3,2},{4,3},{5,4},{6,5},{7,6},{8,7},{9,8},{10,9},{11,1... | collective-permute-start | bytes 989192 | tf_op jit(solution)/shard_map/ppermute | solution.py:167
  23.4 15.0 %collective-permute-start.6 = (bf16[46,7,512]{2,1,0:T(8,128)(2,1)}, bf16[46,7,512]{2,1,0:T(8,128)(2,1)}, u32[]{:S(2)}, u32[]{:S(2)}) collective-permute-start(bf16[46,7,512]{2,1,0:T(8,128)(2,1)} %get-tuple-element.29), channel_id=1, source_target_pairs={{0,1},{1,2},{2,3},{3,4},{4,5},{5,6},{6,7},{7,8},{8,9},{9,10},{10,1... | collective-permute-start | bytes 989192 | tf_op jit(solution)/shard_map/ppermute | solution.py:167
  28.2 0.6 copy-start.8
  28.3 0.6 copy-start.10
  30.9 11.3 %copy-start.1 = (f32[40,32,512]{2,1,0:T(8,128)}, f32[40,32,512]{2,1,0:T(8,128)S(1)}, u32[]{:S(2)}) copy-start(f32[40,32,512]{2,1,0:T(8,128)S(1)} %constant_dynamic-update-slice_fusion) | copy-start | bytes 7864324
  32.1 27.2 %collective-permute-start.3 = (f32[82032]{0:T(1024)}, f32[82032]{0:T(1024)}, u32[]{:S(2)}, u32[]{:S(2)}) collective-permute-start(f32[82032]{0:T(1024)} %pad_maximum_fusion.2), channel_id=1, source_target_pairs={{1,0},{2,1},{3,2},{4,3},{5,4},{6,5},{7,6},{8,7},{9,8},{10,9},{11,1... | collective-permute-start | bytes 984392 | tf_op jit(solution)/shard_map/ppermute | solution.py:169
  33.6 27.5 %collective-permute-start.2 = (f32[82032]{0:T(1024)S(1)}, f32[82032]{0:T(1024)}, u32[]{:S(2)}, u32[]{:S(2)}) collective-permute-start(f32[82032]{0:T(1024)S(1)} %pad_maximum_fusion.1), channel_id=1, source_target_pairs={{0,1},{1,2},{2,3},{3,4},{4,5},{5,6},{6,7},{7,8},{8,9},{9,10},{10,1... | collective-permute-start | bytes 984392 | tf_op jit(solution)/shard_map/ppermute | solution.py:169
  69.4 3.0 %copy-start.7 = (f32[2,2,4,1]{3,2,1,0:T(4,128)S(1)}, f32[2,2,4,1]{3,2,1,0:T(4,128)}, u32[]{:S(2)}) copy-start(f32[2,2,4,1]{3,2,1,0:T(4,128)} %copy-done.6) | copy-start | bytes 196
  69.4 3.0 %copy-start.9 = (f32[1,2,4,7]{3,2,1,0:T(4,128)S(1)}, f32[1,2,4,7]{3,2,1,0:T(4,128)}, u32[]{:S(2)}) copy-start(f32[1,2,4,7]{3,2,1,0:T(4,128)} %copy-done.8) | copy-start | bytes 676
  69.4 3.0 %copy-start.11 = (f32[1,2,4,7]{3,2,1,0:T(4,128)S(1)}, f32[1,2,4,7]{3,2,1,0:T(4,128)}, u32[]{:S(2)}) copy-start(f32[1,2,4,7]{3,2,1,0:T(4,128)} %copy-done.10) | copy-start | bytes 676
  69.4 3.0 %copy-start.21 = (s32[7]{0:T(128)S(1)}, s32[7]{0:T(128)}, u32[]{:S(2)}) copy-start(s32[7]{0:T(128)} %constant.230.clone) | copy-start | bytes 88
  69.4 8.5 %copy-start.18 = (pred[512]{0:T(512)(128)(4,1)S(1)}, pred[512]{0:T(512)(128)(4,1)}, u32[]{:S(2)}) copy-start(pred[512]{0:T(512)(128)(4,1)} %get-tuple-element.49) | copy-start | bytes 1540
  69.4 8.5 %copy-start.19 = (pred[512]{0:T(512)(128)(4,1)S(1)}, pred[512]{0:T(512)(128)(4,1)}, u32[]{:S(2)}) copy-start(pred[512]{0:T(512)(128)(4,1)} %get-tuple-element.50) | copy-start | bytes 1540
  69.4 8.5 %copy-start.20 = (pred[512]{0:T(512)(128)(4,1)S(1)}, pred[512]{0:T(512)(128)(4,1)}, u32[]{:S(2)}) copy-start(pred[512]{0:T(512)(128)(4,1)} %get-tuple-element.55) | copy-start | bytes 1540
  73.1 5.8 %copy-start.13 = (s32[512]{0:T(512)S(1)}, s32[512]{0:T(512)}, u32[]{:S(2)}) copy-start(s32[512]{0:T(512)} %get-tuple-element.53) | copy-start | bytes 6148
  73.1 5.8 %copy-start.14 = (s32[512]{0:T(512)S(1)}, s32[512]{0:T(512)}, u32[]{:S(2)}) copy-start(s32[512]{0:T(512)} %get-tuple-element.54) | copy-start | bytes 6148
  73.1 5.8 %copy-start.15 = (s32[40]{0:T(128)S(1)}, s32[40]{0:T(128)}, u32[]{:S(2)}) copy-start(s32[40]{0:T(128)} %get-tuple-element.51) | copy-start | bytes 484
  73.1 5.8 %copy-start.16 = (s32[40]{0:T(128)S(1)}, s32[40]{0:T(128)}, u32[]{:S(2)}) copy-start(s32[40]{0:T(128)} %get-tuple-element.52) | copy-start | bytes 484
  73.1 5.8 %copy-start.17 = (pred[40]{0:T(512)(128)(4,1)S(1)}, pred[40]{0:T(512)(128)(4,1)}, u32[]{:S(2)}) copy-start(pred[40]{0:T(512)(128)(4,1)} %compare_and_fusion) | copy-start | bytes 124
  73.1 5.8 %copy-start.22 = (pred[512]{0:T(512)(128)(4,1)S(1)}, pred[512]{0:T(512)(128)(4,1)}, u32[]{:S(2)}) copy-start(pred[512]{0:T(512)(128)(4,1)} %get-tuple-element.56) | copy-start | bytes 1540
  77.9 2.6 %copy-start = (f32[40,40,512]{2,1,0:T(8,128)S(1)}, f32[40,40,512]{2,1,0:T(8,128)}, u32[]{:S(2)}) copy-start(f32[40,40,512]{2,1,0:T(8,128)} %fusion.18) | copy-start | bytes 9830404
  77.9 2.6 %copy-start.3 = (f32[38,38,1]{2,1,0:T(8,128)S(1)}, f32[38,38,1]{2,1,0:T(8,128)}, u32[]{:S(2)}) copy-start(f32[38,38,1]{2,1,0:T(8,128)} %get-tuple-element.11) | copy-start | bytes 17332
  78.0 2.6 %copy-start.4 = (f32[38,38,1]{2,1,0:T(8,128)S(1)}, f32[38,38,1]{2,1,0:T(8,128)}, u32[]{:S(2)}) copy-start(f32[38,38,1]{2,1,0:T(8,128)} %get-tuple-element.12) | copy-start | bytes 17332
  122.9 12.5 %copy-start.23 = (s32[8]{0:T(128)S(1)}, s32[8]{0:T(128)}, u32[]{:S(2)}) copy-start(s32[8]{0:T(128)} %param.10) | copy-start | bytes 100
  122.9 106.8 %all-to-all-start = ((f32[32,16,16,128]{3,2,1,0:T(8,128)}), f32[32,16,16,128]{3,2,1,0:T(8,128)}, u32[]{:S(2)}, u32[]{:S(2)}) async-start(f32[32,16,16,128]{3,2,1,0:T(8,128)} %gather_fusion), calls=%async_computation | async-start | bytes 8388608 | tf_op jit(solution)/shard_map/all_to_all | solution.py:264

commit v9 on v8

--- a/solution.py
+++ b/solution.py
@@ -257,10 +257,12 @@
     source_dev = brick_of_band // bricks_here % partners
     matches = (owner_dev[None, :] == jnp.arange(partners)[:, None]) & in_band[None, :]
     chosen = jnp.sum(jnp.where(matches, jnp.arange(bricks_here)[None, :], 0), axis=1)
-    view = lvl.reshape(BXN, BX, BYN, BY, BZN, BZ)
-    sending = view.at[chosen // (BYN * BZN), :, chosen // BZN % BYN, :, chosen % BZN, :].get(
-        mode="promise_in_bounds"
-    )
+    corner_x = chosen // (BYN * BZN) * BX
+    corner_y = chosen // BZN % BYN * BY
+    corner_z = chosen % BZN * BZ
+    sending = jax.vmap(
+        lambda cx, cy, cz: lax.dynamic_slice(lvl, (cx, cy, cz), (BX, BY, BZ))
+    )(corner_x, corner_y, corner_z)
     arrived = lax.all_to_all(sending, "dev", split_axis=0, concat_axis=0, tiled=True)
     return arrived.at[source_dev].get(mode="promise_in_bounds")
 

time: 237 us -> 337 us (1.42)
  local copies, waits for them, and re-layouts: 39.2 us -> 137 us
    gather x1 -> x96, local copies, waits for them, and re-layouts: 2.9 us -> 104 us  [per_device(): view.at[chosen // (BYN * BZN), :, chosen // BZN % BYN, :, chosen % BZN, :]]
    reshape x2 -> x0, local copies, waits for them, and re-layouts: 3.53 us -> none  [per_device(): view = lvl.reshape(BXN, BX, BYN, BY, BZN, BZ)]
  transfers between devices with their start and end apart: 9 -> 9, of which waited for: 1 -> 1; matrix products, arithmetic and copies ran while one was open for 14% -> 10% of each run, Pallas kernels for 0% -> 0%
where the time goes in v9:
time: 337 us; the launch traced here: 333 us
  local copies, waits for them, and re-layouts  137 us (41%)
  waiting for transfers between devices  94.4 us (28%)
  other arithmetic  64.6 us (19%)
  starting transfers between devices  36 us (11%)
    gather x96, local copies, waits for them, and re-layouts  104 us
    all_to_all x1, waiting for transfers between devices, per_device(): lax.all_to_all(sending, 'dev', split_axis=0, concat_axis=0, tiled=True)  94.3 us
    add x4, other arithmetic, region_step(): return centre + time_step * edge * force * jnp.sqrt(1.0 + gradient)  31 us
    ppermute x4, starting transfers between devices, sent(): flat = lax.ppermute(flat, axis, pairs)  13 us
    all_to_all x1, starting transfers between devices, per_device(): lax.all_to_all(sending, 'dev', split_axis=0, concat_axis=0, tiled=True)  12.6 us
    add x3, other arithmetic, smooth_axis(): summed + gauss_taps[offset] * lax.slice_in_dim(values, offset, offset + l...  11 us
    ppermute x4, starting transfers between devices, sent(): image_part = lax.ppermute(pieces[0], axis, pairs)  10.4 us
    slice x4, local copies, waits for them, and re-layouts, region_step(): centre[:, :, 1:]  8.07 us
  transfers between devices with their start and end apart: 9, of which 1 were waited for; matrix products, arithmetic and copies ran while one was open for 10% of the time, Pallas kernels for 0%

profile of v9, /device:TPU:1, one launch (start us, length us, event | category | flops | bytes accessed | tf_op | source)
XLA Modules:
  0.0 333.0 jit_solution(815416286612625968)
XLA Ops:
  3.1 5.1 %collective-permute-start.1 = (f32[65592]{0:T(1024)S(1)}, f32[65592]{0:T(1024)S(1)}, u32[]{:S(2)}, u32[]{:S(2)}) collective-permute-start(f32[65592]{0:T(1024)S(1)} %pad_maximum_fusion.4), channel_id=1, source_target_pairs={{32,0},{64,32},{96,64},{128,96},{160,128},{192,160},{224,192},{33,... | collective-permute-start | bytes 787112 | tf_op jit(solution)/shard_map/ppermute | solution.py:169
  8.4 1.9 collective-permute-start
  10.3 1.9 collective-permute-start.4
  12.3 2.4 collective-permute-start.5
  21.8 1.3 collective-permute-start.7
  23.1 4.7 %collective-permute-start.6 = (bf16[46,7,512]{2,1,0:T(8,128)(2,1)S(1)}, bf16[46,7,512]{2,1,0:T(8,128)(2,1)}, u32[]{:S(2)}, u32[]{:S(2)}) collective-permute-start(bf16[46,7,512]{2,1,0:T(8,128)(2,1)S(1)} %get-tuple-element.48), channel_id=1, source_target_pairs={{0,1},{1,2},{2,3},{3,4},{4,5},{5,6},{6,7},{7,8},{8,9},{9,10},{10,1... | collective-permute-start | bytes 989192 | tf_op jit(solution)/shard_map/ppermute | solution.py:167
  29.5 1.8 constant_dynamic-update-slice_fusion.1
  31.7 1.4 pad_maximum_fusion.2
  33.1 1.3 collective-permute-start.3
  34.7 4.7 %collective-permute-start.2 = (f32[82032]{0:T(1024)S(1)}, f32[82032]{0:T(1024)}, u32[]{:S(2)}, u32[]{:S(2)}) collective-permute-start(f32[82032]{0:T(1024)S(1)} %pad_maximum_fusion.1), channel_id=1, source_target_pairs={{0,1},{1,2},{2,3},{3,4},{4,5},{5,6},{6,7},{7,8},{8,9},{9,10},{10,1... | collective-permute-start | bytes 984392 | tf_op jit(solution)/shard_map/ppermute | solution.py:169
  39.4 3.8 %fusion.35 = f32[46,46,518]{2,1,0:T(8,128)S(1)} fusion(bf16[46,7,512]{2,1,0:T(8,128)(2,1)} %collective-permute-done.7, bf16[46,32,512]{2,1,0:T(8,128)(2,1)} %copy-done.2, bf16[46,7,512]{2,1,0:T(8,128)(2,1)} %collective-permute-done.6), kind=kLoop, calls=%fused_computation.95 | loop fusion | flops 13153056 | bytes 6551136 | tf_op jit(solution)/shard_map/jit(_pad)/pad | solution.py:216
  43.2 2.6 fusion.9
  45.9 2.9 fusion.5
  48.8 5.5 %fusion.1 = f32[42,42,514]{2,1,0:T(8,128)S(1)} fusion(f32[42,42,518]{2,1,0:T(8,128)S(1)} %fusion.5), kind=kLoop, calls=%fused_computation.7 | loop fusion | flops 8160264 | bytes 21760704 | tf_op jit(solution)/shard_map/add | solution.py:49
  54.2 6.1 %fusion.18 = f32[40,40,512]{2,1,0:T(8,128)} fusion(f32[42,42,514]{2,1,0:T(8,128)S(1)} %fusion.1), kind=kLoop, calls=%fused_computation.45 | loop fusion | flops 11468800 | bytes 22937600 | tf_op jit(solution)/shard_map/div | solution.py:60
  64.0 2.4 pad_maximum_fusion
  66.4 4.1 %fusion.55 = (f32[38,38,511]{2,1,0:T(8,128)}, f32[38,38,511]{2,1,0:T(8,128)}) fusion(f32[40,40,512]{2,1,0:T(8,128)S(1)} %pad_maximum_fusion), kind=kLoop, calls=%fused_computation.220 | loop fusion | bytes 11806144 | tf_op jit(solution)/shard_map/slice | solution.py:193
  70.5 1.4 fusion.56
  75.2 1.3 reshape.353
  77.7 1.3 reshape.352
  79.1 1.7 select_select_fusion
  80.9 1.6 shift-left_or_fusion
  82.5 10.0 %fusion.29 = f32[38,38,512]{2,1,0:T(8,128)S(1)} fusion(f32[40,40,512]{2,1,0:T(8,128)S(1)} %select_select_fusion, f32[40,40,512]{2,1,0:T(8,128)S(1)} %copy-done, f32[38,38,511]{2,1,0:T(8,128)} %get-tuple-element.29, f32[38,38,1]{2,1,0:T(8,128)S(1)} %copy-done.4, f32[38,38,1]{2,1,0:T(8,128)S(1)} %copy-done.3, f32[38,38,511]{2,1,0:T(8,128)} %get-tuple-element.28, ...), kind=kLoop, calls=%fused_computation.62 | loop fusion | flops 37705728 | bytes 32530432 | tf_op jit(solution)/shard_map/add | solution.py:204
  92.5 1.5 fusion.57
  94.4 7.6 %fusion.32 = f32[36,36,512]{2,1,0:T(8,128)S(1)} fusion(f32[40,40,512]{2,1,0:T(8,128)S(1)} %select_select_fusion, f32[40,40,512]{2,1,0:T(8,128)S(1)} %copy-done, f32[36,36,511]{2,1,0:T(8,128)S(1)} %get-tuple-element.33, f32[36,36,1]{2,1,0:T(8,128)S(1)} %get-tuple-element.35, f32[36,36,1]{2,1,0:T(8,128)S(1)} %get-tuple-element.34, ...), kind=kLoop, calls=%fused_computation.79 | loop fusion | flops 33841152 | bytes 29196288 | tf_op jit(solution)/shard_map/add | solution.py:204
  102.0 1.4 fusion.59
  103.7 8.0 %fusion.38 = f32[34,34,512]{2,1,0:T(8,128)S(1)} fusion(f32[40,40,512]{2,1,0:T(8,128)S(1)} %select_select_fusion, f32[40,40,512]{2,1,0:T(8,128)S(1)} %copy-done, f32[34,34,511]{2,1,0:T(8,128)S(1)} %get-tuple-element.37, f32[34,34,1]{2,1,0:T(8,128)S(1)} %get-tuple-element.39, f32[34,34,1]{2,1,0:T(8,128)S(1)} %get-tuple-element.38, ...), kind=kLoop, calls=%fused_computation.99 | loop fusion | flops 30185472 | bytes 26042368 | tf_op jit(solution)/shard_map/add | solution.py:204
  113.0 5.4 %fusion.41 = f32[32,32,512]{2,1,0:T(8,128)S(1)} fusion(f32[40,40,512]{2,1,0:T(8,128)S(1)} %select_select_fusion, f32[40,40,512]{2,1,0:T(8,128)S(1)} %copy-done, f32[32,32,511]{2,1,0:T(8,128)S(1)} %get-tuple-element.41, f32[32,32,1]{2,1,0:T(8,128)S(1)} %get-tuple-element.43, f32[32,32,1]{2,1,0:T(8,128)S(1)} %get-tuple-element.42, ...), kind=kLoop, calls=%fused_computation.116 | loop fusion | flops 26738688 | bytes 23068672 | tf_op jit(solution)/shard_map/add | solution.py:204
  118.4 103.8 %while.1 = (s32[]{:T(128)}, f32[32,32,512]{2,1,0:T(8,128)S(1)}, s32[32,3]{0,1:T(4,128)S(1)}, f32[32,16,16,128]{3,2,1,0:T(8,128)}, s32[]{:T(128)}) while((s32[]{:T(128)}, f32[32,32,512]{2,1,0:T(8,128)S(1)}, s32[32,3]{0,1:T(4,128)S(1)}, f32[32,16,16,128]{3,2,1,0:T(8,128)}, s32[]{:T(128)}) %tuple.50), condition=%wide.while_cond, body=%wide.while_body.sunk | while | flops 2 | bytes 263805 | solution.py:264
  119.1 2.6 bitcast_dynamic-update-slice_fusion.2
  122.3 2.6 bitcast_dynamic-update-slice_fusion.2
  125.6 2.6 bitcast_dynamic-update-slice_fusion.2
  128.8 2.6 bitcast_dynamic-update-slice_fusion.2
  132.1 2.6 bitcast_dynamic-update-slice_fusion.2
  135.3 2.6 bitcast_dynamic-update-slice_fusion.2
  138.6 2.6 bitcast_dynamic-update-slice_fusion.2
  141.8 2.6 bitcast_dynamic-update-slice_fusion.2
  145.0 2.6 bitcast_dynamic-update-slice_fusion.2
  148.3 2.6 bitcast_dynamic-update-slice_fusion.2
  151.5 2.6 bitcast_dynamic-update-slice_fusion.2
  154.8 2.6 bitcast_dynamic-update-slice_fusion.2
  158.0 2.6 bitcast_dynamic-update-slice_fusion.2
  161.2 2.6 bitcast_dynamic-update-slice_fusion.2
  164.5 2.6 bitcast_dynamic-update-slice_fusion.2
  167.7 2.6 bitcast_dynamic-update-slice_fusion.2
  171.0 2.6 bitcast_dynamic-update-slice_fusion.2
  174.2 2.6 bitcast_dynamic-update-slice_fusion.2
  177.5 2.6 bitcast_dynamic-update-slice_fusion.2
  180.7 2.6 bitcast_dynamic-update-slice_fusion.2
  183.9 2.6 bitcast_dynamic-update-slice_fusion.2
  187.2 2.6 bitcast_dynamic-update-slice_fusion.2
  190.4 2.6 bitcast_dynamic-update-slice_fusion.2
  193.7 2.6 bitcast_dynamic-update-slice_fusion.2
  196.9 2.6 bitcast_dynamic-update-slice_fusion.2
  200.1 2.6 bitcast_dynamic-update-slice_fusion.2
  203.4 2.6 bitcast_dynamic-update-slice_fusion.2
  206.6 2.6 bitcast_dynamic-update-slice_fusion.2
  209.9 2.6 bitcast_dynamic-update-slice_fusion.2
  213.1 2.6 bitcast_dynamic-update-slice_fusion.2
  216.3 2.6 bitcast_dynamic-update-slice_fusion.2
  219.6 2.6 bitcast_dynamic-update-slice_fusion.2
  222.2 12.6 %all-to-all-start = ((f32[32,16,16,128]{3,2,1,0:T(8,128)}), f32[32,16,16,128]{3,2,1,0:T(8,128)}, u32[]{:S(2)}, u32[]{:S(2)}) async-start(f32[32,16,16,128]{3,2,1,0:T(8,128)} %get-tuple-element.12), calls=%async_computation | async-start | bytes 8388608 | tf_op jit(solution)/shard_map/all_to_all | solution.py:266
  234.9 94.3 %all-to-all-done = f32[32,16,16,128]{3,2,1,0:T(8,128)} async-done(((f32[32,16,16,128]{3,2,1,0:T(8,128)}), f32[32,16,16,128]{3,2,1,0:T(8,128)}, u32[]{:S(2)}, u32[]{:S(2)}) %all-to-all-start) | async-done | bytes 4194336 | tf_op jit(solution)/shard_map/all_to_all | solution.py:266
  329.2 3.8 %gather_fusion = f32[8,16,16,128]{3,2,1,0:T(8,128)} fusion(f32[32,16,16,128]{3,2,1,0:T(8,128)} %all-to-all-done, s32[1024]{0:T(1024)S(1)} %pad_clamp_fusion), kind=kCustom, calls=%fused_computation | custom fusion | bytes 2097184 | tf_op jit(solution)/shard_map/gather | solution.py:267
  (183 shorter events, 43.1 us)
Async XLA Ops:
  0.0 16.4 %copy-start.9 = (s32[16,6]{0,1:T(8,128)S(1)}, s32[16,6]{0,1:T(8,128)}, u32[]{:S(2)}) copy-start(s32[16,6]{0,1:T(8,128)} %param.11) | copy-start | bytes 1156
  0.0 10.3 %copy-start.5 = (bf16[32,32,512]{2,1,0:T(8,128)(2,1)S(1)}, bf16[32,32,512]{2,1,0:T(8,128)(2,1)}, u32[]{:S(2)}) copy-start(bf16[32,32,512]{2,1,0:T(8,128)(2,1)} %param.7) | copy-start | bytes 3145732
  3.1 24.7 %collective-permute-start.1 = (f32[65592]{0:T(1024)S(1)}, f32[65592]{0:T(1024)S(1)}, u32[]{:S(2)}, u32[]{:S(2)}) collective-permute-start(f32[65592]{0:T(1024)S(1)} %pad_maximum_fusion.4), channel_id=1, source_target_pairs={{32,0},{64,32},{96,64},{128,96},{160,128},{192,160},{224,192},{33,... | collective-permute-start | bytes 787112 | tf_op jit(solution)/shard_map/ppermute | solution.py:169
  8.4 19.5 %collective-permute-start = (f32[65592]{0:T(1024)S(1)}, f32[65592]{0:T(1024)S(1)}, u32[]{:S(2)}, u32[]{:S(2)}) collective-permute-start(f32[65592]{0:T(1024)S(1)} %pad_maximum_fusion.3), channel_id=1, source_target_pairs={{0,32},{32,64},{64,96},{96,128},{128,160},{160,192},{192,224},{1,3... | collective-permute-start | bytes 787112 | tf_op jit(solution)/shard_map/ppermute | solution.py:169
  10.3 9.3 %collective-permute-start.4 = (bf16[7,32,512]{2,1,0:T(8,128)(2,1)S(1)}, bf16[7,32,512]{2,1,0:T(8,128)(2,1)S(1)}, u32[]{:S(2)}, u32[]{:S(2)}) collective-permute-start(bf16[7,32,512]{2,1,0:T(8,128)(2,1)S(1)} %get-tuple-element.51), channel_id=1, source_target_pairs={{0,32},{32,64},{64,96},{96,128},{128,160},{160,192},{192,224},{1,3... | collective-permute-start | bytes 688136 | tf_op jit(solution)/shard_map/ppermute | solution.py:167
  12.3 7.5 %collective-permute-start.5 = (bf16[7,32,512]{2,1,0:T(8,128)(2,1)S(1)}, bf16[7,32,512]{2,1,0:T(8,128)(2,1)S(1)}, u32[]{:S(2)}, u32[]{:S(2)}) collective-permute-start(bf16[7,32,512]{2,1,0:T(8,128)(2,1)S(1)} %get-tuple-element.50), channel_id=1, source_target_pairs={{32,0},{64,32},{96,64},{128,96},{160,128},{192,160},{224,192},{33,... | collective-permute-start | bytes 688136 | tf_op jit(solution)/shard_map/ppermute | solution.py:167
  19.8 1.1 copy-start.2
  21.8 17.6 %collective-permute-start.7 = (bf16[46,7,512]{2,1,0:T(8,128)(2,1)}, bf16[46,7,512]{2,1,0:T(8,128)(2,1)}, u32[]{:S(2)}, u32[]{:S(2)}) collective-permute-start(bf16[46,7,512]{2,1,0:T(8,128)(2,1)} %get-tuple-element.49), channel_id=1, source_target_pairs={{1,0},{2,1},{3,2},{4,3},{5,4},{6,5},{7,6},{8,7},{9,8},{10,9},{11,1... | collective-permute-start | bytes 989192 | tf_op jit(solution)/shard_map/ppermute | solution.py:167
  23.1 16.3 %collective-permute-start.6 = (bf16[46,7,512]{2,1,0:T(8,128)(2,1)S(1)}, bf16[46,7,512]{2,1,0:T(8,128)(2,1)}, u32[]{:S(2)}, u32[]{:S(2)}) collective-permute-start(bf16[46,7,512]{2,1,0:T(8,128)(2,1)S(1)} %get-tuple-element.48), channel_id=1, source_target_pairs={{0,1},{1,2},{2,3},{3,4},{4,5},{5,6},{6,7},{7,8},{8,9},{9,10},{10,1... | collective-permute-start | bytes 989192 | tf_op jit(solution)/shard_map/ppermute | solution.py:167
  27.8 1.6 copy-start.6
  29.4 1.9 copy-start.7
  31.4 3.0 copy-start.8
  31.4 11.8 %copy-start.1 = (f32[40,32,512]{2,1,0:T(8,128)}, f32[40,32,512]{2,1,0:T(8,128)S(1)}, u32[]{:S(2)}) copy-start(f32[40,32,512]{2,1,0:T(8,128)S(1)} %constant_dynamic-update-slice_fusion) | copy-start | bytes 7864324
  33.1 27.2 %collective-permute-start.3 = (f32[82032]{0:T(1024)}, f32[82032]{0:T(1024)}, u32[]{:S(2)}, u32[]{:S(2)}) collective-permute-start(f32[82032]{0:T(1024)} %pad_maximum_fusion.2), channel_id=1, source_target_pairs={{1,0},{2,1},{3,2},{4,3},{5,4},{6,5},{7,6},{8,7},{9,8},{10,9},{11,1... | collective-permute-start | bytes 984392 | tf_op jit(solution)/shard_map/ppermute | solution.py:169
  34.7 27.5 %collective-permute-start.2 = (f32[82032]{0:T(1024)S(1)}, f32[82032]{0:T(1024)}, u32[]{:S(2)}, u32[]{:S(2)}) collective-permute-start(f32[82032]{0:T(1024)S(1)} %pad_maximum_fusion.1), channel_id=1, source_target_pairs={{0,1},{1,2},{2,3},{3,4},{4,5},{5,6},{6,7},{7,8},{8,9},{9,10},{10,1... | collective-permute-start | bytes 984392 | tf_op jit(solution)/shard_map/ppermute | solution.py:169
  70.5 3.0 copy-start.17
  74.2 6.6 %copy-start.10 = (s32[512]{0:T(512)S(1)}, s32[512]{0:T(512)}, u32[]{:S(2)}) copy-start(s32[512]{0:T(512)} %get-tuple-element.76) | copy-start | bytes 6148
  74.2 6.6 %copy-start.11 = (s32[40]{0:T(128)S(1)}, s32[40]{0:T(128)}, u32[]{:S(2)}) copy-start(s32[40]{0:T(128)} %get-tuple-element.73) | copy-start | bytes 484
  74.2 6.7 %copy-start.12 = (s32[40]{0:T(128)S(1)}, s32[40]{0:T(128)}, u32[]{:S(2)}) copy-start(s32[40]{0:T(128)} %get-tuple-element.74) | copy-start | bytes 484
  74.2 6.7 %copy-start.13 = (pred[40]{0:T(512)(128)(4,1)S(1)}, pred[40]{0:T(512)(128)(4,1)}, u32[]{:S(2)}) copy-start(pred[40]{0:T(512)(128)(4,1)} %compare_and_fusion) | copy-start | bytes 124
  74.2 6.7 %copy-start.14 = (pred[512]{0:T(512)(128)(4,1)S(1)}, pred[512]{0:T(512)(128)(4,1)}, u32[]{:S(2)}) copy-start(pred[512]{0:T(512)(128)(4,1)} %get-tuple-element.71) | copy-start | bytes 1540
  74.2 6.7 %copy-start.15 = (pred[512]{0:T(512)(128)(4,1)S(1)}, pred[512]{0:T(512)(128)(4,1)}, u32[]{:S(2)}) copy-start(pred[512]{0:T(512)(128)(4,1)} %get-tuple-element.72) | copy-start | bytes 1540
  74.2 6.7 %copy-start.16 = (pred[512]{0:T(512)(128)(4,1)S(1)}, pred[512]{0:T(512)(128)(4,1)}, u32[]{:S(2)}) copy-start(pred[512]{0:T(512)(128)(4,1)} %get-tuple-element.77) | copy-start | bytes 1540
  74.2 6.7 %copy-start.18 = (pred[512]{0:T(512)(128)(4,1)S(1)}, pred[512]{0:T(512)(128)(4,1)}, u32[]{:S(2)}) copy-start(pred[512]{0:T(512)(128)(4,1)} %get-tuple-element.78) | copy-start | bytes 1540
  79.0 3.4 %copy-start = (f32[40,40,512]{2,1,0:T(8,128)S(1)}, f32[40,40,512]{2,1,0:T(8,128)}, u32[]{:S(2)}) copy-start(f32[40,40,512]{2,1,0:T(8,128)} %fusion.18) | copy-start | bytes 9830404
  79.1 3.4 %copy-start.3 = (f32[38,38,1]{2,1,0:T(8,128)S(1)}, f32[38,38,1]{2,1,0:T(8,128)}, u32[]{:S(2)}) copy-start(f32[38,38,1]{2,1,0:T(8,128)} %get-tuple-element.30) | copy-start | bytes 17332
  79.1 3.4 %copy-start.4 = (f32[38,38,1]{2,1,0:T(8,128)S(1)}, f32[38,38,1]{2,1,0:T(8,128)}, u32[]{:S(2)}) copy-start(f32[38,38,1]{2,1,0:T(8,128)} %get-tuple-element.31) | copy-start | bytes 17332
  222.2 12.6 %copy-start.19 = (s32[8]{0:T(128)S(1)}, s32[8]{0:T(128)}, u32[]{:S(2)}) copy-start(s32[8]{0:T(128)} %param.10) | copy-start | bytes 100
  222.2 107.0 %all-to-all-start = ((f32[32,16,16,128]{3,2,1,0:T(8,128)}), f32[32,16,16,128]{3,2,1,0:T(8,128)}, u32[]{:S(2)}, u32[]{:S(2)}) async-start(f32[32,16,16,128]{3,2,1,0:T(8,128)} %get-tuple-element.12), calls=%async_computation | async-start | bytes 8388608 | tf_op jit(solution)/shard_map/all_to_all | solution.py:266

commit v10 on v8

--- a/solution.py
+++ b/solution.py
@@ -183,14 +183,14 @@
 
 
 def region_step(lvl, edge, rate, code):
-    centre = lvl[1:-1, 1:-1]
+    centre = lvl[1:-1, 1:-1, 1:-1]
     shifted = (
-        lvl[:-2, 1:-1],
-        lvl[2:, 1:-1],
-        lvl[1:-1, :-2],
-        lvl[1:-1, 2:],
-        jnp.concatenate([centre[:, :, :1], centre[:, :, :-1]], axis=2),
-        jnp.concatenate([centre[:, :, 1:], centre[:, :, -1:]], axis=2),
+        lvl[:-2, 1:-1, 1:-1],
+        lvl[2:, 1:-1, 1:-1],
+        lvl[1:-1, :-2, 1:-1],
+        lvl[1:-1, 2:, 1:-1],
+        lvl[1:-1, 1:-1, :-2],
+        lvl[1:-1, 1:-1, 2:],
     )
     minus_x, plus_x, minus_y, plus_y, minus_z, plus_z = (
         jnp.where((code >> side) & 1 == 1, value, centre) for side, value in enumerate(shifted)
@@ -201,7 +201,8 @@
     diff_z = (plus_z - minus_z) * 0.5
     gradient = diff_x * diff_x + diff_y * diff_y + diff_z * diff_z
     force = smoothing * laplace + rate
-    return centre + time_step * edge * force * jnp.sqrt(1.0 + gradient)
+    updated = centre + time_step * edge * force * jnp.sqrt(1.0 + gradient)
+    return jnp.pad(updated, ((0, 0), (0, 0), (1, 1)))
 
 
 def per_device(em_image, level_set, speeds, brick_of_band, neighbours, speed_index):
@@ -241,7 +242,7 @@
         pos = place[side // 2] % sizes[side]
         inner = pos != (0 if side % 2 == 0 else sizes[side] - 1)
         code = code | (inner.astype(jnp.int32) << side)
-    lvl = wide_level
+    lvl = jnp.pad(wide_level, ((0, 0), (0, 0), (1, 1)))
     for repeat in range(STEPS):
         lo = repeat + 1
         hi_x = span_x - repeat - 1
@@ -257,6 +258,7 @@
     source_dev = brick_of_band // bricks_here % partners
     matches = (owner_dev[None, :] == jnp.arange(partners)[:, None]) & in_band[None, :]
     chosen = jnp.sum(jnp.where(matches, jnp.arange(bricks_here)[None, :], 0), axis=1)
+    lvl = lvl[:, :, 1:-1]
     view = lvl.reshape(BXN, BX, BYN, BY, BZN, BZ)
     sending = view.at[chosen // (BYN * BZN), :, chosen // BZN % BYN, :, chosen % BZN, :].get(
         mode="promise_in_bounds"

time: 237 us -> 231 us (0.975)
  local copies, waits for them, and re-layouts: 39.2 us -> 33.3 us
    slice x8 -> x0, local copies, waits for them, and re-layouts: 10.3 us -> none  [the longest x4 8 us: region_step(): centre[:, :, 1:]]
    unnamed x58 -> x52, local copies, waits for them, and re-layouts: 4.85 us -> 4.81 us
where the time goes in v10:
time: 231 us; the launch traced here: 228 us
  waiting for transfers between devices  94.3 us (41%)
  other arithmetic  64 us (28%)
  starting transfers between devices  35.9 us (16%)
  local copies, waits for them, and re-layouts  33.3 us (14%)
    all_to_all x1, waiting for transfers between devices, per_device(): lax.all_to_all(sending, 'dev', split_axis=0, concat_axis=0, tiled=True)  94.3 us
    add x4, other arithmetic, region_step(): updated = centre + time_step * edge * force * jnp.sqrt(1.0 + gradient)  31.9 us
    ppermute x4, starting transfers between devices, sent(): flat = lax.ppermute(flat, axis, pairs)  13 us
    all_to_all x1, starting transfers between devices, per_device(): lax.all_to_all(sending, 'dev', split_axis=0, concat_axis=0, tiled=True)  12.5 us
    add x3, other arithmetic, smooth_axis(): summed + gauss_taps[offset] * lax.slice_in_dim(values, offset, offset + l...  11 us
    ppermute x4, starting transfers between devices, sent(): image_part = lax.ppermute(pieces[0], axis, pairs)  10.4 us
    div x1, other arithmetic, edge_map(): 1.0 / (1.0 + (grad_x * grad_x + grad_y * grad_y + grad_z * grad_z) / cont...  5.12 us
    unnamed x52, local copies, waits for them, and re-layouts  4.81 us
  transfers between devices with their start and end apart: 9, of which 1 were waited for; matrix products, arithmetic and copies ran while one was open for 14% of the time, Pallas kernels for 0%

profile of v10, /device:TPU:1, one launch (start us, length us, event | category | flops | bytes accessed | tf_op | source)
XLA Modules:
  0.0 228.2 jit_solution(16482215501195237251)
XLA Ops:
  0.0 0.9 copy.35
  0.9 0.8 select_reduce_fusion.2
  1.9 1.1 fusion.69
  3.1 5.1 %collective-permute-start.1 = (f32[65592]{0:T(1024)S(1)}, f32[65592]{0:T(1024)S(1)}, u32[]{:S(2)}, u32[]{:S(2)}) collective-permute-start(f32[65592]{0:T(1024)S(1)} %pad_maximum_fusion.4), channel_id=1, source_target_pairs={{32,0},{64,32},{96,64},{128,96},{160,128},{192,160},{224,192},{33,... | collective-permute-start | bytes 787112 | tf_op jit(solution)/shard_map/ppermute | solution.py:169
  8.4 1.9 collective-permute-start
  10.3 1.9 collective-permute-start.4
  12.3 2.4 %collective-permute-start.5 = (bf16[7,32,512]{2,1,0:T(8,128)(2,1)S(1)}, bf16[7,32,512]{2,1,0:T(8,128)(2,1)S(1)}, u32[]{:S(2)}, u32[]{:S(2)}) collective-permute-start(bf16[7,32,512]{2,1,0:T(8,128)(2,1)S(1)} %get-tuple-element.15), channel_id=1, source_target_pairs={{32,0},{64,32},{96,64},{128,96},{160,128},{192,160},{224,192},{33,... | collective-permute-start | bytes 688136 | tf_op jit(solution)/shard_map/ppermute | solution.py:167
  14.7 0.6 iota_compare_fusion.4
  15.3 0.6 iota_compare_fusion.6
  15.9 0.6 iota_and_fusion
  16.5 0.5 compare_select_fusion.10
  17.1 0.6 fusion.73
  17.6 1.3 broadcast_compare_fusion
  18.9 0.1 select_reduce_fusion.1
  19.0 0.6 compare_and_fusion
  19.6 0.1 concatenate.94
  19.8 0.1 constant_dynamic-update-slice_fusion.4
  19.9 1.1 copy-done.1
  21.0 1.0 fusion.70
  22.0 1.3 collective-permute-start.7
  23.3 4.8 %collective-permute-start.6 = (bf16[46,7,512]{2,1,0:T(8,128)(2,1)}, bf16[46,7,512]{2,1,0:T(8,128)(2,1)}, u32[]{:S(2)}, u32[]{:S(2)}) collective-permute-start(bf16[46,7,512]{2,1,0:T(8,128)(2,1)} %get-tuple-element.13), channel_id=1, source_target_pairs={{0,1},{1,2},{2,3},{3,4},{4,5},{5,6},{6,7},{7,8},{8,9},{9,10},{10,1... | collective-permute-start | bytes 989192 | tf_op jit(solution)/shard_map/ppermute | solution.py:167
  28.3 0.1 reshape.342
  28.5 0.3 copy-done.5
  28.7 0.1 copy-done.7
  28.9 1.8 constant_dynamic-update-slice_fusion.1
  30.8 0.1 slice_bitcast_fusion.1
  31.1 1.0 pad_maximum_fusion.2
  32.1 1.3 collective-permute-start.3
  33.4 0.1 reshape.339
  33.6 0.7 pad_maximum_fusion.1
  34.3 4.7 %collective-permute-start.2 = (f32[82032]{0:T(1024)}, f32[82032]{0:T(1024)}, u32[]{:S(2)}, u32[]{:S(2)}) collective-permute-start(f32[82032]{0:T(1024)} %pad_maximum_fusion.1), channel_id=1, source_target_pairs={{0,1},{1,2},{2,3},{3,4},{4,5},{5,6},{6,7},{7,8},{8,9},{9,10},{10,1... | collective-permute-start | bytes 984392 | tf_op jit(solution)/shard_map/ppermute | solution.py:169
  39.0 3.8 %fusion.39 = f32[46,46,518]{2,1,0:T(8,128)S(1)} fusion(bf16[46,7,512]{2,1,0:T(8,128)(2,1)} %collective-permute-done.7, bf16[46,32,512]{2,1,0:T(8,128)(2,1)} %copy-done.1, bf16[46,7,512]{2,1,0:T(8,128)(2,1)} %collective-permute-done.6), kind=kLoop, calls=%fused_computation.102 | loop fusion | flops 13153056 | bytes 6551136 | tf_op jit(solution)/shard_map/jit(_pad)/pad | solution.py:217
  42.9 2.6 %fusion.9 = f32[42,46,518]{2,1,0:T(8,128)S(1)} fusion(f32[46,46,518]{2,1,0:T(8,128)S(1)} %fusion.39), kind=kLoop, calls=%fused_computation.24 | loop fusion | flops 9006984 | bytes 24018624 | tf_op jit(solution)/shard_map/add | solution.py:49
  45.5 2.9 %fusion.5 = f32[42,42,518]{2,1,0:T(8,128)S(1)} fusion(f32[42,46,518]{2,1,0:T(8,128)S(1)} %fusion.9), kind=kLoop, calls=%fused_computation.15 | loop fusion | flops 8223768 | bytes 21930048 | tf_op jit(solution)/shard_map/add | solution.py:49
  48.4 5.5 %fusion.1 = f32[42,42,514]{2,1,0:T(8,128)S(1)} fusion(f32[42,42,518]{2,1,0:T(8,128)S(1)} %fusion.5), kind=kLoop, calls=%fused_computation.6 | loop fusion | flops 8160264 | bytes 21760704 | tf_op jit(solution)/shard_map/add | solution.py:49
  53.9 5.1 %fusion.18 = f32[40,40,512]{2,1,0:T(8,128)S(1)} fusion(f32[42,42,514]{2,1,0:T(8,128)S(1)} %fusion.1), kind=kLoop, calls=%fused_computation.52 | loop fusion | flops 11468800 | bytes 22937600 | tf_op jit(solution)/shard_map/div | solution.py:60
  59.1 0.7 slice.452
  59.8 0.1 reshape.345
  59.9 0.7 slice.451
  60.5 0.1 reshape.344
  60.7 0.4 select_reduce_fusion
  61.1 0.2 copy.43
  61.3 0.9 broadcast_in_dim.149
  62.3 1.3 reshape.347
  63.7 1.7 slice.425
  65.4 1.8 reshape.343
  67.2 1.7 slice.422
  68.9 1.8 reshape.340
  70.7 0.1 copy.40
  70.8 0.9 broadcast_in_dim.139
  71.7 1.3 reshape.346
  73.2 2.3 %pad_maximum_fusion = f32[40,40,512]{2,1,0:T(8,128)S(1)} fusion(f32[40,4,512]{2,1,0:T(4,128)} %reshape.343, f32[40,32,512]{2,1,0:T(8,128)} %copy-done, f32[40,4,512]{2,1,0:T(4,128)} %reshape.340), kind=kLoop, calls=%fused_computation.60 | loop fusion | flops 1638400 | bytes 6553600 | tf_op jit(solution)/shard_map/concatenate | solution.py:179
  75.6 0.9 select_select_fusion
  76.6 1.6 shift-left_or_fusion
  78.1 8.9 %fusion.31 = f32[38,38,512]{2,1,0:T(8,128)S(1)} fusion(f32[40,40,512]{2,1,0:T(8,128)S(1)} %select_select_fusion, f32[40,40,512]{2,1,0:T(8,128)S(1)} %fusion.18, f32[40,40,512]{2,1,0:T(8,128)S(1)} %pad_maximum_fusion, s32[40,40,512]{2,1,0:T(8,128)S(1)} %shift-left_or_fusion), kind=kLoop, calls=%fused_computation.71 | loop fusion | flops 36227072 | bytes 31137792 | tf_op jit(solution)/shard_map/add | solution.py:204
  87.1 7.9 %fusion.36 = f32[36,36,512]{2,1,0:T(8,128)S(1)} fusion(f32[40,40,512]{2,1,0:T(8,128)S(1)} %select_select_fusion, f32[40,40,512]{2,1,0:T(8,128)S(1)} %fusion.18, f32[38,38,512]{2,1,0:T(8,128)S(1)} %fusion.31, s32[40,40,512]{2,1,0:T(8,128)S(1)} %shift-left_or_fusion), kind=kLoop, calls=%fused_computation.88 | loop fusion | flops 32514048 | bytes 29360128 | tf_op jit(solution)/shard_map/add | solution.py:204
  95.0 8.0 %fusion.44 = f32[34,34,512]{2,1,0:T(8,128)S(1)} fusion(f32[40,40,512]{2,1,0:T(8,128)S(1)} %select_select_fusion, f32[40,40,512]{2,1,0:T(8,128)S(1)} %fusion.18, f32[36,36,512]{2,1,0:T(8,128)S(1)} %fusion.36, s32[40,40,512]{2,1,0:T(8,128)S(1)} %shift-left_or_fusion), kind=kLoop, calls=%fused_computation.108 | loop fusion | flops 29001728 | bytes 27598848 | tf_op jit(solution)/shard_map/add | solution.py:204
  103.0 7.0 %fusion.49 = f32[32,32,512]{2,1,0:T(8,128)} fusion(f32[40,40,512]{2,1,0:T(8,128)S(1)} %select_select_fusion, f32[40,40,512]{2,1,0:T(8,128)S(1)} %fusion.18, f32[34,34,512]{2,1,0:T(8,128)S(1)} %fusion.44, s32[40,40,512]{2,1,0:T(8,128)S(1)} %shift-left_or_fusion), kind=kLoop, calls=%fused_computation.125 | loop fusion | flops 25690112 | bytes 21659648 | tf_op jit(solution)/shard_map/add | solution.py:204
  110.0 2.9 %reshape.348 = f32[2,16,2,16,4,128]{5,4,3,2,1,0:T(4,128)} reshape(f32[32,32,512]{2,1,0:T(8,128)} %fusion.49) | data formatting | bytes 4194304 | tf_op jit(solution)/shard_map/reshape | solution.py:262
  112.9 1.8 copy.42
  114.7 2.9 %gather_fusion = f32[32,16,16,128]{3,2,1,0:T(8,128)} fusion(f32[2,16,2,16,4,128]{5,3,4,2,1,0:T(8,128)S(1)} %copy.42, s32[32]{0:T(128)S(1)} %fusion.68), kind=kCustom, calls=%fused_computation | custom fusion | bytes 8388992 | tf_op jit(solution)/shard_map/gather | solution.py:263
  117.6 12.5 %all-to-all-start = ((f32[32,16,16,128]{3,2,1,0:T(8,128)}), f32[32,16,16,128]{3,2,1,0:T(8,128)}, u32[]{:S(2)}, u32[]{:S(2)}) async-start(f32[32,16,16,128]{3,2,1,0:T(8,128)} %gather_fusion), calls=%async_computation | async-start | bytes 8388608 | tf_op jit(solution)/shard_map/all_to_all | solution.py:266
  130.1 94.3 %all-to-all-done = f32[32,16,16,128]{3,2,1,0:T(8,128)} async-done(((f32[32,16,16,128]{3,2,1,0:T(8,128)}), f32[32,16,16,128]{3,2,1,0:T(8,128)}, u32[]{:S(2)}, u32[]{:S(2)}) %all-to-all-start) | async-done | bytes 4194336 | tf_op jit(solution)/shard_map/all_to_all | solution.py:266
  224.4 3.8 %gather_fusion.1 = f32[8,16,16,128]{3,2,1,0:T(8,128)} fusion(f32[32,16,16,128]{3,2,1,0:T(8,128)} %all-to-all-done, s32[1024]{0:T(1024)S(1)} %pad_clamp_fusion), kind=kCustom, calls=%fused_computation.1 | custom fusion | bytes 2097184 | tf_op jit(solution)/shard_map/gather | solution.py:267
  (81 shorter events, 1.7 us)
Async XLA Ops:
  0.0 17.0 %copy-start.9 = (s32[16,6]{0,1:T(8,128)S(1)}, s32[16,6]{0,1:T(8,128)}, u32[]{:S(2)}) copy-start(s32[16,6]{0,1:T(8,128)} %param.11) | copy-start | bytes 1156
  0.0 10.3 %copy-start.2 = (bf16[32,32,512]{2,1,0:T(8,128)(2,1)S(1)}, bf16[32,32,512]{2,1,0:T(8,128)(2,1)}, u32[]{:S(2)}) copy-start(bf16[32,32,512]{2,1,0:T(8,128)(2,1)} %param.7) | copy-start | bytes 3145732
  3.1 25.0 %collective-permute-start.1 = (f32[65592]{0:T(1024)S(1)}, f32[65592]{0:T(1024)S(1)}, u32[]{:S(2)}, u32[]{:S(2)}) collective-permute-start(f32[65592]{0:T(1024)S(1)} %pad_maximum_fusion.4), channel_id=1, source_target_pairs={{32,0},{64,32},{96,64},{128,96},{160,128},{192,160},{224,192},{33,... | collective-permute-start | bytes 787112 | tf_op jit(solution)/shard_map/ppermute | solution.py:169
  8.4 19.8 %collective-permute-start = (f32[65592]{0:T(1024)S(1)}, f32[65592]{0:T(1024)S(1)}, u32[]{:S(2)}, u32[]{:S(2)}) collective-permute-start(f32[65592]{0:T(1024)S(1)} %pad_maximum_fusion.3), channel_id=1, source_target_pairs={{0,32},{32,64},{64,96},{96,128},{128,160},{160,192},{192,224},{1,3... | collective-permute-start | bytes 787112 | tf_op jit(solution)/shard_map/ppermute | solution.py:169
  10.3 9.4 %collective-permute-start.4 = (bf16[7,32,512]{2,1,0:T(8,128)(2,1)S(1)}, bf16[7,32,512]{2,1,0:T(8,128)(2,1)S(1)}, u32[]{:S(2)}, u32[]{:S(2)}) collective-permute-start(bf16[7,32,512]{2,1,0:T(8,128)(2,1)S(1)} %get-tuple-element.16), channel_id=1, source_target_pairs={{0,32},{32,64},{64,96},{96,128},{128,160},{160,192},{192,224},{1,3... | collective-permute-start | bytes 688136 | tf_op jit(solution)/shard_map/ppermute | solution.py:167
  12.3 7.6 %collective-permute-start.5 = (bf16[7,32,512]{2,1,0:T(8,128)(2,1)S(1)}, bf16[7,32,512]{2,1,0:T(8,128)(2,1)S(1)}, u32[]{:S(2)}, u32[]{:S(2)}) collective-permute-start(bf16[7,32,512]{2,1,0:T(8,128)(2,1)S(1)} %get-tuple-element.15), channel_id=1, source_target_pairs={{32,0},{64,32},{96,64},{128,96},{160,128},{192,160},{224,192},{33,... | collective-permute-start | bytes 688136 | tf_op jit(solution)/shard_map/ppermute | solution.py:167
  19.7 8.8 %copy-start.3 = (f32[2,2,4,1]{3,2,1,0:T(4,128)}, f32[2,2,4,1]{3,2,1,0:T(4,128)S(1)}, u32[]{:S(2)}) copy-start(f32[2,2,4,1]{3,2,1,0:T(4,128)S(1)} %concatenate.94) | copy-start | bytes 196
  19.9 1.1 copy-start.1
  22.0 17.0 %collective-permute-start.7 = (bf16[46,7,512]{2,1,0:T(8,128)(2,1)}, bf16[46,7,512]{2,1,0:T(8,128)(2,1)}, u32[]{:S(2)}, u32[]{:S(2)}) collective-permute-start(bf16[46,7,512]{2,1,0:T(8,128)(2,1)} %get-tuple-element.14), channel_id=1, source_target_pairs={{1,0},{2,1},{3,2},{4,3},{5,4},{6,5},{7,6},{8,7},{9,8},{10,9},{11,1... | collective-permute-start | bytes 989192 | tf_op jit(solution)/shard_map/ppermute | solution.py:167
  23.3 15.8 %collective-permute-start.6 = (bf16[46,7,512]{2,1,0:T(8,128)(2,1)}, bf16[46,7,512]{2,1,0:T(8,128)(2,1)}, u32[]{:S(2)}, u32[]{:S(2)}) collective-permute-start(bf16[46,7,512]{2,1,0:T(8,128)(2,1)} %get-tuple-element.13), channel_id=1, source_target_pairs={{0,1},{1,2},{2,3},{3,4},{4,5},{5,6},{6,7},{7,8},{8,9},{9,10},{10,1... | collective-permute-start | bytes 989192 | tf_op jit(solution)/shard_map/ppermute | solution.py:167
  28.1 0.6 copy-start.5
  28.2 0.6 copy-start.7
  30.8 12.1 %copy-start = (f32[40,32,512]{2,1,0:T(8,128)}, f32[40,32,512]{2,1,0:T(8,128)S(1)}, u32[]{:S(2)}) copy-start(f32[40,32,512]{2,1,0:T(8,128)S(1)} %constant_dynamic-update-slice_fusion) | copy-start | bytes 7864324
  32.1 27.0 %collective-permute-start.3 = (f32[82032]{0:T(1024)}, f32[82032]{0:T(1024)}, u32[]{:S(2)}, u32[]{:S(2)}) collective-permute-start(f32[82032]{0:T(1024)} %pad_maximum_fusion.2), channel_id=1, source_target_pairs={{1,0},{2,1},{3,2},{4,3},{5,4},{6,5},{7,6},{8,7},{9,8},{10,9},{11,1... | collective-permute-start | bytes 984392 | tf_op jit(solution)/shard_map/ppermute | solution.py:169
  34.3 25.5 %collective-permute-start.2 = (f32[82032]{0:T(1024)}, f32[82032]{0:T(1024)}, u32[]{:S(2)}, u32[]{:S(2)}) collective-permute-start(f32[82032]{0:T(1024)} %pad_maximum_fusion.1), channel_id=1, source_target_pairs={{0,1},{1,2},{2,3},{3,4},{4,5},{5,6},{6,7},{7,8},{8,9},{9,10},{10,1... | collective-permute-start | bytes 984392 | tf_op jit(solution)/shard_map/ppermute | solution.py:169
  53.9 6.7 %copy-start.4 = (f32[2,2,4,1]{3,2,1,0:T(4,128)S(1)}, f32[2,2,4,1]{3,2,1,0:T(4,128)}, u32[]{:S(2)}) copy-start(f32[2,2,4,1]{3,2,1,0:T(4,128)} %copy-done.3) | copy-start | bytes 196
  53.9 6.7 %copy-start.6 = (f32[1,2,4,7]{3,2,1,0:T(4,128)S(1)}, f32[1,2,4,7]{3,2,1,0:T(4,128)}, u32[]{:S(2)}) copy-start(f32[1,2,4,7]{3,2,1,0:T(4,128)} %copy-done.5) | copy-start | bytes 676
  53.9 6.7 %copy-start.8 = (f32[1,2,4,7]{3,2,1,0:T(4,128)S(1)}, f32[1,2,4,7]{3,2,1,0:T(4,128)}, u32[]{:S(2)}) copy-start(f32[1,2,4,7]{3,2,1,0:T(4,128)} %copy-done.7) | copy-start | bytes 676
  53.9 6.7 %copy-start.19 = (s32[7]{0:T(128)S(1)}, s32[7]{0:T(128)}, u32[]{:S(2)}) copy-start(s32[7]{0:T(128)} %constant.230.clone) | copy-start | bytes 88
  73.1 2.4 %copy-start.15 = (pred[512]{0:T(512)(128)(4,1)S(1)}, pred[512]{0:T(512)(128)(4,1)}, u32[]{:S(2)}) copy-start(pred[512]{0:T(512)(128)(4,1)} %get-tuple-element.33) | copy-start | bytes 1540
  73.1 2.4 %copy-start.16 = (pred[512]{0:T(512)(128)(4,1)S(1)}, pred[512]{0:T(512)(128)(4,1)}, u32[]{:S(2)}) copy-start(pred[512]{0:T(512)(128)(4,1)} %get-tuple-element.34) | copy-start | bytes 1540
  73.2 2.4 %copy-start.17 = (pred[512]{0:T(512)(128)(4,1)S(1)}, pred[512]{0:T(512)(128)(4,1)}, u32[]{:S(2)}) copy-start(pred[512]{0:T(512)(128)(4,1)} %get-tuple-element.39) | copy-start | bytes 1540
  75.5 1.0 copy-start.10
  75.5 1.0 copy-start.11
  75.5 1.0 copy-start.12
  75.5 1.0 copy-start.13
  75.5 1.0 copy-start.14
  75.6 1.0 copy-start.18
  117.6 12.5 %copy-start.20 = (s32[8]{0:T(128)S(1)}, s32[8]{0:T(128)}, u32[]{:S(2)}) copy-start(s32[8]{0:T(128)} %param.10) | copy-start | bytes 100
  117.6 106.8 %all-to-all-start = ((f32[32,16,16,128]{3,2,1,0:T(8,128)}), f32[32,16,16,128]{3,2,1,0:T(8,128)}, u32[]{:S(2)}, u32[]{:S(2)}) async-start(f32[32,16,16,128]{3,2,1,0:T(8,128)} %gather_fusion), calls=%async_computation | async-start | bytes 8388608 | tf_op jit(solution)/shard_map/all_to_all | solution.py:266

commit v11 on v10

--- a/solution.py
+++ b/solution.py
@@ -221,10 +221,14 @@
     weights = jnp.asarray([1 << side for side in range(6)] + [0], jnp.int32)
     brick_code = jnp.sum(jnp.where(wide_info > 0.5, weights, 0), axis=-1)
     def spread(per_brick):
-        table = jnp.broadcast_to(
-            per_brick.reshape(BXN + 2, 1, BYN + 2, 1, BZN), (BXN + 2, BX, BYN + 2, BY, BZN)
-        ).reshape((BXN + 2) * BX, (BYN + 2) * BY, BZN)
-        table = table[lead : lead + span_x, lead : lead + span_y]
+        xe = lax.broadcasted_iota(jnp.int32, (span_x, BYN + 2, BZN), 0) + lead
+        along_x = per_brick[BXN + 1][None]
+        for bx in range(BXN, -1, -1):
+            along_x = jnp.where(xe < (bx + 1) * BX, per_brick[bx][None], along_x)
+        ye = lax.broadcasted_iota(jnp.int32, (span_x, span_y, BZN), 1) + lead
+        table = along_x[:, BYN + 1][:, None]
+        for by in range(BYN, -1, -1):
+            table = jnp.where(ye < (by + 1) * BY, along_x[:, by][:, None], table)
         zi = lax.broadcasted_iota(jnp.int32, wide_level.shape, 2)
         value = table[:, :, BZN - 1][..., None]
         for bz in range(BZN - 2, -1, -1):

time: 231 us -> 228 us (0.987)
  local copies, waits for them, and re-layouts: 33.3 us -> 28.6 us
    reshape x2 -> x0, local copies, waits for them, and re-layouts: 2.59 us -> none  [spread(): table = jnp.broadcast_to(per_brick.reshape(BXN + 2, 1, BYN + 2, 1, BZN),...]
    unnamed x52 -> x58, local copies, waits for them, and re-layouts: 4.81 us -> 4.82 us
  transfers between devices with their start and end apart: 9 -> 9, of which waited for: 1 -> 1; matrix products, arithmetic and copies ran while one was open for 14% -> 15% of each run, Pallas kernels for 0% -> 0%
where the time goes in v11:
time: 228 us; the launch traced here: 224 us
  waiting for transfers between devices  92.9 us (41%)
  other arithmetic  65.7 us (29%)
  starting transfers between devices  35.7 us (16%)
  local copies, waits for them, and re-layouts  28.6 us (13%)
    all_to_all x1, waiting for transfers between devices, per_device(): lax.all_to_all(sending, 'dev', split_axis=0, concat_axis=0, tiled=True)  92.8 us
    add x4, other arithmetic, region_step(): updated = centre + time_step * edge * force * jnp.sqrt(1.0 + gradient)  31.8 us
    ppermute x4, starting transfers between devices, sent(): flat = lax.ppermute(flat, axis, pairs)  13 us
    all_to_all x1, starting transfers between devices, per_device(): lax.all_to_all(sending, 'dev', split_axis=0, concat_axis=0, tiled=True)  12.3 us
    add x3, other arithmetic, smooth_axis(): summed + gauss_taps[offset] * lax.slice_in_dim(values, offset, offset + l...  11 us
    ppermute x4, starting transfers between devices, sent(): image_part = lax.ppermute(pieces[0], axis, pairs)  10.3 us
    div x1, other arithmetic, edge_map(): 1.0 / (1.0 + (grad_x * grad_x + grad_y * grad_y + grad_z * grad_z) / cont...  5.12 us
    unnamed x58, local copies, waits for them, and re-layouts  4.82 us
  transfers between devices with their start and end apart: 9, of which 1 were waited for; matrix products, arithmetic and copies ran while one was open for 15% of the time, Pallas kernels for 0%

profile of v11, /device:TPU:1, one launch (start us, length us, event | category | flops | bytes accessed | tf_op | source)
XLA Modules:
  0.0 223.6 jit_solution(2764000310800742233)
XLA Ops:
  0.0 0.9 copy.24
  0.9 0.8 select_reduce_fusion.2
  1.9 1.1 fusion.72
  3.1 5.1 %collective-permute-start.1 = (f32[65592]{0:T(1024)S(1)}, f32[65592]{0:T(1024)S(1)}, u32[]{:S(2)}, u32[]{:S(2)}) collective-permute-start(f32[65592]{0:T(1024)S(1)} %pad_maximum_fusion.4), channel_id=1, source_target_pairs={{32,0},{64,32},{96,64},{128,96},{160,128},{192,160},{224,192},{33,... | collective-permute-start | bytes 787112 | tf_op jit(solution)/shard_map/ppermute | solution.py:169
  8.4 1.9 collective-permute-start
  10.3 1.9 collective-permute-start.4
  12.3 2.4 %collective-permute-start.5 = (bf16[7,32,512]{2,1,0:T(8,128)(2,1)S(1)}, bf16[7,32,512]{2,1,0:T(8,128)(2,1)S(1)}, u32[]{:S(2)}, u32[]{:S(2)}) collective-permute-start(bf16[7,32,512]{2,1,0:T(8,128)(2,1)S(1)} %get-tuple-element.19), channel_id=1, source_target_pairs={{32,0},{64,32},{96,64},{128,96},{160,128},{192,160},{224,192},{33,... | collective-permute-start | bytes 688136 | tf_op jit(solution)/shard_map/ppermute | solution.py:167
  14.7 0.6 fusion.69
  15.3 0.5 fusion.71
  15.8 0.5 iota_compare_fusion.4
  16.3 0.6 iota_compare_fusion.6
  16.9 0.6 iota_and_fusion
  17.5 0.6 compare_select_fusion.10
  18.1 0.6 fusion.76
  18.8 1.4 broadcast_compare_fusion
  20.2 0.1 select_reduce_fusion.1
  20.3 0.6 compare_and_fusion
  20.9 0.1 concatenate.94
  21.0 0.1 constant_dynamic-update-slice_fusion.4
  21.2 1.1 copy-done.1
  22.3 1.0 fusion.73
  23.3 1.3 collective-permute-start.7
  24.6 4.7 %collective-permute-start.6 = (bf16[46,7,512]{2,1,0:T(8,128)(2,1)}, bf16[46,7,512]{2,1,0:T(8,128)(2,1)}, u32[]{:S(2)}, u32[]{:S(2)}) collective-permute-start(bf16[46,7,512]{2,1,0:T(8,128)(2,1)} %get-tuple-element.17), channel_id=1, source_target_pairs={{0,1},{1,2},{2,3},{3,4},{4,5},{5,6},{6,7},{7,8},{8,9},{9,10},{10,1... | collective-permute-start | bytes 989192 | tf_op jit(solution)/shard_map/ppermute | solution.py:167
  29.3 0.1 reshape.337
  29.6 0.1 reshape.341
  29.7 0.3 copy-done.5
  30.0 0.1 copy-done.7
  30.1 1.8 constant_dynamic-update-slice_fusion.1
  32.1 0.1 slice_bitcast_fusion.1
  32.3 1.0 pad_maximum_fusion.2
  33.3 1.3 collective-permute-start.3
  34.6 0.1 reshape.338
  34.8 0.8 pad_maximum_fusion.1
  35.6 4.7 %collective-permute-start.2 = (f32[82032]{0:T(1024)}, f32[82032]{0:T(1024)}, u32[]{:S(2)}, u32[]{:S(2)}) collective-permute-start(f32[82032]{0:T(1024)} %pad_maximum_fusion.1), channel_id=1, source_target_pairs={{0,1},{1,2},{2,3},{3,4},{4,5},{5,6},{6,7},{7,8},{8,9},{9,10},{10,1... | collective-permute-start | bytes 984392 | tf_op jit(solution)/shard_map/ppermute | solution.py:169
  40.3 3.8 %fusion.39 = f32[46,46,518]{2,1,0:T(8,128)S(1)} fusion(bf16[46,7,512]{2,1,0:T(8,128)(2,1)} %collective-permute-done.7, bf16[46,32,512]{2,1,0:T(8,128)(2,1)} %copy-done.1, bf16[46,7,512]{2,1,0:T(8,128)(2,1)} %collective-permute-done.6), kind=kLoop, calls=%fused_computation.102 | loop fusion | flops 13153056 | bytes 6551136 | tf_op jit(solution)/shard_map/jit(_pad)/pad | solution.py:217
  44.1 2.6 %fusion.9 = f32[42,46,518]{2,1,0:T(8,128)S(1)} fusion(f32[46,46,518]{2,1,0:T(8,128)S(1)} %fusion.39), kind=kLoop, calls=%fused_computation.24 | loop fusion | flops 9006984 | bytes 24018624 | tf_op jit(solution)/shard_map/add | solution.py:49
  46.7 2.9 %fusion.5 = f32[42,42,518]{2,1,0:T(8,128)S(1)} fusion(f32[42,46,518]{2,1,0:T(8,128)S(1)} %fusion.9), kind=kLoop, calls=%fused_computation.15 | loop fusion | flops 8223768 | bytes 21930048 | tf_op jit(solution)/shard_map/add | solution.py:49
  49.6 5.5 %fusion.1 = f32[42,42,514]{2,1,0:T(8,128)S(1)} fusion(f32[42,42,518]{2,1,0:T(8,128)S(1)} %fusion.5), kind=kLoop, calls=%fused_computation.6 | loop fusion | flops 8160264 | bytes 21760704 | tf_op jit(solution)/shard_map/add | solution.py:49
  55.2 5.1 %fusion.18 = f32[40,40,512]{2,1,0:T(8,128)S(1)} fusion(f32[42,42,514]{2,1,0:T(8,128)S(1)} %fusion.1), kind=kLoop, calls=%fused_computation.52 | loop fusion | flops 11468800 | bytes 22937600 | tf_op jit(solution)/shard_map/div | solution.py:60
  60.3 0.7 slice.511
  61.0 0.1 reshape.344
  61.1 0.7 slice.510
  61.8 0.1 reshape.343
  61.9 0.4 select_reduce_fusion
  62.3 0.2 slice_reduce_fusion.3
  62.6 0.2 select_select_fusion.1
  62.8 1.7 slice.484
  64.5 1.8 reshape.342
  66.3 1.7 slice.481
  68.0 1.8 reshape.339
  69.9 0.2 select_select_fusion.2
  70.1 2.3 %pad_maximum_fusion = f32[40,40,512]{2,1,0:T(8,128)S(1)} fusion(f32[40,4,512]{2,1,0:T(4,128)} %reshape.342, f32[40,32,512]{2,1,0:T(8,128)} %copy-done, f32[40,4,512]{2,1,0:T(4,128)} %reshape.339), kind=kLoop, calls=%fused_computation.60 | loop fusion | flops 1638400 | bytes 6553600 | tf_op jit(solution)/shard_map/concatenate | solution.py:179
  72.6 0.9 select_select_fusion
  73.5 1.6 shift-left_or_fusion
  75.1 8.9 %fusion.31 = f32[38,38,512]{2,1,0:T(8,128)S(1)} fusion(f32[40,40,512]{2,1,0:T(8,128)S(1)} %select_select_fusion, f32[40,40,512]{2,1,0:T(8,128)S(1)} %fusion.18, f32[40,40,512]{2,1,0:T(8,128)S(1)} %pad_maximum_fusion, s32[40,40,512]{2,1,0:T(8,128)S(1)} %shift-left_or_fusion), kind=kLoop, calls=%fused_computation.71 | loop fusion | flops 36227072 | bytes 31137792 | tf_op jit(solution)/shard_map/add | solution.py:204
  84.0 7.9 %fusion.36 = f32[36,36,512]{2,1,0:T(8,128)S(1)} fusion(f32[40,40,512]{2,1,0:T(8,128)S(1)} %select_select_fusion, f32[40,40,512]{2,1,0:T(8,128)S(1)} %fusion.18, f32[38,38,512]{2,1,0:T(8,128)S(1)} %fusion.31, s32[40,40,512]{2,1,0:T(8,128)S(1)} %shift-left_or_fusion), kind=kLoop, calls=%fused_computation.88 | loop fusion | flops 32514048 | bytes 29360128 | tf_op jit(solution)/shard_map/add | solution.py:204
  92.0 8.0 %fusion.44 = f32[34,34,512]{2,1,0:T(8,128)S(1)} fusion(f32[40,40,512]{2,1,0:T(8,128)S(1)} %select_select_fusion, f32[40,40,512]{2,1,0:T(8,128)S(1)} %fusion.18, f32[36,36,512]{2,1,0:T(8,128)S(1)} %fusion.36, s32[40,40,512]{2,1,0:T(8,128)S(1)} %shift-left_or_fusion), kind=kLoop, calls=%fused_computation.108 | loop fusion | flops 29001728 | bytes 27598848 | tf_op jit(solution)/shard_map/add | solution.py:204
  100.0 7.0 %fusion.49 = f32[32,32,512]{2,1,0:T(8,128)} fusion(f32[40,40,512]{2,1,0:T(8,128)S(1)} %select_select_fusion, f32[40,40,512]{2,1,0:T(8,128)S(1)} %fusion.18, f32[34,34,512]{2,1,0:T(8,128)S(1)} %fusion.44, s32[40,40,512]{2,1,0:T(8,128)S(1)} %shift-left_or_fusion), kind=kLoop, calls=%fused_computation.125 | loop fusion | flops 25690112 | bytes 21659648 | tf_op jit(solution)/shard_map/add | solution.py:204
  107.0 2.9 %reshape.345 = f32[2,16,2,16,4,128]{5,4,3,2,1,0:T(4,128)} reshape(f32[32,32,512]{2,1,0:T(8,128)} %fusion.49) | data formatting | bytes 4194304 | tf_op jit(solution)/shard_map/reshape | solution.py:266
  109.9 1.8 copy.29
  111.7 2.9 %gather_fusion = f32[32,16,16,128]{3,2,1,0:T(8,128)} fusion(f32[2,16,2,16,4,128]{5,3,4,2,1,0:T(8,128)S(1)} %copy.29, s32[32]{0:T(128)S(1)} %fusion.68), kind=kCustom, calls=%fused_computation | custom fusion | bytes 8388992 | tf_op jit(solution)/shard_map/gather | solution.py:267
  114.6 12.3 %all-to-all-start = ((f32[32,16,16,128]{3,2,1,0:T(8,128)}), f32[32,16,16,128]{3,2,1,0:T(8,128)}, u32[]{:S(2)}, u32[]{:S(2)}) async-start(f32[32,16,16,128]{3,2,1,0:T(8,128)} %gather_fusion), calls=%async_computation | async-start | bytes 8388608 | tf_op jit(solution)/shard_map/all_to_all | solution.py:270
  126.9 92.8 %all-to-all-done = f32[32,16,16,128]{3,2,1,0:T(8,128)} async-done(((f32[32,16,16,128]{3,2,1,0:T(8,128)}), f32[32,16,16,128]{3,2,1,0:T(8,128)}, u32[]{:S(2)}, u32[]{:S(2)}) %all-to-all-start) | async-done | bytes 4194336 | tf_op jit(solution)/shard_map/all_to_all | solution.py:270
  219.8 3.8 %gather_fusion.1 = f32[8,16,16,128]{3,2,1,0:T(8,128)} fusion(f32[32,16,16,128]{3,2,1,0:T(8,128)} %all-to-all-done, s32[1024]{0:T(1024)S(1)} %pad_clamp_fusion), kind=kCustom, calls=%fused_computation.1 | custom fusion | bytes 2097184 | tf_op jit(solution)/shard_map/gather | solution.py:271
  (90 shorter events, 1.5 us)
Async XLA Ops:
  0.0 18.1 %copy-start.9 = (s32[16,6]{0,1:T(8,128)S(1)}, s32[16,6]{0,1:T(8,128)}, u32[]{:S(2)}) copy-start(s32[16,6]{0,1:T(8,128)} %param.11) | copy-start | bytes 1156
  0.0 10.3 %copy-start.2 = (bf16[32,32,512]{2,1,0:T(8,128)(2,1)S(1)}, bf16[32,32,512]{2,1,0:T(8,128)(2,1)}, u32[]{:S(2)}) copy-start(bf16[32,32,512]{2,1,0:T(8,128)(2,1)} %param.7) | copy-start | bytes 3145732
  3.1 26.2 %collective-permute-start.1 = (f32[65592]{0:T(1024)S(1)}, f32[65592]{0:T(1024)S(1)}, u32[]{:S(2)}, u32[]{:S(2)}) collective-permute-start(f32[65592]{0:T(1024)S(1)} %pad_maximum_fusion.4), channel_id=1, source_target_pairs={{32,0},{64,32},{96,64},{128,96},{160,128},{192,160},{224,192},{33,... | collective-permute-start | bytes 787112 | tf_op jit(solution)/shard_map/ppermute | solution.py:169
  8.4 21.0 %collective-permute-start = (f32[65592]{0:T(1024)S(1)}, f32[65592]{0:T(1024)S(1)}, u32[]{:S(2)}, u32[]{:S(2)}) collective-permute-start(f32[65592]{0:T(1024)S(1)} %pad_maximum_fusion.3), channel_id=1, source_target_pairs={{0,32},{32,64},{64,96},{96,128},{128,160},{160,192},{192,224},{1,3... | collective-permute-start | bytes 787112 | tf_op jit(solution)/shard_map/ppermute | solution.py:169
  10.3 10.7 %collective-permute-start.4 = (bf16[7,32,512]{2,1,0:T(8,128)(2,1)S(1)}, bf16[7,32,512]{2,1,0:T(8,128)(2,1)S(1)}, u32[]{:S(2)}, u32[]{:S(2)}) collective-permute-start(bf16[7,32,512]{2,1,0:T(8,128)(2,1)S(1)} %get-tuple-element.20), channel_id=1, source_target_pairs={{0,32},{32,64},{64,96},{96,128},{128,160},{160,192},{192,224},{1,3... | collective-permute-start | bytes 688136 | tf_op jit(solution)/shard_map/ppermute | solution.py:167
  12.3 8.9 %collective-permute-start.5 = (bf16[7,32,512]{2,1,0:T(8,128)(2,1)S(1)}, bf16[7,32,512]{2,1,0:T(8,128)(2,1)S(1)}, u32[]{:S(2)}, u32[]{:S(2)}) collective-permute-start(bf16[7,32,512]{2,1,0:T(8,128)(2,1)S(1)} %get-tuple-element.19), channel_id=1, source_target_pairs={{32,0},{64,32},{96,64},{128,96},{160,128},{192,160},{224,192},{33,... | collective-permute-start | bytes 688136 | tf_op jit(solution)/shard_map/ppermute | solution.py:167
  21.0 8.7 %copy-start.3 = (f32[2,2,4,1]{3,2,1,0:T(4,128)}, f32[2,2,4,1]{3,2,1,0:T(4,128)S(1)}, u32[]{:S(2)}) copy-start(f32[2,2,4,1]{3,2,1,0:T(4,128)S(1)} %concatenate.94) | copy-start | bytes 196
  21.2 1.1 copy-start.1
  23.3 17.0 %collective-permute-start.7 = (bf16[46,7,512]{2,1,0:T(8,128)(2,1)}, bf16[46,7,512]{2,1,0:T(8,128)(2,1)}, u32[]{:S(2)}, u32[]{:S(2)}) collective-permute-start(bf16[46,7,512]{2,1,0:T(8,128)(2,1)} %get-tuple-element.18), channel_id=1, source_target_pairs={{1,0},{2,1},{3,2},{4,3},{5,4},{6,5},{7,6},{8,7},{9,8},{10,9},{11,1... | collective-permute-start | bytes 989192 | tf_op jit(solution)/shard_map/ppermute | solution.py:167
  24.6 15.7 %collective-permute-start.6 = (bf16[46,7,512]{2,1,0:T(8,128)(2,1)}, bf16[46,7,512]{2,1,0:T(8,128)(2,1)}, u32[]{:S(2)}, u32[]{:S(2)}) collective-permute-start(bf16[46,7,512]{2,1,0:T(8,128)(2,1)} %get-tuple-element.17), channel_id=1, source_target_pairs={{0,1},{1,2},{2,3},{3,4},{4,5},{5,6},{6,7},{7,8},{8,9},{9,10},{10,1... | collective-permute-start | bytes 989192 | tf_op jit(solution)/shard_map/ppermute | solution.py:167
  29.4 0.6 copy-start.5
  29.5 0.6 copy-start.7
  32.1 12.0 %copy-start = (f32[40,32,512]{2,1,0:T(8,128)}, f32[40,32,512]{2,1,0:T(8,128)S(1)}, u32[]{:S(2)}) copy-start(f32[40,32,512]{2,1,0:T(8,128)S(1)} %constant_dynamic-update-slice_fusion) | copy-start | bytes 7864324
  33.3 27.0 %collective-permute-start.3 = (f32[82032]{0:T(1024)}, f32[82032]{0:T(1024)}, u32[]{:S(2)}, u32[]{:S(2)}) collective-permute-start(f32[82032]{0:T(1024)} %pad_maximum_fusion.2), channel_id=1, source_target_pairs={{1,0},{2,1},{3,2},{4,3},{5,4},{6,5},{7,6},{8,7},{9,8},{10,9},{11,1... | collective-permute-start | bytes 984392 | tf_op jit(solution)/shard_map/ppermute | solution.py:169
  35.6 25.5 %collective-permute-start.2 = (f32[82032]{0:T(1024)}, f32[82032]{0:T(1024)}, u32[]{:S(2)}, u32[]{:S(2)}) collective-permute-start(f32[82032]{0:T(1024)} %pad_maximum_fusion.1), channel_id=1, source_target_pairs={{0,1},{1,2},{2,3},{3,4},{4,5},{5,6},{6,7},{7,8},{8,9},{9,10},{10,1... | collective-permute-start | bytes 984392 | tf_op jit(solution)/shard_map/ppermute | solution.py:169
  55.1 6.8 %copy-start.4 = (f32[2,2,4,1]{3,2,1,0:T(4,128)S(1)}, f32[2,2,4,1]{3,2,1,0:T(4,128)}, u32[]{:S(2)}) copy-start(f32[2,2,4,1]{3,2,1,0:T(4,128)} %copy-done.3) | copy-start | bytes 196
  55.1 6.8 %copy-start.6 = (f32[1,2,4,7]{3,2,1,0:T(4,128)S(1)}, f32[1,2,4,7]{3,2,1,0:T(4,128)}, u32[]{:S(2)}) copy-start(f32[1,2,4,7]{3,2,1,0:T(4,128)} %copy-done.5) | copy-start | bytes 676
  55.1 6.8 %copy-start.8 = (f32[1,2,4,7]{3,2,1,0:T(4,128)S(1)}, f32[1,2,4,7]{3,2,1,0:T(4,128)}, u32[]{:S(2)}) copy-start(f32[1,2,4,7]{3,2,1,0:T(4,128)} %copy-done.7) | copy-start | bytes 676
  55.1 6.8 %copy-start.22 = (s32[7]{0:T(128)S(1)}, s32[7]{0:T(128)}, u32[]{:S(2)}) copy-start(s32[7]{0:T(128)} %constant.239.clone) | copy-start | bytes 88
  55.1 7.3 %copy-start.10 = (pred[40]{0:T(512)(128)(4,1)S(1)}, pred[40]{0:T(512)(128)(4,1)}, u32[]{:S(2)}) copy-start(pred[40]{0:T(512)(128)(4,1)} %get-tuple-element.49) | copy-start | bytes 124
  55.2 7.3 %copy-start.11 = (pred[40]{0:T(512)(128)(4,1)S(1)}, pred[40]{0:T(512)(128)(4,1)}, u32[]{:S(2)}) copy-start(pred[40]{0:T(512)(128)(4,1)} %get-tuple-element.50) | copy-start | bytes 124
  55.2 7.3 %copy-start.12 = (pred[40]{0:T(512)(128)(4,1)S(1)}, pred[40]{0:T(512)(128)(4,1)}, u32[]{:S(2)}) copy-start(pred[40]{0:T(512)(128)(4,1)} %fusion.71) | copy-start | bytes 124
  70.1 2.4 %copy-start.18 = (pred[512]{0:T(512)(128)(4,1)S(1)}, pred[512]{0:T(512)(128)(4,1)}, u32[]{:S(2)}) copy-start(pred[512]{0:T(512)(128)(4,1)} %get-tuple-element.51) | copy-start | bytes 1540
  70.1 2.4 %copy-start.19 = (pred[512]{0:T(512)(128)(4,1)S(1)}, pred[512]{0:T(512)(128)(4,1)}, u32[]{:S(2)}) copy-start(pred[512]{0:T(512)(128)(4,1)} %get-tuple-element.52) | copy-start | bytes 1540
  70.1 2.4 %copy-start.20 = (pred[512]{0:T(512)(128)(4,1)S(1)}, pred[512]{0:T(512)(128)(4,1)}, u32[]{:S(2)}) copy-start(pred[512]{0:T(512)(128)(4,1)} %get-tuple-element.57) | copy-start | bytes 1540
  72.5 1.0 copy-start.13
  72.5 1.0 copy-start.14
  72.5 1.0 copy-start.15
  72.5 1.0 copy-start.16
  72.5 1.0 copy-start.17
  72.5 1.0 copy-start.21
  114.6 12.3 %copy-start.23 = (s32[8]{0:T(128)S(1)}, s32[8]{0:T(128)}, u32[]{:S(2)}) copy-start(s32[8]{0:T(128)} %param.10) | copy-start | bytes 100
  114.6 105.2 %all-to-all-start = ((f32[32,16,16,128]{3,2,1,0:T(8,128)}), f32[32,16,16,128]{3,2,1,0:T(8,128)}, u32[]{:S(2)}, u32[]{:S(2)}) async-start(f32[32,16,16,128]{3,2,1,0:T(8,128)} %gather_fusion), calls=%async_computation | async-start | bytes 8388608 | tf_op jit(solution)/shard_map/all_to_all | solution.py:270

commit v12 on v11

--- a/solution.py
+++ b/solution.py
@@ -201,7 +201,7 @@
     diff_z = (plus_z - minus_z) * 0.5
     gradient = diff_x * diff_x + diff_y * diff_y + diff_z * diff_z
     force = smoothing * laplace + rate
-    updated = centre + time_step * edge * force * jnp.sqrt(1.0 + gradient)
+    updated = centre + edge * force * jnp.sqrt(1.0 + gradient)
     return jnp.pad(updated, ((0, 0), (0, 0), (1, 1)))
 
 
@@ -215,7 +215,7 @@
     ).reshape(BXN, BYN, BZN, 7)
     margin, wide_level, wide_info = extended_packed(em_image, level_set, info)
     window = jnp.pad(margin.astype(jnp.float32), ((0, 0), (0, 0), (3, 3)))
-    edge = edge_map(window)
+    edge = time_step * edge_map(window)
     span_x, span_y, span_z = wide_level.shape
     lead = BX - STEPS
     weights = jnp.asarray([1 << side for side in range(6)] + [0], jnp.int32)

time: 228 us -> 228 us (level)
    div x1 -> x0, other arithmetic: 5.12 us -> none  [edge_map(): 1.0 / (1.0 + (grad_x * grad_x + grad_y * grad_y + grad_z * grad_z) / cont...]
    mul x0 -> x1, other arithmetic: none -> 5.1 us  [per_device(): edge = time_step * edge_map(window)]
where the time goes in v12:
time: 228 us; the launch traced here: 223 us
  waiting for transfers between devices  92.9 us (41%)
  other arithmetic  65.3 us (29%)
  starting transfers between devices  35.7 us (16%)
  local copies, waits for them, and re-layouts  28.6 us (13%)
    all_to_all x1, waiting for transfers between devices, per_device(): lax.all_to_all(sending, 'dev', split_axis=0, concat_axis=0, tiled=True)  92.9 us
    add x4, other arithmetic, region_step(): updated = centre + edge * force * jnp.sqrt(1.0 + gradient)  31.5 us
    ppermute x4, starting transfers between devices, sent(): flat = lax.ppermute(flat, axis, pairs)  13 us
    all_to_all x1, starting transfers between devices, per_device(): lax.all_to_all(sending, 'dev', split_axis=0, concat_axis=0, tiled=True)  12.3 us
    add x3, other arithmetic, smooth_axis(): summed + gauss_taps[offset] * lax.slice_in_dim(values, offset, offset + l...  11 us
    ppermute x4, starting transfers between devices, sent(): image_part = lax.ppermute(pieces[0], axis, pairs)  10.3 us
    mul x1, other arithmetic, per_device(): edge = time_step * edge_map(window)  5.1 us
    unnamed x58, local copies, waits for them, and re-layouts  4.82 us
  transfers between devices with their start and end apart: 9, of which 1 were waited for; matrix products, arithmetic and copies ran while one was open for 15% of the time, Pallas kernels for 0%

profile of v12, /device:TPU:1, one launch (start us, length us, event | category | flops | bytes accessed | tf_op | source)
XLA Modules:
  0.0 223.3 jit_solution(6398617095041488730)
XLA Ops:
  0.0 0.9 copy.24
  0.9 0.8 select_reduce_fusion.2
  1.9 1.1 fusion.73
  3.1 5.1 %collective-permute-start.1 = (f32[65592]{0:T(1024)S(1)}, f32[65592]{0:T(1024)S(1)}, u32[]{:S(2)}, u32[]{:S(2)}) collective-permute-start(f32[65592]{0:T(1024)S(1)} %pad_maximum_fusion.4), channel_id=1, source_target_pairs={{32,0},{64,32},{96,64},{128,96},{160,128},{192,160},{224,192},{33,... | collective-permute-start | bytes 787112 | tf_op jit(solution)/shard_map/ppermute | solution.py:169
  8.4 1.9 collective-permute-start
  10.3 1.9 collective-permute-start.4
  12.3 2.4 %collective-permute-start.5 = (bf16[7,32,512]{2,1,0:T(8,128)(2,1)S(1)}, bf16[7,32,512]{2,1,0:T(8,128)(2,1)S(1)}, u32[]{:S(2)}, u32[]{:S(2)}) collective-permute-start(bf16[7,32,512]{2,1,0:T(8,128)(2,1)S(1)} %get-tuple-element.19), channel_id=1, source_target_pairs={{32,0},{64,32},{96,64},{128,96},{160,128},{192,160},{224,192},{33,... | collective-permute-start | bytes 688136 | tf_op jit(solution)/shard_map/ppermute | solution.py:167
  14.7 0.6 fusion.70
  15.3 0.5 fusion.72
  15.8 0.5 iota_compare_fusion.4
  16.3 0.6 iota_compare_fusion.6
  16.9 0.6 iota_and_fusion
  17.5 0.6 compare_select_fusion.10
  18.1 0.6 fusion.77
  18.8 1.4 broadcast_compare_fusion
  20.2 0.1 select_reduce_fusion.1
  20.3 0.6 compare_and_fusion
  20.9 0.1 concatenate.94
  21.0 0.1 constant_dynamic-update-slice_fusion.4
  21.2 1.1 copy-done.1
  22.3 1.0 fusion.74
  23.3 1.3 collective-permute-start.7
  24.6 4.7 %collective-permute-start.6 = (bf16[46,7,512]{2,1,0:T(8,128)(2,1)}, bf16[46,7,512]{2,1,0:T(8,128)(2,1)}, u32[]{:S(2)}, u32[]{:S(2)}) collective-permute-start(bf16[46,7,512]{2,1,0:T(8,128)(2,1)} %get-tuple-element.17), channel_id=1, source_target_pairs={{0,1},{1,2},{2,3},{3,4},{4,5},{5,6},{6,7},{7,8},{8,9},{9,10},{10,1... | collective-permute-start | bytes 989192 | tf_op jit(solution)/shard_map/ppermute | solution.py:167
  29.3 0.1 reshape.337
  29.6 0.1 reshape.341
  29.7 0.3 copy-done.5
  30.0 0.1 copy-done.7
  30.1 1.8 constant_dynamic-update-slice_fusion.1
  32.1 0.1 slice_bitcast_fusion.1
  32.3 1.0 pad_maximum_fusion.2
  33.3 1.3 collective-permute-start.3
  34.6 0.1 reshape.338
  34.8 0.8 pad_maximum_fusion.1
  35.6 4.7 %collective-permute-start.2 = (f32[82032]{0:T(1024)}, f32[82032]{0:T(1024)}, u32[]{:S(2)}, u32[]{:S(2)}) collective-permute-start(f32[82032]{0:T(1024)} %pad_maximum_fusion.1), channel_id=1, source_target_pairs={{0,1},{1,2},{2,3},{3,4},{4,5},{5,6},{6,7},{7,8},{8,9},{9,10},{10,1... | collective-permute-start | bytes 984392 | tf_op jit(solution)/shard_map/ppermute | solution.py:169
  40.3 3.8 %fusion.40 = f32[46,46,518]{2,1,0:T(8,128)S(1)} fusion(bf16[46,7,512]{2,1,0:T(8,128)(2,1)} %collective-permute-done.7, bf16[46,32,512]{2,1,0:T(8,128)(2,1)} %copy-done.1, bf16[46,7,512]{2,1,0:T(8,128)(2,1)} %collective-permute-done.6), kind=kLoop, calls=%fused_computation.101 | loop fusion | flops 13153056 | bytes 6551136 | tf_op jit(solution)/shard_map/jit(_pad)/pad | solution.py:217
  44.1 2.6 %fusion.9 = f32[42,46,518]{2,1,0:T(8,128)S(1)} fusion(f32[46,46,518]{2,1,0:T(8,128)S(1)} %fusion.40), kind=kLoop, calls=%fused_computation.24 | loop fusion | flops 9006984 | bytes 24018624 | tf_op jit(solution)/shard_map/add | solution.py:49
  46.7 2.9 %fusion.5 = f32[42,42,518]{2,1,0:T(8,128)S(1)} fusion(f32[42,46,518]{2,1,0:T(8,128)S(1)} %fusion.9), kind=kLoop, calls=%fused_computation.15 | loop fusion | flops 8223768 | bytes 21930048 | tf_op jit(solution)/shard_map/add | solution.py:49
  49.6 5.5 %fusion.1 = f32[42,42,514]{2,1,0:T(8,128)S(1)} fusion(f32[42,42,518]{2,1,0:T(8,128)S(1)} %fusion.5), kind=kLoop, calls=%fused_computation.6 | loop fusion | flops 8160264 | bytes 21760704 | tf_op jit(solution)/shard_map/add | solution.py:49
  55.2 5.1 %fusion.24 = f32[40,40,512]{2,1,0:T(8,128)S(1)} fusion(f32[42,42,514]{2,1,0:T(8,128)S(1)} %fusion.1), kind=kLoop, calls=%fused_computation.63 | loop fusion | flops 12288000 | bytes 22937600 | tf_op jit(solution)/shard_map/mul | solution.py:218
  60.3 0.7 slice.511
  61.0 0.1 reshape.344
  61.1 0.7 slice.510
  61.8 0.1 reshape.343
  61.9 0.4 select_reduce_fusion
  62.3 0.2 slice_reduce_fusion.3
  62.6 0.2 select_select_fusion.1
  62.8 1.7 slice.484
  64.5 1.8 reshape.342
  66.3 1.7 slice.481
  68.0 1.8 reshape.339
  69.9 0.2 select_select_fusion.2
  70.1 2.3 %pad_maximum_fusion = f32[40,40,512]{2,1,0:T(8,128)S(1)} fusion(f32[40,4,512]{2,1,0:T(4,128)} %reshape.342, f32[40,32,512]{2,1,0:T(8,128)} %copy-done, f32[40,4,512]{2,1,0:T(4,128)} %reshape.339), kind=kLoop, calls=%fused_computation.60 | loop fusion | flops 1638400 | bytes 6553600 | tf_op jit(solution)/shard_map/concatenate | solution.py:179
  72.6 0.9 select_select_fusion
  73.5 1.6 shift-left_or_fusion
  75.1 8.9 %fusion.32 = f32[38,38,512]{2,1,0:T(8,128)S(1)} fusion(f32[40,40,512]{2,1,0:T(8,128)S(1)} %select_select_fusion, f32[40,40,512]{2,1,0:T(8,128)S(1)} %fusion.24, f32[40,40,512]{2,1,0:T(8,128)S(1)} %pad_maximum_fusion, s32[40,40,512]{2,1,0:T(8,128)S(1)} %shift-left_or_fusion), kind=kLoop, calls=%fused_computation.72 | loop fusion | flops 35487744 | bytes 31137792 | tf_op jit(solution)/shard_map/add | solution.py:204
  84.0 7.9 %fusion.37 = f32[36,36,512]{2,1,0:T(8,128)S(1)} fusion(f32[40,40,512]{2,1,0:T(8,128)S(1)} %select_select_fusion, f32[40,40,512]{2,1,0:T(8,128)S(1)} %fusion.24, f32[38,38,512]{2,1,0:T(8,128)S(1)} %fusion.32, s32[40,40,512]{2,1,0:T(8,128)S(1)} %shift-left_or_fusion), kind=kLoop, calls=%fused_computation.88 | loop fusion | flops 31850496 | bytes 29360128 | tf_op jit(solution)/shard_map/add | solution.py:204
  91.8 7.9 %fusion.45 = f32[34,34,512]{2,1,0:T(8,128)S(1)} fusion(f32[40,40,512]{2,1,0:T(8,128)S(1)} %select_select_fusion, f32[40,40,512]{2,1,0:T(8,128)S(1)} %fusion.24, f32[36,36,512]{2,1,0:T(8,128)S(1)} %fusion.37, s32[40,40,512]{2,1,0:T(8,128)S(1)} %shift-left_or_fusion), kind=kLoop, calls=%fused_computation.107 | loop fusion | flops 28409856 | bytes 27598848 | tf_op jit(solution)/shard_map/add | solution.py:204
  99.7 6.9 %fusion.50 = f32[32,32,512]{2,1,0:T(8,128)} fusion(f32[40,40,512]{2,1,0:T(8,128)S(1)} %select_select_fusion, f32[40,40,512]{2,1,0:T(8,128)S(1)} %fusion.24, f32[34,34,512]{2,1,0:T(8,128)S(1)} %fusion.45, s32[40,40,512]{2,1,0:T(8,128)S(1)} %shift-left_or_fusion), kind=kLoop, calls=%fused_computation.123 | loop fusion | flops 25165824 | bytes 21659648 | tf_op jit(solution)/shard_map/add | solution.py:204
  106.7 2.9 %reshape.345 = f32[2,16,2,16,4,128]{5,4,3,2,1,0:T(4,128)} reshape(f32[32,32,512]{2,1,0:T(8,128)} %fusion.50) | data formatting | bytes 4194304 | tf_op jit(solution)/shard_map/reshape | solution.py:266
  109.6 1.8 copy.29
  111.4 2.9 %gather_fusion = f32[32,16,16,128]{3,2,1,0:T(8,128)} fusion(f32[2,16,2,16,4,128]{5,3,4,2,1,0:T(8,128)S(1)} %copy.29, s32[32]{0:T(128)S(1)} %fusion.69), kind=kCustom, calls=%fused_computation | custom fusion | bytes 8388992 | tf_op jit(solution)/shard_map/gather | solution.py:267
  114.3 12.3 %all-to-all-start = ((f32[32,16,16,128]{3,2,1,0:T(8,128)}), f32[32,16,16,128]{3,2,1,0:T(8,128)}, u32[]{:S(2)}, u32[]{:S(2)}) async-start(f32[32,16,16,128]{3,2,1,0:T(8,128)} %gather_fusion), calls=%async_computation | async-start | bytes 8388608 | tf_op jit(solution)/shard_map/all_to_all | solution.py:270
  126.6 92.9 %all-to-all-done = f32[32,16,16,128]{3,2,1,0:T(8,128)} async-done(((f32[32,16,16,128]{3,2,1,0:T(8,128)}), f32[32,16,16,128]{3,2,1,0:T(8,128)}, u32[]{:S(2)}, u32[]{:S(2)}) %all-to-all-start) | async-done | bytes 4194336 | tf_op jit(solution)/shard_map/all_to_all | solution.py:270
  219.5 3.8 %gather_fusion.1 = f32[8,16,16,128]{3,2,1,0:T(8,128)} fusion(f32[32,16,16,128]{3,2,1,0:T(8,128)} %all-to-all-done, s32[1024]{0:T(1024)S(1)} %pad_clamp_fusion), kind=kCustom, calls=%fused_computation.1 | custom fusion | bytes 2097184 | tf_op jit(solution)/shard_map/gather | solution.py:271
  (90 shorter events, 1.5 us)
Async XLA Ops:
  0.0 18.1 %copy-start.9 = (s32[16,6]{0,1:T(8,128)S(1)}, s32[16,6]{0,1:T(8,128)}, u32[]{:S(2)}) copy-start(s32[16,6]{0,1:T(8,128)} %param.11) | copy-start | bytes 1156
  0.0 10.3 %copy-start.2 = (bf16[32,32,512]{2,1,0:T(8,128)(2,1)S(1)}, bf16[32,32,512]{2,1,0:T(8,128)(2,1)}, u32[]{:S(2)}) copy-start(bf16[32,32,512]{2,1,0:T(8,128)(2,1)} %param.7) | copy-start | bytes 3145732
  3.1 26.2 %collective-permute-start.1 = (f32[65592]{0:T(1024)S(1)}, f32[65592]{0:T(1024)S(1)}, u32[]{:S(2)}, u32[]{:S(2)}) collective-permute-start(f32[65592]{0:T(1024)S(1)} %pad_maximum_fusion.4), channel_id=1, source_target_pairs={{32,0},{64,32},{96,64},{128,96},{160,128},{192,160},{224,192},{33,... | collective-permute-start | bytes 787112 | tf_op jit(solution)/shard_map/ppermute | solution.py:169
  8.4 21.0 %collective-permute-start = (f32[65592]{0:T(1024)S(1)}, f32[65592]{0:T(1024)S(1)}, u32[]{:S(2)}, u32[]{:S(2)}) collective-permute-start(f32[65592]{0:T(1024)S(1)} %pad_maximum_fusion.3), channel_id=1, source_target_pairs={{0,32},{32,64},{64,96},{96,128},{128,160},{160,192},{192,224},{1,3... | collective-permute-start | bytes 787112 | tf_op jit(solution)/shard_map/ppermute | solution.py:169
  10.3 10.7 %collective-permute-start.4 = (bf16[7,32,512]{2,1,0:T(8,128)(2,1)S(1)}, bf16[7,32,512]{2,1,0:T(8,128)(2,1)S(1)}, u32[]{:S(2)}, u32[]{:S(2)}) collective-permute-start(bf16[7,32,512]{2,1,0:T(8,128)(2,1)S(1)} %get-tuple-element.20), channel_id=1, source_target_pairs={{0,32},{32,64},{64,96},{96,128},{128,160},{160,192},{192,224},{1,3... | collective-permute-start | bytes 688136 | tf_op jit(solution)/shard_map/ppermute | solution.py:167
  12.3 8.9 %collective-permute-start.5 = (bf16[7,32,512]{2,1,0:T(8,128)(2,1)S(1)}, bf16[7,32,512]{2,1,0:T(8,128)(2,1)S(1)}, u32[]{:S(2)}, u32[]{:S(2)}) collective-permute-start(bf16[7,32,512]{2,1,0:T(8,128)(2,1)S(1)} %get-tuple-element.19), channel_id=1, source_target_pairs={{32,0},{64,32},{96,64},{128,96},{160,128},{192,160},{224,192},{33,... | collective-permute-start | bytes 688136 | tf_op jit(solution)/shard_map/ppermute | solution.py:167
  21.0 8.7 %copy-start.3 = (f32[2,2,4,1]{3,2,1,0:T(4,128)}, f32[2,2,4,1]{3,2,1,0:T(4,128)S(1)}, u32[]{:S(2)}) copy-start(f32[2,2,4,1]{3,2,1,0:T(4,128)S(1)} %concatenate.94) | copy-start | bytes 196
  21.2 1.1 copy-start.1
  23.3 17.0 %collective-permute-start.7 = (bf16[46,7,512]{2,1,0:T(8,128)(2,1)}, bf16[46,7,512]{2,1,0:T(8,128)(2,1)}, u32[]{:S(2)}, u32[]{:S(2)}) collective-permute-start(bf16[46,7,512]{2,1,0:T(8,128)(2,1)} %get-tuple-element.18), channel_id=1, source_target_pairs={{1,0},{2,1},{3,2},{4,3},{5,4},{6,5},{7,6},{8,7},{9,8},{10,9},{11,1... | collective-permute-start | bytes 989192 | tf_op jit(solution)/shard_map/ppermute | solution.py:167
  24.6 15.7 %collective-permute-start.6 = (bf16[46,7,512]{2,1,0:T(8,128)(2,1)}, bf16[46,7,512]{2,1,0:T(8,128)(2,1)}, u32[]{:S(2)}, u32[]{:S(2)}) collective-permute-start(bf16[46,7,512]{2,1,0:T(8,128)(2,1)} %get-tuple-element.17), channel_id=1, source_target_pairs={{0,1},{1,2},{2,3},{3,4},{4,5},{5,6},{6,7},{7,8},{8,9},{9,10},{10,1... | collective-permute-start | bytes 989192 | tf_op jit(solution)/shard_map/ppermute | solution.py:167
  29.4 0.6 copy-start.5
  29.5 0.6 copy-start.7
  32.1 12.0 %copy-start = (f32[40,32,512]{2,1,0:T(8,128)}, f32[40,32,512]{2,1,0:T(8,128)S(1)}, u32[]{:S(2)}) copy-start(f32[40,32,512]{2,1,0:T(8,128)S(1)} %constant_dynamic-update-slice_fusion) | copy-start | bytes 7864324
  33.3 27.0 %collective-permute-start.3 = (f32[82032]{0:T(1024)}, f32[82032]{0:T(1024)}, u32[]{:S(2)}, u32[]{:S(2)}) collective-permute-start(f32[82032]{0:T(1024)} %pad_maximum_fusion.2), channel_id=1, source_target_pairs={{1,0},{2,1},{3,2},{4,3},{5,4},{6,5},{7,6},{8,7},{9,8},{10,9},{11,1... | collective-permute-start | bytes 984392 | tf_op jit(solution)/shard_map/ppermute | solution.py:169
  35.6 25.5 %collective-permute-start.2 = (f32[82032]{0:T(1024)}, f32[82032]{0:T(1024)}, u32[]{:S(2)}, u32[]{:S(2)}) collective-permute-start(f32[82032]{0:T(1024)} %pad_maximum_fusion.1), channel_id=1, source_target_pairs={{0,1},{1,2},{2,3},{3,4},{4,5},{5,6},{6,7},{7,8},{8,9},{9,10},{10,1... | collective-permute-start | bytes 984392 | tf_op jit(solution)/shard_map/ppermute | solution.py:169
  55.1 6.8 %copy-start.4 = (f32[2,2,4,1]{3,2,1,0:T(4,128)S(1)}, f32[2,2,4,1]{3,2,1,0:T(4,128)}, u32[]{:S(2)}) copy-start(f32[2,2,4,1]{3,2,1,0:T(4,128)} %copy-done.3) | copy-start | bytes 196
  55.1 6.8 %copy-start.6 = (f32[1,2,4,7]{3,2,1,0:T(4,128)S(1)}, f32[1,2,4,7]{3,2,1,0:T(4,128)}, u32[]{:S(2)}) copy-start(f32[1,2,4,7]{3,2,1,0:T(4,128)} %copy-done.5) | copy-start | bytes 676
  55.1 6.8 %copy-start.8 = (f32[1,2,4,7]{3,2,1,0:T(4,128)S(1)}, f32[1,2,4,7]{3,2,1,0:T(4,128)}, u32[]{:S(2)}) copy-start(f32[1,2,4,7]{3,2,1,0:T(4,128)} %copy-done.7) | copy-start | bytes 676
  55.1 6.8 %copy-start.22 = (s32[7]{0:T(128)S(1)}, s32[7]{0:T(128)}, u32[]{:S(2)}) copy-start(s32[7]{0:T(128)} %constant.236.clone) | copy-start | bytes 88
  55.1 7.3 %copy-start.10 = (pred[40]{0:T(512)(128)(4,1)S(1)}, pred[40]{0:T(512)(128)(4,1)}, u32[]{:S(2)}) copy-start(pred[40]{0:T(512)(128)(4,1)} %get-tuple-element.49) | copy-start | bytes 124
  55.2 7.3 %copy-start.11 = (pred[40]{0:T(512)(128)(4,1)S(1)}, pred[40]{0:T(512)(128)(4,1)}, u32[]{:S(2)}) copy-start(pred[40]{0:T(512)(128)(4,1)} %get-tuple-element.50) | copy-start | bytes 124
  55.2 7.3 %copy-start.12 = (pred[40]{0:T(512)(128)(4,1)S(1)}, pred[40]{0:T(512)(128)(4,1)}, u32[]{:S(2)}) copy-start(pred[40]{0:T(512)(128)(4,1)} %fusion.72) | copy-start | bytes 124
  70.1 2.4 %copy-start.18 = (pred[512]{0:T(512)(128)(4,1)S(1)}, pred[512]{0:T(512)(128)(4,1)}, u32[]{:S(2)}) copy-start(pred[512]{0:T(512)(128)(4,1)} %get-tuple-element.51) | copy-start | bytes 1540
  70.1 2.4 %copy-start.19 = (pred[512]{0:T(512)(128)(4,1)S(1)}, pred[512]{0:T(512)(128)(4,1)}, u32[]{:S(2)}) copy-start(pred[512]{0:T(512)(128)(4,1)} %get-tuple-element.52) | copy-start | bytes 1540
  70.1 2.4 %copy-start.20 = (pred[512]{0:T(512)(128)(4,1)S(1)}, pred[512]{0:T(512)(128)(4,1)}, u32[]{:S(2)}) copy-start(pred[512]{0:T(512)(128)(4,1)} %get-tuple-element.57) | copy-start | bytes 1540
  72.5 1.0 copy-start.13
  72.5 1.0 copy-start.14
  72.5 1.0 copy-start.15
  72.5 1.0 copy-start.16
  72.5 1.0 copy-start.17
  72.5 1.0 copy-start.21
  114.3 12.3 %copy-start.23 = (s32[8]{0:T(128)S(1)}, s32[8]{0:T(128)}, u32[]{:S(2)}) copy-start(s32[8]{0:T(128)} %param.10) | copy-start | bytes 100
  114.3 105.2 %all-to-all-start = ((f32[32,16,16,128]{3,2,1,0:T(8,128)}), f32[32,16,16,128]{3,2,1,0:T(8,128)}, u32[]{:S(2)}, u32[]{:S(2)}) async-start(f32[32,16,16,128]{3,2,1,0:T(8,128)} %gather_fusion), calls=%async_computation | async-start | bytes 8388608 | tf_op jit(solution)/shard_map/all_to_all | solution.py:270

commit v13 on v12

--- a/solution.py
+++ b/solution.py
@@ -152,7 +152,7 @@
 
 def extended_packed(em_image, level_set, info):
     cells = [em_image, level_set, info]
-    widths = [3 + STEPS, STEPS, 1]
+    widths = [2 + STEPS, STEPS, 1]
     for axis, dim in (("group", 0), ("dev", 1)):
         count = lax.axis_size(axis)
         ends = count - 1
@@ -251,7 +251,7 @@
         lo = repeat + 1
         hi_x = span_x - repeat - 1
         hi_y = span_y - repeat - 1
-        lvl = region_step(lvl, edge[lo:hi_x, lo:hi_y], rate[lo:hi_x, lo:hi_y], code[lo:hi_x, lo:hi_y])
+        lvl = region_step(lvl, edge[lo - 1 : hi_x - 1, lo - 1 : hi_y - 1], rate[lo:hi_x, lo:hi_y], code[lo:hi_x, lo:hi_y])
     band_here = brick_of_band.shape[0]
     lower = jnp.concatenate([neighbours[1:, 4], neighbours[:1, 4]])
     upper = jnp.concatenate([neighbours[-1:, 5], neighbours[:-1, 5]])

time: 228 us -> 222 us (0.974); the launches traced: 223 us -> 220 us
  local copies, waits for them, and re-layouts: 28.6 us -> 23.9 us
  waiting for transfers between devices: 92.9 us -> 95.8 us
    add x4, other arithmetic: 31.5 us -> 38.5 us  [region_step(): updated = centre + edge * force * jnp.sqrt(1.0 + gradient)]
    mul x1 -> x0, other arithmetic: 5.1 us -> none  [per_device(): edge = time_step * edge_map(window)]
    all_to_all x1, waiting for transfers between devices: 92.9 us -> 95.4 us  [per_device(): lax.all_to_all(sending, 'dev', split_axis=0, concat_axis=0, tiled=True)]
    reshape x4, local copies, waits for them, and re-layouts: 3.69 us -> 1.27 us  [sent(): flat[:size].reshape(pieces[1].shape)]
    unnamed x58 -> x40, local copies, waits for them, and re-layouts: 4.82 us -> 4.54 us
  transfers between devices with their start and end apart: 9 -> 9, of which waited for: 1 -> 2; matrix products, arithmetic and copies ran while one was open for 15% -> 11% of each run, Pallas kernels for 0% -> 0%
where the time goes in v13:
time: 222 us; the launch traced here: 220 us
  waiting for transfers between devices  95.8 us (43%)
  other arithmetic  63.3 us (29%)
  starting transfers between devices  36.6 us (16%)
  local copies, waits for them, and re-layouts  23.9 us (11%)
    all_to_all x1, waiting for transfers between devices, per_device(): lax.all_to_all(sending, 'dev', split_axis=0, concat_axis=0, tiled=True)  95.4 us
    add x4, other arithmetic, region_step(): updated = centre + edge * force * jnp.sqrt(1.0 + gradient)  38.5 us
    all_to_all x1, starting transfers between devices, per_device(): lax.all_to_all(sending, 'dev', split_axis=0, concat_axis=0, tiled=True)  12.9 us
    ppermute x4, starting transfers between devices, sent(): flat = lax.ppermute(flat, axis, pairs)  12.6 us
    ppermute x4, starting transfers between devices, sent(): image_part = lax.ppermute(pieces[0], axis, pairs)  11.1 us
    add x3, other arithmetic, smooth_axis(): summed + gauss_taps[offset] * lax.slice_in_dim(values, offset, offset + l...  10.4 us
    unnamed x40, local copies, waits for them, and re-layouts  4.54 us
  transfers between devices with their start and end apart: 9, of which 2 were waited for; matrix products, arithmetic and copies ran while one was open for 11% of the time, Pallas kernels for 0%

profile of v13, /device:TPU:1, one launch (start us, length us, event | category | flops | bytes accessed | tf_op | source)
XLA Modules:
  0.0 220.2 jit_solution(8036502569109075504)
XLA Ops:
  0.0 0.9 copy.24
  0.9 0.8 select_reduce_fusion.2
  1.6 0.1 copy.25
  1.8 0.1 reshape.330
  1.9 1.1 fusion.74
  3.1 4.5 %collective-permute-start = (f32[65592]{0:T(1024)S(1)}, f32[65592]{0:T(1024)S(1)}, u32[]{:S(2)}, u32[]{:S(2)}) collective-permute-start(f32[65592]{0:T(1024)S(1)} %pad_maximum_fusion.3), channel_id=1, source_target_pairs={{0,32},{32,64},{64,96},{96,128},{128,160},{160,192},{192,224},{1,3... | collective-permute-start | bytes 787112 | tf_op jit(solution)/shard_map/ppermute | solution.py:169
  7.6 0.1 reshape.333
  7.7 1.9 collective-permute-start.1
  9.7 3.6 %collective-permute-start.4 = (bf16[6,32,512]{2,1,0:T(8,128)(2,1)S(1)}, bf16[6,32,512]{2,1,0:T(8,128)(2,1)S(1)}, u32[]{:S(2)}, u32[]{:S(2)}) collective-permute-start(bf16[6,32,512]{2,1,0:T(8,128)(2,1)S(1)} %get-tuple-element.22), channel_id=1, source_target_pairs={{0,32},{32,64},{64,96},{96,128},{128,160},{160,192},{192,224},{1,3... | collective-permute-start | bytes 589832 | tf_op jit(solution)/shard_map/ppermute | solution.py:167
  13.4 1.9 collective-permute-start.5
  15.3 0.1 concatenate.94
  15.4 0.6 iota_compare_fusion.4
  16.0 0.6 iota_compare_fusion.6
  16.6 0.6 compare_select_fusion.10
  17.2 0.6 compare_and_fusion
  17.8 0.6 fusion.78
  18.4 1.3 broadcast_compare_fusion
  19.7 0.1 select_reduce_fusion.1
  19.9 0.1 constant_dynamic-update-slice_fusion.4
  20.0 0.4 collective-permute-done.5
  20.4 1.1 copy-done.3
  21.5 0.9 fusion.75
  22.4 4.3 %collective-permute-start.6 = (bf16[44,6,512]{2,1,0:T(8,128)(2,1)}, bf16[44,6,512]{2,1,0:T(8,128)(2,1)}, u32[]{:S(2)}, u32[]{:S(2)}) collective-permute-start(bf16[44,6,512]{2,1,0:T(8,128)(2,1)} %get-tuple-element.19), channel_id=1, source_target_pairs={{0,1},{1,2},{2,3},{3,4},{4,5},{5,6},{6,7},{7,8},{8,9},{9,10},{10,1... | collective-permute-start | bytes 811016 | tf_op jit(solution)/shard_map/ppermute | solution.py:167
  26.7 1.3 collective-permute-start.7
  28.0 0.1 reshape.336
  28.1 0.1 reshape.337
  28.3 0.1 reshape.338
  28.5 1.8 constant_dynamic-update-slice_fusion.1
  30.4 0.1 slice_bitcast_fusion.1
  30.6 0.1 copy.32
  30.7 0.8 pad_maximum_fusion.1
  31.4 4.7 %collective-permute-start.2 = (f32[82032]{0:T(1024)}, f32[82032]{0:T(1024)}, u32[]{:S(2)}, u32[]{:S(2)}) collective-permute-start(f32[82032]{0:T(1024)} %pad_maximum_fusion.1), channel_id=1, source_target_pairs={{0,1},{1,2},{2,3},{3,4},{4,5},{5,6},{6,7},{7,8},{8,9},{9,10},{10,1... | collective-permute-start | bytes 984392 | tf_op jit(solution)/shard_map/ppermute | solution.py:169
  36.2 0.1 reshape.341
  36.3 0.1 copy.33
  36.4 1.5 collective-permute-start.3
  37.9 3.7 %fusion.45 = f32[44,44,518]{2,1,0:T(8,128)S(1)} fusion(bf16[44,6,512]{2,1,0:T(8,128)(2,1)} %collective-permute-done.7, bf16[44,32,512]{2,1,0:T(8,128)(2,1)} %copy-done.3, bf16[44,6,512]{2,1,0:T(8,128)(2,1)} %collective-permute-done.6), kind=kLoop, calls=%fused_computation.117 | loop fusion | flops 12034176 | bytes 5993856 | tf_op jit(solution)/shard_map/jit(_pad)/pad | solution.py:217
  41.6 2.4 %fusion.1 = f32[40,44,518]{2,1,0:T(8,128)S(1)} fusion(f32[44,44,518]{2,1,0:T(8,128)S(1)} %fusion.45), kind=kLoop, calls=%fused_computation.6 | loop fusion | flops 8205120 | bytes 21880320 | tf_op jit(solution)/shard_map/add | solution.py:49
  44.0 2.3 %fusion.9 = f32[40,40,518]{2,1,0:T(8,128)S(1)} fusion(f32[40,44,518]{2,1,0:T(8,128)S(1)} %fusion.1), kind=kLoop, calls=%fused_computation.32 | loop fusion | flops 7459200 | bytes 19891200 | tf_op jit(solution)/shard_map/add | solution.py:49
  46.3 5.7 %fusion.5 = f32[40,40,514]{2,1,0:T(8,128)} fusion(f32[40,40,518]{2,1,0:T(8,128)S(1)} %fusion.9), kind=kLoop, calls=%fused_computation.23 | loop fusion | flops 7401600 | bytes 19737600 | tf_op jit(solution)/shard_map/add | solution.py:49
  52.0 0.7 slice.505
  52.7 0.1 reshape.343
  52.8 0.7 slice.506
  53.5 0.1 reshape.344
  53.6 0.4 select_reduce_fusion
  54.0 0.2 select_select_fusion.2
  54.2 0.2 slice_reduce_fusion.3
  54.5 0.2 select_select_fusion.1
  54.7 1.0 slice.477
  55.7 0.1 reshape.339
  55.8 1.7 slice.480
  57.5 1.1 reshape.342
  58.6 0.5 pad_maximum_fusion
  59.3 0.9 select_select_fusion
  60.2 2.9 %shift-left_or_fusion = s32[40,40,512]{2,1,0:T(8,128)} fusion(s32[512]{0:T(512)S(1)} %get-tuple-element.57, s32[512]{0:T(512)S(1)} %get-tuple-element.58, s32[40]{0:T(128)S(1)} %copy-done.6, s32[40]{0:T(128)S(1)} %copy-done.7, s32[40,40]{1,0:T(8,128)S(1)} %get-tuple-element.24, s32[40,40]{1,0:T(8,128)S(1)} %get-tuple-element.25, ...), kind=kLoop, calls=%fused_computation.48 | loop fusion | flops 24576000 | bytes 3308904 | tf_op jit(solution)/shard_map/or | solution.py:248
  63.2 15.1 %fusion.20 = (f32[38,38,512]{2,1,0:T(8,128)S(1)}, f32[38,38,512]{2,1,0:T(8,128)}) fusion(f32[40,40,512]{2,1,0:T(8,128)S(1)} %select_select_fusion, f32[40,40,512]{2,1,0:T(8,128)S(1)} %pad_maximum_fusion, s32[40,40,512]{2,1,0:T(8,128)} %shift-left_or_fusion, f32[40,40,514]{2,1,0:T(8,128)S(1)} %copy-done), kind=kLoop, calls=%fused_computation.57 | loop fusion | flops 46577664 | bytes 49504256 | tf_op jit(solution)/shard_map/add | solution.py:204
  78.3 9.6 %fusion.37 = f32[36,36,512]{2,1,0:T(8,128)S(1)} fusion(f32[40,40,512]{2,1,0:T(8,128)S(1)} %select_select_fusion, f32[38,38,512]{2,1,0:T(8,128)} %get-tuple-element.12, f32[38,38,512]{2,1,0:T(8,128)S(1)} %get-tuple-element.11, s32[40,40,512]{2,1,0:T(8,128)} %shift-left_or_fusion), kind=kLoop, calls=%fused_computation.88 | loop fusion | flops 31850496 | bytes 28770304 | tf_op jit(solution)/shard_map/add | solution.py:204
  87.9 7.9 %fusion.42 = f32[34,34,512]{2,1,0:T(8,128)S(1)} fusion(f32[40,40,512]{2,1,0:T(8,128)S(1)} %select_select_fusion, f32[38,38,512]{2,1,0:T(8,128)S(1)} %copy-done.2, f32[36,36,512]{2,1,0:T(8,128)S(1)} %fusion.37, s32[40,40,512]{2,1,0:T(8,128)S(1)} %copy-done.1), kind=kLoop, calls=%fused_computation.104 | loop fusion | flops 28409856 | bytes 27598848 | tf_op jit(solution)/shard_map/add | solution.py:204
  95.8 5.9 %fusion.50 = f32[32,32,512]{2,1,0:T(8,128)S(1)} fusion(f32[40,40,512]{2,1,0:T(8,128)S(1)} %select_select_fusion, f32[38,38,512]{2,1,0:T(8,128)S(1)} %copy-done.2, f32[34,34,512]{2,1,0:T(8,128)S(1)} %fusion.42, s32[40,40,512]{2,1,0:T(8,128)S(1)} %copy-done.1), kind=kLoop, calls=%fused_computation.123 | loop fusion | flops 25165824 | bytes 21659648 | tf_op jit(solution)/shard_map/add | solution.py:204
  101.7 1.7 reshape.345
  103.4 1.8 copy.29
  105.2 2.9 %gather_fusion = f32[32,16,16,128]{3,2,1,0:T(8,128)} fusion(f32[2,16,2,16,4,128]{5,3,4,2,1,0:T(8,128)S(1)} %copy.29, s32[32]{0:T(128)S(1)} %fusion.69), kind=kCustom, calls=%fused_computation | custom fusion | bytes 8388992 | tf_op jit(solution)/shard_map/gather | solution.py:267
  108.1 12.9 %all-to-all-start = ((f32[32,16,16,128]{3,2,1,0:T(8,128)}), f32[32,16,16,128]{3,2,1,0:T(8,128)}, u32[]{:S(2)}, u32[]{:S(2)}) async-start(f32[32,16,16,128]{3,2,1,0:T(8,128)} %gather_fusion), calls=%async_computation | async-start | bytes 8388608 | tf_op jit(solution)/shard_map/all_to_all | solution.py:270
  121.0 95.4 %all-to-all-done = f32[32,16,16,128]{3,2,1,0:T(8,128)} async-done(((f32[32,16,16,128]{3,2,1,0:T(8,128)}), f32[32,16,16,128]{3,2,1,0:T(8,128)}, u32[]{:S(2)}, u32[]{:S(2)}) %all-to-all-start) | async-done | bytes 4194336 | tf_op jit(solution)/shard_map/all_to_all | solution.py:270
  216.4 3.8 %gather_fusion.1 = f32[8,16,16,128]{3,2,1,0:T(8,128)} fusion(f32[32,16,16,128]{3,2,1,0:T(8,128)} %all-to-all-done, s32[1024]{0:T(1024)S(1)} %pad_clamp_fusion), kind=kCustom, calls=%fused_computation.1 | custom fusion | bytes 2097184 | tf_op jit(solution)/shard_map/gather | solution.py:271
  (71 shorter events, 1.1 us)
Async XLA Ops:
  0.0 17.8 %copy-start.5 = (s32[16,6]{0,1:T(8,128)S(1)}, s32[16,6]{0,1:T(8,128)}, u32[]{:S(2)}) copy-start(s32[16,6]{0,1:T(8,128)} %param.11) | copy-start | bytes 1156
  0.0 9.7 %copy-start.4 = (bf16[32,32,512]{2,1,0:T(8,128)(2,1)S(1)}, bf16[32,32,512]{2,1,0:T(8,128)(2,1)}, u32[]{:S(2)}) copy-start(bf16[32,32,512]{2,1,0:T(8,128)(2,1)} %param.7) | copy-start | bytes 3145732
  3.1 25.0 %collective-permute-start = (f32[65592]{0:T(1024)S(1)}, f32[65592]{0:T(1024)S(1)}, u32[]{:S(2)}, u32[]{:S(2)}) collective-permute-start(f32[65592]{0:T(1024)S(1)} %pad_maximum_fusion.3), channel_id=1, source_target_pairs={{0,32},{32,64},{64,96},{96,128},{128,160},{160,192},{192,224},{1,3... | collective-permute-start | bytes 787112 | tf_op jit(solution)/shard_map/ppermute | solution.py:169
  7.7 20.4 %collective-permute-start.1 = (f32[65592]{0:T(1024)S(1)}, f32[65592]{0:T(1024)S(1)}, u32[]{:S(2)}, u32[]{:S(2)}) collective-permute-start(f32[65592]{0:T(1024)S(1)} %pad_maximum_fusion.4), channel_id=1, source_target_pairs={{32,0},{64,32},{96,64},{128,96},{160,128},{192,160},{224,192},{33,... | collective-permute-start | bytes 787112 | tf_op jit(solution)/shard_map/ppermute | solution.py:169
  9.7 10.1 %collective-permute-start.4 = (bf16[6,32,512]{2,1,0:T(8,128)(2,1)S(1)}, bf16[6,32,512]{2,1,0:T(8,128)(2,1)S(1)}, u32[]{:S(2)}, u32[]{:S(2)}) collective-permute-start(bf16[6,32,512]{2,1,0:T(8,128)(2,1)S(1)} %get-tuple-element.22), channel_id=1, source_target_pairs={{0,32},{32,64},{64,96},{96,128},{128,160},{160,192},{192,224},{1,3... | collective-permute-start | bytes 589832 | tf_op jit(solution)/shard_map/ppermute | solution.py:167
  13.4 7.0 %collective-permute-start.5 = (bf16[6,32,512]{2,1,0:T(8,128)(2,1)S(1)}, bf16[6,32,512]{2,1,0:T(8,128)(2,1)S(1)}, u32[]{:S(2)}, u32[]{:S(2)}) collective-permute-start(bf16[6,32,512]{2,1,0:T(8,128)(2,1)S(1)} %get-tuple-element.21), channel_id=1, source_target_pairs={{32,0},{64,32},{96,64},{128,96},{160,128},{192,160},{224,192},{33,... | collective-permute-start | bytes 589832 | tf_op jit(solution)/shard_map/ppermute | solution.py:167
  20.4 1.1 copy-start.3
  22.4 15.4 %collective-permute-start.6 = (bf16[44,6,512]{2,1,0:T(8,128)(2,1)}, bf16[44,6,512]{2,1,0:T(8,128)(2,1)}, u32[]{:S(2)}, u32[]{:S(2)}) collective-permute-start(bf16[44,6,512]{2,1,0:T(8,128)(2,1)} %get-tuple-element.19), channel_id=1, source_target_pairs={{0,1},{1,2},{2,3},{3,4},{4,5},{5,6},{6,7},{7,8},{8,9},{9,10},{10,1... | collective-permute-start | bytes 811016 | tf_op jit(solution)/shard_map/ppermute | solution.py:167
  26.7 11.1 %collective-permute-start.7 = (bf16[44,6,512]{2,1,0:T(8,128)(2,1)}, bf16[44,6,512]{2,1,0:T(8,128)(2,1)}, u32[]{:S(2)}, u32[]{:S(2)}) collective-permute-start(bf16[44,6,512]{2,1,0:T(8,128)(2,1)} %get-tuple-element.20), channel_id=1, source_target_pairs={{1,0},{2,1},{3,2},{4,3},{5,4},{6,5},{7,6},{8,7},{9,8},{10,9},{11,1... | collective-permute-start | bytes 811016 | tf_op jit(solution)/shard_map/ppermute | solution.py:167
  31.4 20.5 %collective-permute-start.2 = (f32[82032]{0:T(1024)}, f32[82032]{0:T(1024)}, u32[]{:S(2)}, u32[]{:S(2)}) collective-permute-start(f32[82032]{0:T(1024)} %pad_maximum_fusion.1), channel_id=1, source_target_pairs={{0,1},{1,2},{2,3},{3,4},{4,5},{5,6},{6,7},{7,8},{8,9},{9,10},{10,1... | collective-permute-start | bytes 984392 | tf_op jit(solution)/shard_map/ppermute | solution.py:169
  36.4 16.4 %collective-permute-start.3 = (f32[82032]{0:T(1024)S(1)}, f32[82032]{0:T(1024)}, u32[]{:S(2)}, u32[]{:S(2)}) collective-permute-start(f32[82032]{0:T(1024)S(1)} %pad_maximum_fusion.2), channel_id=1, source_target_pairs={{1,0},{2,1},{3,2},{4,3},{5,4},{6,5},{7,6},{8,7},{9,8},{10,9},{11,1... | collective-permute-start | bytes 984392 | tf_op jit(solution)/shard_map/ppermute | solution.py:169
  46.3 7.3 %copy-start.13 = (s32[7]{0:T(128)S(1)}, s32[7]{0:T(128)}, u32[]{:S(2)}) copy-start(s32[7]{0:T(128)} %constant.234.clone) | copy-start | bytes 88
  58.6 0.6 copy-start.9
  58.6 0.7 copy-start.10
  58.6 0.7 copy-start.11
  59.1 1.1 copy-start.6
  59.1 1.1 copy-start.7
  59.1 1.1 copy-start.8
  59.1 1.1 copy-start.12
  59.3 3.9 %copy-start = (f32[40,40,514]{2,1,0:T(8,128)S(1)}, f32[40,40,514]{2,1,0:T(8,128)}, u32[]{:S(2)}) copy-start(f32[40,40,514]{2,1,0:T(8,128)} %fusion.5) | copy-start | bytes 9868804
  78.3 9.6 %copy-start.1 = (s32[40,40,512]{2,1,0:T(8,128)S(1)}, s32[40,40,512]{2,1,0:T(8,128)}, u32[]{:S(2)}) copy-start(s32[40,40,512]{2,1,0:T(8,128)} %shift-left_or_fusion) | copy-start | bytes 9830404
  78.3 9.6 %copy-start.2 = (f32[38,38,512]{2,1,0:T(8,128)S(1)}, f32[38,38,512]{2,1,0:T(8,128)}, u32[]{:S(2)}) copy-start(f32[38,38,512]{2,1,0:T(8,128)} %get-tuple-element.12) | copy-start | bytes 8871940
  108.1 12.9 %copy-start.14 = (s32[8]{0:T(128)S(1)}, s32[8]{0:T(128)}, u32[]{:S(2)}) copy-start(s32[8]{0:T(128)} %param.10) | copy-start | bytes 100
  108.1 108.3 %all-to-all-start = ((f32[32,16,16,128]{3,2,1,0:T(8,128)}), f32[32,16,16,128]{3,2,1,0:T(8,128)}, u32[]{:S(2)}, u32[]{:S(2)}) async-start(f32[32,16,16,128]{3,2,1,0:T(8,128)} %gather_fusion), calls=%async_computation | async-start | bytes 8388608 | tf_op jit(solution)/shard_map/all_to_all | solution.py:270
